TPU v7x, 32 devices: a whole 2x2x4 slice. The times are simulated.
32 devices in a mesh: groups: 2 (over y), video: 8 (over z, x), fsdp: 2 (over core).
Axes of the slice: x: 2, y: 2, z: 4, core: 2. Of those that a mesh axis runs over, the one named last changes fastest.
Arguments:
- video: bfloat16 [32, 32, 16, 512], P(('groups', 'video', 'fsdp')), parts along dimension 0, may hold values from -6 to 6
- w_spatial: bfloat16 [3, 3, 512, 512], P(None, None, 'fsdp'), may hold values from -0.09375 to 0.09375
- norm_gain: float32 [512], replicated, may hold values from 0.1 to 1.9
- norm_shift: float32 [512], replicated, may hold values from -3 to 3
- w_time: bfloat16 [3, 512, 512], P(None, 'fsdp'), may hold values from -0.15625 to 0.15625
Outputs:
- result: bfloat16 [32, 32, 16, 512], P(('groups', 'video', 'fsdp')), parts along dimension 0
There are 2 independent parts, one for each index of `groups`. A program takes and returns all parts, laid end to end along the dimension named above; an argument that names none is the same for every part. Nothing has to cross between parts.
All inputs are finite; a program needn't handle non-finite values.
Results may differ from a plain program's by a relative error of at most 0.0049.
Values may be sent and summed in bfloat16 or wider, within the bound.
No kernel may reach another device: no remote copies, remote signals or barrier semaphores. Data moves between devices by JAX's collectives and lax.ppermute only.
A program may use at most 64 MiB of HBM per device.

v0:
```python
import jax
import jax.numpy as jnp
from jax import lax
from jax.sharding import PartitionSpec as P

GROUPS = 32
CLIP = 16


def partner_2(block, axis, bit):
    count = lax.axis_size(axis)
    route = []
    for low in range(count):
        high = low | 1 << bit
        if high != low and high < count:
            route += [(low, high), (high, low)]
    return lax.ppermute(block, axis, route)


def spatial_conv(frames, w_spatial):
    count, height, width, channels = frames.shape
    outputs = w_spatial.shape[3]
    padded = jnp.pad(frames, ((0, 0), (1, 1), (1, 1), (0, 0)))
    initial = jnp.zeros((count * height * width, outputs), jnp.float32)
    total = initial
    piece = lax.all_gather(w_spatial, "fsdp", axis=2, tiled=True)
    span = piece.shape[2]
    for row_tap in range(3):
        for col_tap in range(3):
            window = padded[:, row_tap : row_tap + height, col_tap : col_tap + width, :].reshape(
                -1, span
            )
            total = total + jnp.dot(
                window, piece[row_tap, col_tap], preferred_element_type=jnp.float32
            )
    return total


def temporal_conv(stacked, w_time):
    rows = stacked[1].shape[0]
    outputs = w_time.shape[2]
    initial = jnp.zeros((rows, outputs), jnp.float32)
    total = initial
    piece = lax.all_gather(w_time, "fsdp", axis=1, tiled=True)
    for tap in range(3):
        columns = stacked[tap]
        total = total + jnp.dot(columns, piece[tap], preferred_element_type=jnp.float32)
    return total


def body(video, w_spatial, norm_gain, norm_shift, w_time):
    count, height, width, channels = video.shape
    spatial = spatial_conv(video, w_spatial)
    grouped = spatial.reshape(count, height * width, GROUPS, channels // GROUPS)
    mean = jnp.mean(grouped, axis=(1, 3), keepdims=True)
    variance = jnp.mean(jnp.square(grouped - mean), axis=(1, 3), keepdims=True)
    normed = ((grouped - mean) * lax.rsqrt(variance + 1e-05)).reshape(
        count, height * width, channels
    )
    hidden = jax.nn.silu(normed * norm_gain + norm_shift).astype(jnp.bfloat16)
    blocks = lax.axis_size("video")
    pairs = lax.axis_size("fsdp")
    pixels = height * width // blocks
    local = hidden.reshape(count, blocks, pixels, channels)
    arrived = lax.all_to_all(local, "video", split_axis=1, concat_axis=0, tiled=True)
    edges = jnp.stack([arrived[:, 0], arrived[:, count - 1]])
    partner = partner_2(edges, "fsdp", 0)
    other_first = partner[0]
    other_last = partner[1]
    side = lax.axis_index("fsdp")
    zero_block = jnp.zeros_like(other_last[:1])
    last_before = jnp.concatenate([zero_block, other_last[:-1]], axis=0)
    first_after = jnp.concatenate([other_first[1:], zero_block], axis=0)
    before_edge = jnp.where(side == 0, last_before, other_last)
    after_edge = jnp.where(side == 0, other_first, first_after)
    previous = jnp.concatenate([before_edge[:, None], arrived[:, :-1]], axis=1)
    following = jnp.concatenate([arrived[:, 1:], after_edge[:, None]], axis=1)
    frame_ids = (jnp.arange(blocks)[:, None] * pairs + side) * count + jnp.arange(count)[None, :]
    keep_before = (frame_ids % CLIP != 0)[:, :, None, None]
    keep_after = (frame_ids % CLIP != CLIP - 1)[:, :, None, None]
    previous = jnp.where(keep_before, previous, jnp.zeros_like(previous))
    following = jnp.where(keep_after, following, jnp.zeros_like(following))
    total = temporal_conv(
        (
            previous.reshape(-1, channels),
            arrived.reshape(-1, channels),
            following.reshape(-1, channels),
        ),
        w_time,
    )
    mixed = (arrived.reshape(-1, channels).astype(jnp.float32) + total).astype(jnp.bfloat16)
    mixed = mixed.reshape(blocks * count, 1, pixels, channels)
    returned = lax.all_to_all(mixed, "video", split_axis=0, concat_axis=1, tiled=True)
    return returned.reshape(count, height, width, channels)


def solution(mesh):
    placed = (
        P(("groups", "video", "fsdp"), None, None, None),
        P(None, None, "fsdp", None),
        P(),
        P(),
        P(None, "fsdp", None),
    )
    return jax.shard_map(
        body,
        mesh=mesh,
        in_specs=placed,
        out_specs=P(("groups", "video", "fsdp"), None, None, None),
        check_vma=False,
    )
```

profile of v0, /device:TPU:0, one launch (start us, length us, event | category | flops | bytes accessed | tf_op | source)
XLA Modules:
  0.0 88.9 jit_solution(9656500367549770682)
XLA Ops:
  6.5 0.7 all-gather.3.cloned.1.call-update
  7.3 5.2 %pad_slice_fusion = (bf16[1,32,16,512]{3,2,1,0:T(8,128)(2,1)S(1)}, bf16[1,32,16,512]{3,2,1,0:T(8,128)(2,1)}, bf16[1,32,16,512]{3,2,1,0:T(8,128)(2,1)S(1)}, bf16[...) fusion(bf16[1,32,16,512]{3,2,1,0:T(8,128)(2,1)} %param.5), kind=kLoop, calls=%fused_computation.12 | loop fusion | bytes 4718592 | tf_op jit(solution)/shard_map/slice | solution.py:30
  12.4 13.6 %all-gather.3.cloned.1.call-done = bf16[3,3,512,512]{3,2,1,0:T(8,128)(2,1)} async-done(((bf16[3,3,256,512]{3,2,1,0:T(8,128)(2,1)}), bf16[3,3,512,512]{3,2,1,0:T(8,128)(2,1)}) %all-gather.3.cloned.1.call-update) | async-done | bytes 4718608 | tf_op jit(solution)/shard_map/all_gather | solution.py:26
  26.1 1.8 %fusion.7 = f32[512,512]{1,0:T(8,128)S(1)} fusion(bf16[512,512]{1,0:T(8,128)(2,1)} %bitcast.101, bf16[3,3,512,512]{3,2,1,0:T(8,128)(2,1)} %all-gather.3.cloned.1.call-done), kind=kOutput, calls=%fused_computation.42 | convolution fusion | flops 268435456 | bytes 2097152 | tf_op jit(solution)/shard_map/dot_general | solution.py:33
  27.9 1.7 %convolution_add_fusion.9 = f32[512,512]{1,0:T(8,128)S(1)} fusion(f32[512,512]{1,0:T(8,128)S(1)} %fusion.7, bf16[512,512]{1,0:T(8,128)(2,1)} %bitcast.100, bf16[3,3,512,512]{3,2,1,0:T(8,128)(2,1)} %all-gather.3.cloned.1.call-done), kind=kOutput, calls=%fused_computation.10 | convolution fusion | flops 268697600 | bytes 3145728 | tf_op jit(solution)/shard_map/dot_general | solution.py:33
  29.6 0.4 convolution_add_fusion.8
  30.0 0.4 convolution_add_fusion.7
  30.5 0.4 convolution_add_fusion.6
  30.9 0.4 convolution_add_fusion.5
  31.4 0.4 convolution_add_fusion.4
  31.8 0.4 convolution_add_fusion.3
  32.3 0.5 fusion.9
  33.1 0.2 multiply_reduce_fusion
  33.7 1.1 %multiply_convert_fusion = bf16[512,512]{1,0:T(8,128)(2,1)} fusion(f32[512,512]{1,0:T(8,128)S(1)} %get-tuple-element.18, f32[512]{0:T(512)S(1)} %copy-done.2, f32[512]{0:T(512)S(1)} %copy-done.3, f32[512]{0:T(512)S(1)} %mul.43, f32[512]{0:T(512)S(1)} %sub.22), kind=kLoop, calls=%fused_computation.21 | loop fusion | flops 2359296 | bytes 1581056 | tf_op jit(solution)/shard_map/convert_element_type | solution.py:60
  34.8 5.8 %all-to-all-start = ((bf16[1,8,64,512]{3,2,0,1:T(8,128)(2,1)}), bf16[1,8,64,512]{3,2,0,1:T(8,128)(2,1)S(1)}, u32[]{:S(2)}, u32[]{:S(2)}) async-start(bf16[1,8,64,512]{3,2,0,1:T(8,128)(2,1)} %bitcast.19), calls=%async_computation | async-start | bytes 1048576 | tf_op jit(solution)/shard_map/all_to_all | solution.py:65
  40.6 0.7 all-gather.5.cloned.1.call-update
  41.3 14.2 %all-to-all-done = bf16[1,8,64,512]{3,2,0,1:T(8,128)(2,1)S(1)} async-done(((bf16[1,8,64,512]{3,2,0,1:T(8,128)(2,1)}), bf16[1,8,64,512]{3,2,0,1:T(8,128)(2,1)S(1)}, u32[]{:S(2)}, u32[]{:S(2)}) %all-to-all-start) | async-done | bytes 524320 | tf_op jit(solution)/shard_map/all_to_all | solution.py:65
  55.7 2.6 %collective-permute-done = bf16[2,8,64,512]{3,2,0,1:T(8,128)(2,1)S(1)} collective-permute-done((bf16[2,8,64,512]{3,2,0,1:T(8,128)(2,1)S(1)}, bf16[2,8,64,512]{3,2,0,1:T(8,128)(2,1)S(1)}, u32[]{:S(2)}, u32[]{:S(2)}) %collective-permute-start) | collective-permute-done | bytes 1048608 | tf_op jit(solution)/shard_map/ppermute | solution.py:17
  58.4 0.2 fusion.3
  58.6 1.5 %fusion.4 = f32[512,512]{1,0:T(8,128)S(1)} fusion(bf16[512,512]{1,0:T(8,128)(2,1)S(1)} %bitcast.105, bf16[3,512,512]{2,1,0:T(8,128)(2,1)} %all-gather.5.cloned.1.call-done), kind=kOutput, calls=%fused_computation.29 | convolution fusion | flops 268435456 | bytes 2097152 | tf_op jit(solution)/shard_map/dot_general | solution.py:47
  60.1 1.5 %convolution_add_fusion.1 = f32[512,512]{1,0:T(8,128)S(1)} fusion(f32[512,512]{1,0:T(8,128)S(1)} %fusion.4, bf16[512,512]{1,0:T(8,128)(2,1)S(1)} %bitcast.91, bf16[3,512,512]{2,1,0:T(8,128)(2,1)} %all-gather.5.cloned.1.call-done), kind=kOutput, calls=%fused_computation.2 | convolution fusion | flops 268697600 | bytes 3145728 | tf_op jit(solution)/shard_map/dot_general | solution.py:47
  61.6 1.5 %fusion.1 = bf16[512,512]{1,0:T(8,128)(2,1)S(1)} fusion(f32[512,512]{1,0:T(8,128)S(1)} %convolution_add_fusion.1, bf16[512,512]{1,0:T(8,128)(2,1)S(1)} %bitcast.104, bf16[512,512]{1,0:T(8,128)(2,1)S(1)} %bitcast.92, bf16[3,512,512]{2,1,0:T(8,128)(2,1)} %all-gather.5.cloned.1.call-done), kind=kOutput, calls=%fused_computation.11 | convolution fusion | flops 269484032 | bytes 3145728 | tf_op jit(solution)/shard_map/dot_general | solution.py:47
  63.1 18.2 %all_to_all.8 = bf16[8,1,64,512]{3,2,1,0:T(8,128)(2,1)S(1)} all-to-all(bf16[8,1,64,512]{3,2,1,0:T(8,128)(2,1)S(1)} %bitcast.103), channel_id=1, replica_groups=mesh['groups'=2,'video'=8,'fsdp'=2] {'video'}, dimensions={0} | all-to-all | bytes 1048576 | tf_op jit(solution)/shard_map/all_to_all | solution.py:93
  81.3 0.8 copy.15
  (25 shorter events, 1.0 us)
Async XLA Ops:
  6.5 19.5 %all-gather.3.cloned.1.call-start = ((), (), s32[]{:S(2)}) async-start(), calls=%async_computation.2 | async-start | bytes 7077888 | tf_op jit(solution)/shard_map/all_gather | solution.py:26
  26.1 3.5 %copy-start = (bf16[3,3,512,512]{3,2,1,0:T(8,128)(2,1)S(1)}, bf16[3,3,512,512]{3,2,1,0:T(8,128)(2,1)}, u32[]{:S(2)}) copy-start(bf16[3,3,512,512]{3,2,1,0:T(8,128)(2,1)} %all-gather.3.cloned.1.call-done) | copy-start | bytes 14155780
  27.9 2.6 %copy-start.1 = (bf16[1,32,16,512]{3,2,1,0:T(8,128)(2,1)S(1)}, bf16[1,32,16,512]{3,2,1,0:T(8,128)(2,1)}, u32[]{:S(2)}) copy-start(bf16[1,32,16,512]{3,2,1,0:T(8,128)(2,1)} %param.5) | copy-start | bytes 1572868
  31.4 2.3 %copy-start.2 = (f32[512]{0:T(512)S(1)}, f32[512]{0:T(512)}, u32[]{:S(2)}) copy-start(f32[512]{0:T(512)} %param.8) | copy-start | bytes 6148
  31.4 2.3 %copy-start.3 = (f32[512]{0:T(512)S(1)}, f32[512]{0:T(512)}, u32[]{:S(2)}) copy-start(f32[512]{0:T(512)} %param.7) | copy-start | bytes 6148
  34.8 20.7 %all-to-all-start = ((bf16[1,8,64,512]{3,2,0,1:T(8,128)(2,1)}), bf16[1,8,64,512]{3,2,0,1:T(8,128)(2,1)S(1)}, u32[]{:S(2)}, u32[]{:S(2)}) async-start(bf16[1,8,64,512]{3,2,0,1:T(8,128)(2,1)} %bitcast.19), calls=%async_computation | async-start | bytes 1048576 | tf_op jit(solution)/shard_map/all_to_all | solution.py:65
  40.6 18.0 %all-gather.5.cloned.1.call-start = ((), (), s32[]{:S(2)}) async-start(), calls=%async_computation.3 | async-start | bytes 2359296 | tf_op jit(solution)/shard_map/all_gather | solution.py:44
  55.6 2.7 %collective-permute-start = (bf16[2,8,64,512]{3,2,0,1:T(8,128)(2,1)S(1)}, bf16[2,8,64,512]{3,2,0,1:T(8,128)(2,1)S(1)}, u32[]{:S(2)}, u32[]{:S(2)}) collective-permute-start(bf16[2,8,64,512]{3,2,0,1:T(8,128)(2,1)S(1)} %pad_maximum_fusion), channel_id=1, source_target_pairs={{0,1},{1,0},{2,3},{3,2},{4,5},{5,4},{6,7},{7,6},{8,9},{9,8},{10,11... | collective-permute-start | bytes 3145736 | tf_op jit(solution)/shard_map/ppermute | solution.py:17
Sparse Core Ops, SparseCore 0:
  8.9 17.1 all-gather.2
  43.0 11.1 all-gather.4
where the time goes:
time: 89.3 us; the launch traced here: 88.9 us
  waiting for transfers between devices  31.9 us (36%)
  blocking collectives  18.2 us (20%)
  between operations  13.6 us (15%)
  matrix products  11 us (12%)
  local copies, waits for them, and re-layouts  6.52 us (7%)
  starting transfers between devices  5.88 us (7%)
  other arithmetic  1.84 us (2%)
    all_to_all x1, blocking collectives, body(): lax.all_to_all(mixed, 'video', split_axis=0, concat_axis=1, tiled=True)  18.2 us
    all_to_all x1, waiting for transfers between devices, body(): lax.all_to_all(local, 'video', split_axis=1, concat_axis=0, tiled=True)  14.2 us
    all_gather x1, waiting for transfers between devices, spatial_conv(): piece = lax.all_gather(w_spatial, 'fsdp', axis=2, tiled=True)  13.6 us
    dot_general x9, matrix products, spatial_conv(): jnp.dot(window, piece[row_tap, col_tap], preferred_element_type=jnp.float32)  6.53 us
    all_to_all x1, starting transfers between devices, body(): lax.all_to_all(local, 'video', split_axis=1, concat_axis=0, tiled=True)  5.77 us
    slice x1, local copies, waits for them, and re-layouts, spatial_conv(): padded[:, row_tap:row_tap + height, col_tap:col_tap + width, :]  5.18 us
    dot_general x3, matrix products, temporal_conv(): jnp.dot(columns, piece[tap], preferred_element_type=jnp.float32)  4.43 us
    ppermute x1, waiting for transfers between devices, partner_2(): return lax.ppermute(block, axis, route)  2.62 us
  transfers between devices with their start and end apart: 4, of which 3 were waited for; matrix products, arithmetic and copies ran while one was open for 6% of the time, Pallas kernels for 0%

commit v1 on v0

v1 whole, which is shorter than its diff:
```python
import jax
import jax.numpy as jnp
from jax import lax
from jax.sharding import PartitionSpec as P

GROUPS = 32
CLIP = 16


def swap_pair(block):
    return lax.ppermute(block, "fsdp", [(0, 1), (1, 0)])


def shift_frames(block, step):
    count = lax.axis_size("video") * lax.axis_size("fsdp")
    route = [(j, j + step) for j in range(count) if 0 <= j + step < count]
    return lax.ppermute(block, ("video", "fsdp"), route)


def channel_half(block, side, span):
    return lax.dynamic_slice_in_dim(block, side * span, span, axis=block.ndim - 1)


def spatial_conv(frames, w_spatial):
    side = lax.axis_index("fsdp")
    span = w_spatial.shape[2]
    other_weight = swap_pair(w_spatial)
    numbers = ("NHWC", "HWIO", "NHWC")
    mine = lax.conv_general_dilated(
        channel_half(frames, side, span), w_spatial, (1, 1), ((1, 1), (1, 1)),
        dimension_numbers=numbers, preferred_element_type=jnp.float32,
    )
    other = lax.conv_general_dilated(
        channel_half(frames, 1 - side, span), other_weight, (1, 1), ((1, 1), (1, 1)),
        dimension_numbers=numbers, preferred_element_type=jnp.float32,
    )
    return mine + other


def body(video, w_spatial, norm_gain, norm_shift, w_time):
    count, height, width, channels = video.shape
    other_time = swap_pair(w_time)
    spatial = spatial_conv(video, w_spatial)
    grouped = spatial.reshape(count, height * width, GROUPS, channels // GROUPS)
    mean = jnp.mean(grouped, axis=(1, 3), keepdims=True)
    variance = jnp.mean(jnp.square(grouped - mean), axis=(1, 3), keepdims=True)
    normed = ((grouped - mean) * lax.rsqrt(variance + 1e-05)).reshape(
        count, height * width, channels
    )
    hidden = jax.nn.silu(normed * norm_gain + norm_shift).astype(jnp.bfloat16)

    from_before = shift_frames(hidden[count - 1 :], 1)
    from_after = shift_frames(hidden[:1], -1)
    previous = jnp.concatenate([from_before, hidden[:-1]], axis=0)
    following = jnp.concatenate([hidden[1:], from_after], axis=0)
    position = lax.axis_index("video") * lax.axis_size("fsdp") + lax.axis_index("fsdp")
    frame_ids = position * count + jnp.arange(count)
    keep_before = (frame_ids % CLIP != 0)[:, None, None]
    keep_after = (frame_ids % CLIP != CLIP - 1)[:, None, None]
    previous = jnp.where(keep_before, previous, jnp.zeros_like(previous))
    following = jnp.where(keep_after, following, jnp.zeros_like(following))

    side = lax.axis_index("fsdp")
    span = w_time.shape[1]
    rows = count * height * width
    total = jnp.zeros((rows, channels), jnp.float32)
    for tap, frames in enumerate((previous, hidden, following)):
        flat = frames.reshape(rows, channels)
        total = total + jnp.dot(
            channel_half(flat, side, span), w_time[tap], preferred_element_type=jnp.float32
        )
        total = total + jnp.dot(
            channel_half(flat, 1 - side, span), other_time[tap], preferred_element_type=jnp.float32
        )
    mixed = (hidden.reshape(rows, channels).astype(jnp.float32) + total).astype(jnp.bfloat16)
    return mixed.reshape(count, height, width, channels)


def solution(mesh):
    placed = (
        P(("groups", "video", "fsdp"), None, None, None),
        P(None, None, "fsdp", None),
        P(),
        P(),
        P(None, "fsdp", None),
    )
    return jax.shard_map(
        body,
        mesh=mesh,
        in_specs=placed,
        out_specs=P(("groups", "video", "fsdp"), None, None, None),
        check_vma=False,
    )
```

time: 89.3 us -> 34.9 us (0.39)
  the two profiles are of different devices: /device:TPU:0 before, /device:TPU:17 now
where the time goes in v1:
time: 34.9 us; the launch traced here: 34.6 us
  matrix products  11.2 us (32%)
  waiting for transfers between devices  10.7 us (31%)
  starting transfers between devices  6.11 us (18%)
  local copies, waits for them, and re-layouts  5.06 us (14%)
  other arithmetic  1.29 us (4%)
    ppermute x2, waiting for transfers between devices, shift_frames(): return lax.ppermute(block, ('video', 'fsdp'), route)  10.7 us
    ppermute x2, starting transfers between devices, shift_frames(): return lax.ppermute(block, ('video', 'fsdp'), route)  5.43 us
    dot_general x3, matrix products, body(): jnp.dot(channel_half(flat, 1 - side, span), other_time[tap], preferred_el...  4.59 us
    conv_general_dilated x1, matrix products, spatial_conv(): lax.conv_general_dilated(channel_half(frames, 1 - side, span), other_weig...  3.72 us
    conv_general_dilated x1, matrix products, spatial_conv(): lax.conv_general_dilated(channel_half(frames, side, span), w_spatial, (1,...  2 us
    add x3, local copies, waits for them, and re-layouts, spatial_conv(): return mine + other  1.64 us
    dynamic_slice x4, local copies, waits for them, and re-layouts, channel_half(): lax.dynamic_slice_in_dim(block, side * span, span, axis=block.ndim - 1)  1.28 us
    unnamed x10, local copies, waits for them, and re-layouts  1.1 us
  transfers between devices with their start and end apart: 4, of which 2 were waited for; matrix products, arithmetic and copies ran while one was open for 33% of the time, Pallas kernels for 0%

profile of v1, /device:TPU:17, one launch (start us, length us, event | category | flops | bytes accessed | tf_op | source)
XLA Modules:
  0.0 34.6 jit_solution(16987798602735688387)
XLA Ops:
  0.0 0.7 %collective-permute-start = (bf16[3,3,256,512]{3,2,1,0:T(8,128)(2,1)}, bf16[3,3,256,512]{3,2,1,0:T(8,128)(2,1)}, u32[]{:S(2)}, u32[]{:S(2)}) collective-permute-start(bf16[3,3,256,512]{3,2,1,0:T(8,128)(2,1)} %param.6), channel_id=1, source_target_pairs={{0,1},{1,0},{2,3},{3,2},{4,5},{5,4},{6,7},{7,6},{8,9},{9,8},{10,11... | collective-permute-start | bytes 7077896 | tf_op jit(solution)/shard_map/ppermute | solution.py:11
  0.7 1.1 %constant_dynamic-slice_fusion = (bf16[1,32,16,256]{3,2,1,0:T(8,128)(2,1)S(1)}, bf16[1,32,16,256]{3,2,1,0:T(8,128)(2,1)S(1)}) fusion(bf16[1,32,16,512]{3,2,1,0:T(8,128)(2,1)} %param.5, s32[]{:T(128)S(6)} %select_n.29, s32[]{:T(128)S(6)} %select_n.28), kind=kLoop, calls=%fused_computation.71 | loop fusion | bytes 1048584 | tf_op jit(solution)/shard_map/dynamic_slice | solution.py:21
  1.7 0.2 copy_bitcast_fusion
  2.0 0.2 copy.16
  2.3 0.2 copy.19
  2.6 1.0 %copy-done.4 = bf16[3,3,256,512]{3,2,1,0:T(8,128)(2,1)S(1)} copy-done((bf16[3,3,256,512]{3,2,1,0:T(8,128)(2,1)S(1)}, bf16[3,3,256,512]{3,2,1,0:T(8,128)(2,1)}, u32[]{:S(2)}) %copy-start.4) | copy-done | bytes 2359320
  3.6 2.0 %fusion.15 = f32[32,8,3,512]{3,1,2,0:T(8,128)S(1)} fusion(bf16[3,3,256,512]{3,2,1,0:T(8,128)(2,1)S(1)} %copy-done.4, bf16[32,1,7,2,256]{4,2,3,0,1:T(8,128)(2,1)S(1)} %slice.27, bf16[32,1,8,3,256]{4,2,3,0,1:T(8,128)(2,1)S(1)} %copy.16), kind=kOutput, calls=%fused_computation.25 | convolution fusion | flops 1776156672 | bytes 4554752 | tf_op jit(solution)/shard_map/conv_general_dilated | solution.py:29
  5.6 3.7 %select_reduce_fusion.1 = (f32[512]{0:T(512)S(1)}, f32[32,8,3,512]{3,1,2,0:T(8,128)S(1)}) fusion(pred[8,3]{0,1:T(4,128)(4,1)S(1)} %copy-done.3, bf16[3,3,256,512]{3,2,1,0:T(8,128)(2,1)} %collective-permute-done, bf16[32,1,7,2,256]{4,2,3,0,1:T(8,128)(2,1)S(1)} %slice.28, bf16[32,1,8,3,256]{4,2,3,0,1:T(8,128)(2,1)S(1)} %copy.19, f32[32,8,3,512]{3,1,2,0:T(8,128)S(1)} %fusion.15), kind=kOutput, calls=%fused_computation.1 | convolution fusion | flops 1778122240 | bytes 6129688 | tf_op jit(solution)/shard_map/conv_general_dilated | solution.py:33
  9.7 0.9 %copy.20 = f32[32,8,3,512]{3,0,2,1:T(8,128)S(1)} copy(f32[32,8,3,512]{3,1,2,0:T(8,128)S(1)} %get-tuple-element.8) | data formatting | bytes 3145728 | tf_op jit(solution)/shard_map/add | solution.py:37
  10.7 0.3 select_reduce_fusion
  11.0 0.1 reduce_sum.37
  11.5 0.6 %copy.21 = f32[32,1,16,512]{3,2,0,1:T(8,128)S(1)} copy(f32[32,1,16,512]{3,0,2,1:T(8,128)S(1)} %slice.29) | data formatting | bytes 2097152 | tf_op jit(solution)/shard_map/add | solution.py:37
  12.1 0.3 multiply_convert_fusion
  12.5 3.5 %collective-permute-start.1 = (bf16[1,512,512]{2,1,0:T(8,128)(2,1)S(1)}, bf16[1,512,512]{2,1,0:T(8,128)(2,1)S(1)}, u32[]{:S(2)}, u32[]{:S(2)}) collective-permute-start(bf16[1,512,512]{2,1,0:T(8,128)(2,1)S(1)} %multiply_convert_fusion), channel_id=1, source_target_pairs={{0,1},{1,2},{2,3},{3,4},{4,5},{5,6},{6,7},{7,8},{8,9},{9,10},{10,1... | collective-permute-start | bytes 1572872 | tf_op jit(solution)/shard_map/ppermute | solution.py:17
  16.0 1.9 %collective-permute-start.3 = (bf16[1,512,512]{2,1,0:T(8,128)(2,1)S(1)}, bf16[1,512,512]{2,1,0:T(8,128)(2,1)S(1)}, u32[]{:S(2)}, u32[]{:S(2)}) collective-permute-start(bf16[1,512,512]{2,1,0:T(8,128)(2,1)S(1)} %multiply_convert_fusion), channel_id=1, source_target_pairs={{1,0},{2,1},{3,2},{4,3},{5,4},{6,5},{7,6},{8,7},{9,8},{10,9},{11,1... | collective-permute-start | bytes 1572872 | tf_op jit(solution)/shard_map/ppermute | solution.py:17
  17.9 0.3 multiply_convert_fusion.1
  18.3 0.3 fusion.35
  18.6 9.1 %collective-permute-done.1 = bf16[1,512,512]{2,1,0:T(8,128)(2,1)S(1)} collective-permute-done((bf16[1,512,512]{2,1,0:T(8,128)(2,1)S(1)}, bf16[1,512,512]{2,1,0:T(8,128)(2,1)S(1)}, u32[]{:S(2)}, u32[]{:S(2)}) %collective-permute-start.1) | collective-permute-done | bytes 524320 | tf_op jit(solution)/shard_map/ppermute | solution.py:17
  27.8 1.5 %collective-permute-done.3 = bf16[1,512,512]{2,1,0:T(8,128)(2,1)S(1)} collective-permute-done((bf16[1,512,512]{2,1,0:T(8,128)(2,1)S(1)}, bf16[1,512,512]{2,1,0:T(8,128)(2,1)S(1)}, u32[]{:S(2)}, u32[]{:S(2)}) %collective-permute-start.3) | collective-permute-done | bytes 524320 | tf_op jit(solution)/shard_map/ppermute | solution.py:17
  29.3 0.3 fusion.31
  29.7 1.2 %fusion.29 = f32[512,512]{1,0:T(8,128)S(1)} fusion(bf16[3,256,512]{2,1,0:T(8,128)(2,1)} %collective-permute-done.2, bf16[1,512,512]{2,1,0:T(8,128)(2,1)S(1)} %broadcast_select_fusion.1, s32[]{:T(128)S(6)} %select_n.29), kind=kOutput, calls=%fused_computation.42 | convolution fusion | flops 134217728 | bytes 1572868 | tf_op jit(solution)/shard_map/dot_general | solution.py:72
  30.9 0.3 fusion.1
  31.2 1.2 %fusion.28 = f32[512,512]{1,0:T(8,128)S(1)} fusion(bf16[3,256,512]{2,1,0:T(8,128)(2,1)} %collective-permute-done.2, bf16[1,512,512]{2,1,0:T(8,128)(2,1)S(1)} %broadcast_select_fusion, s32[]{:T(128)S(6)} %select_n.29), kind=kOutput, calls=%fused_computation.39 | convolution fusion | flops 134217728 | bytes 1572868 | tf_op jit(solution)/shard_map/dot_general | solution.py:72
  32.5 2.1 %fusion.6 = bf16[512,512]{1,0:T(8,128)(2,1)} fusion(f32[512,512]{1,0:T(8,128)S(1)} %fusion.28, f32[512,512]{1,0:T(8,128)S(1)} %fusion.31, f32[512,512]{1,0:T(8,128)S(1)} %fusion.1, bf16[512,512]{1,0:T(8,128)(2,1)S(1)} %multiply_convert_fusion.1, bf16[3,256,512]{2,1,0:T(8,128)(2,1)} %collective-permute-done.2, ...), kind=kOutput, calls=%fused_computation.12 | convolution fusion | flops 135790592 | bytes 4718596 | tf_op jit(solution)/shard_map/dot_general | solution.py:72
  (28 shorter events, 1.0 us)
Async XLA Ops:
  0.0 5.6 %collective-permute-start = (bf16[3,3,256,512]{3,2,1,0:T(8,128)(2,1)}, bf16[3,3,256,512]{3,2,1,0:T(8,128)(2,1)}, u32[]{:S(2)}, u32[]{:S(2)}) collective-permute-start(bf16[3,3,256,512]{3,2,1,0:T(8,128)(2,1)} %param.6), channel_id=1, source_target_pairs={{0,1},{1,0},{2,3},{3,2},{4,5},{5,4},{6,7},{7,6},{8,9},{9,8},{10,11... | collective-permute-start | bytes 7077896 | tf_op jit(solution)/shard_map/ppermute | solution.py:11
  0.7 29.0 %collective-permute-start.2 = (bf16[3,256,512]{2,1,0:T(8,128)(2,1)}, bf16[3,256,512]{2,1,0:T(8,128)(2,1)}, u32[]{:S(2)}, u32[]{:S(2)}) collective-permute-start(bf16[3,256,512]{2,1,0:T(8,128)(2,1)} %param.9), channel_id=1, source_target_pairs={{0,1},{1,0},{2,3},{3,2},{4,5},{5,4},{6,7},{7,6},{8,9},{9,8},{10,11... | collective-permute-start | bytes 2359304 | tf_op jit(solution)/shard_map/ppermute | solution.py:11
  1.9 1.7 %copy-start.4 = (bf16[3,3,256,512]{3,2,1,0:T(8,128)(2,1)S(1)}, bf16[3,3,256,512]{3,2,1,0:T(8,128)(2,1)}, u32[]{:S(2)}) copy-start(bf16[3,3,256,512]{3,2,1,0:T(8,128)(2,1)} %param.6) | copy-start | bytes 7077892
  3.6 2.0 %copy-start.3 = (pred[8,3]{0,1:T(4,128)(4,1)S(1)}, pred[8,3]{0,1:T(4,128)(4,1)}, u32[]{:S(2)}) copy-start(pred[8,3]{0,1:T(4,128)(4,1)} %constant.72) | copy-start | bytes 76
  11.4 0.7 %copy-start.1 = (f32[512]{0:T(512)S(1)}, f32[512]{0:T(512)}, u32[]{:S(2)}) copy-start(f32[512]{0:T(512)} %param.8) | copy-start | bytes 6148
  11.4 0.7 %copy-start.2 = (f32[512]{0:T(512)S(1)}, f32[512]{0:T(512)}, u32[]{:S(2)}) copy-start(f32[512]{0:T(512)} %param.7) | copy-start | bytes 6148
  12.1 6.1 %copy-start = (bf16[3,256,512]{2,1,0:T(8,128)(2,1)S(1)}, bf16[3,256,512]{2,1,0:T(8,128)(2,1)}, u32[]{:S(2)}) copy-start(bf16[3,256,512]{2,1,0:T(8,128)(2,1)} %param.9) | copy-start | bytes 2359300
  12.5 15.2 %collective-permute-start.1 = (bf16[1,512,512]{2,1,0:T(8,128)(2,1)S(1)}, bf16[1,512,512]{2,1,0:T(8,128)(2,1)S(1)}, u32[]{:S(2)}, u32[]{:S(2)}) collective-permute-start(bf16[1,512,512]{2,1,0:T(8,128)(2,1)S(1)} %multiply_convert_fusion), channel_id=1, source_target_pairs={{0,1},{1,2},{2,3},{3,4},{4,5},{5,6},{6,7},{7,8},{8,9},{9,10},{10,1... | collective-permute-start | bytes 1572872 | tf_op jit(solution)/shard_map/ppermute | solution.py:17
  16.0 13.3 %collective-permute-start.3 = (bf16[1,512,512]{2,1,0:T(8,128)(2,1)S(1)}, bf16[1,512,512]{2,1,0:T(8,128)(2,1)S(1)}, u32[]{:S(2)}, u32[]{:S(2)}) collective-permute-start(bf16[1,512,512]{2,1,0:T(8,128)(2,1)S(1)} %multiply_convert_fusion), channel_id=1, source_target_pairs={{1,0},{2,1},{3,2},{4,3},{5,4},{6,5},{7,6},{8,7},{9,8},{10,9},{11,1... | collective-permute-start | bytes 1572872 | tf_op jit(solution)/shard_map/ppermute | solution.py:17

commit v2 on v1

v2 whole, which is shorter than its diff:
```python
import functools

import jax
import jax.numpy as jnp
from jax import lax
from jax.experimental import pallas as pl
from jax.experimental.pallas import tpu as pltpu
from jax.sharding import PartitionSpec as P

GROUPS = 32
CLIP = 16
EPS = 1e-05


def swap_pair(block):
    return lax.ppermute(block, "fsdp", [(0, 1), (1, 0)])


def group_sum(row, size):
    lanes = lax.broadcasted_iota(jnp.int32, row.shape, 1)
    width = row.shape[1]
    step = 1
    while step < size:
        up = pltpu.roll(row, width - step, 1)
        down = pltpu.roll(row, step, 1)
        row = row + jnp.where((lanes & step) == 0, up, down)
        step *= 2
    return row


def conv_norm_kernel(side_ref, xa_ref, xb_ref, wa_ref, wb_ref, gain_ref, shift_ref, o_ref,
                     xs_ref, acc_ref, *, width, group):
    tap = pl.program_id(0)
    rows, half = xa_ref.shape

    @pl.when(tap == 0)
    def _prepare():
        col = lax.broadcasted_iota(jnp.int32, (rows, half), 0) % width
        zeros = jnp.zeros((width, half), jnp.bfloat16)
        for h, x_ref in enumerate((xa_ref, xb_ref)):
            xf = x_ref[...].astype(jnp.float32)
            left = jnp.where(col == 0, 0.0, pltpu.roll(xf, 1, 0))
            right = jnp.where(col == width - 1, 0.0, pltpu.roll(xf, rows - 1, 0))
            for dx, v in enumerate((left, xf, right)):
                xs_ref[h, dx, :width, :] = zeros
                xs_ref[h, dx, width : width + rows, :] = v.astype(jnp.bfloat16)
                xs_ref[h, dx, width + rows :, :] = zeros
        acc_ref[...] = jnp.zeros_like(acc_ref)

    dy = tap // 3
    dx = tap % 3
    start = pl.multiple_of(dy * width, width)
    a = xs_ref[0, dx, pl.ds(start, rows), :]
    b = xs_ref[1, dx, pl.ds(start, rows), :]
    acc_ref[...] += jnp.dot(a, wa_ref[0, 0], preferred_element_type=jnp.float32) + jnp.dot(
        b, wb_ref[0, 0], preferred_element_type=jnp.float32
    )

    @pl.when(tap == 8)
    def _normalize():
        acc = acc_ref[...]
        count = rows * group
        total = jnp.broadcast_to(jnp.sum(acc, axis=0, keepdims=True), (8, acc.shape[1]))
        mean = group_sum(total, group)[0:1] / count
        d = acc - mean
        spread = jnp.broadcast_to(jnp.sum(d * d, axis=0, keepdims=True), (8, acc.shape[1]))
        variance = group_sum(spread, group)[0:1] / count
        v = d * lax.rsqrt(variance + EPS) * gain_ref[...] + shift_ref[...]
        o_ref[...] = (v / (1.0 + jnp.exp(-v))).astype(o_ref.dtype)


def conv_norm(frame, w_mine, w_other, gain, shift, side, width):
    rows, channels = frame.shape
    half = w_mine.shape[2]
    outputs = w_mine.shape[3]
    group = outputs // GROUPS
    kernel = functools.partial(conv_norm_kernel, width=width, group=group)
    weight_block = pl.BlockSpec((1, 1, half, outputs), lambda t, s: (t // 3, t % 3, 0, 0))
    return pl.pallas_call(
        kernel,
        out_shape=jax.ShapeDtypeStruct((rows, outputs), jnp.bfloat16),
        grid_spec=pltpu.PrefetchScalarGridSpec(
            num_scalar_prefetch=1,
            grid=(9,),
            in_specs=[
                pl.BlockSpec((rows, half), lambda t, s: (0, s[0])),
                pl.BlockSpec((rows, half), lambda t, s: (0, 1 - s[0])),
                weight_block,
                weight_block,
                pl.BlockSpec((1, outputs), lambda t, s: (0, 0)),
                pl.BlockSpec((1, outputs), lambda t, s: (0, 0)),
            ],
            out_specs=pl.BlockSpec((rows, outputs), lambda t, s: (0, 0)),
            scratch_shapes=[
                pltpu.VMEM((2, 3, rows + 2 * width, half), jnp.bfloat16),
                pltpu.VMEM((rows, outputs), jnp.float32),
            ],
        ),
        compiler_params=pltpu.CompilerParams(dimension_semantics=("arbitrary",)),
    )(side, frame, frame, w_mine, w_other, gain, shift)


def temporal_kernel(s_ref, ea, eb, pa, pb, ca, cb, cur_ref, wm_e, wo_e, wm_c, wo_c, wm_p, wo_p, o_ref):
    f32 = jnp.float32
    keep_edge = s_ref[1].astype(f32)
    keep_partner = s_ref[2].astype(f32)
    edge = jnp.dot(ea[...], wm_e[0], preferred_element_type=f32) + jnp.dot(
        eb[...], wo_e[0], preferred_element_type=f32
    )
    own = jnp.dot(ca[...], wm_c[0], preferred_element_type=f32) + jnp.dot(
        cb[...], wo_c[0], preferred_element_type=f32
    )
    partner = jnp.dot(pa[...], wm_p[0], preferred_element_type=f32) + jnp.dot(
        pb[...], wo_p[0], preferred_element_type=f32
    )
    total = own + keep_edge * edge + keep_partner * partner
    o_ref[...] = (cur_ref[...].astype(f32) + total).astype(o_ref.dtype)


def temporal(edge, partner, cur, w_mine, w_other, scalars):
    rows, channels = cur.shape
    half = w_mine.shape[1]
    outputs = w_mine.shape[2]
    mine = pl.BlockSpec((rows, half), lambda i, s: (0, s[0]))
    other = pl.BlockSpec((rows, half), lambda i, s: (0, 1 - s[0]))
    edge_tap = pl.BlockSpec((1, half, outputs), lambda i, s: (2 * s[0], 0, 0))
    own_tap = pl.BlockSpec((1, half, outputs), lambda i, s: (1, 0, 0))
    partner_tap = pl.BlockSpec((1, half, outputs), lambda i, s: (2 - 2 * s[0], 0, 0))
    return pl.pallas_call(
        temporal_kernel,
        out_shape=jax.ShapeDtypeStruct((rows, outputs), jnp.bfloat16),
        grid_spec=pltpu.PrefetchScalarGridSpec(
            num_scalar_prefetch=1,
            grid=(1,),
            in_specs=[
                mine, other, mine, other, mine, other,
                pl.BlockSpec((rows, outputs), lambda i, s: (0, 0)),
                edge_tap, edge_tap, own_tap, own_tap, partner_tap, partner_tap,
            ],
            out_specs=pl.BlockSpec((rows, outputs), lambda i, s: (0, 0)),
        ),
    )(scalars, edge, edge, partner, partner, cur, cur, cur,
      w_mine, w_other, w_mine, w_other, w_mine, w_other)


def body(video, w_spatial, norm_gain, norm_shift, w_time):
    count, height, width, channels = video.shape
    assert count == 1 and lax.axis_size("fsdp") == 2
    pixels = height * width
    side = lax.axis_index("fsdp")
    blocks = lax.axis_size("video") * 2
    position = lax.axis_index("video") * 2 + side

    route = []
    for j in range(blocks):
        target = j + 1 if j % 2 == 1 else j - 1
        if 0 <= target < blocks and min(j, target) % CLIP != CLIP - 1:
            route.append((j, target))
    frame = video.reshape(pixels, channels)
    edge_video = lax.ppermute(frame, ("video", "fsdp"), route)
    other_spatial = swap_pair(w_spatial)
    other_time = swap_pair(w_time)

    gain = norm_gain.reshape(1, channels)
    shift = norm_shift.reshape(1, channels)
    sides = side.reshape(1).astype(jnp.int32)
    hidden = conv_norm(frame, w_spatial, other_spatial, gain, shift, sides, width)
    partner = swap_pair(hidden)
    edge = conv_norm(edge_video, w_spatial, other_spatial, gain, shift, sides, width)

    keep_prev = (position % CLIP != 0).astype(jnp.int32)
    keep_next = (position % CLIP != CLIP - 1).astype(jnp.int32)
    keep_edge = jnp.where(side == 0, keep_prev, keep_next)
    keep_partner = jnp.where(side == 0, keep_next, keep_prev)
    scalars = jnp.stack([side.astype(jnp.int32), keep_edge, keep_partner])
    result = temporal(edge, partner, hidden, w_time, other_time, scalars)
    return result.reshape(count, height, width, channels)


def solution(mesh):
    placed = (
        P(("groups", "video", "fsdp"), None, None, None),
        P(None, None, "fsdp", None),
        P(),
        P(),
        P(None, "fsdp", None),
    )
    return jax.shard_map(
        body,
        mesh=mesh,
        in_specs=placed,
        out_specs=P(("groups", "video", "fsdp"), None, None, None),
        check_vma=False,
    )
```

time: 34.9 us -> 34.3 us (0.983)
  Pallas kernels: 0 us -> 24.7 us
  matrix products: 11.2 us -> 0 us
  waiting for transfers between devices: 10.7 us -> 0.86 us
  local copies, waits for them, and re-layouts: 5.06 us -> 3.09 us
  starting transfers between devices: 6.11 us -> 4.55 us
  other arithmetic: 1.29 us -> 0.64 us
    pallas_call x0 -> x3, Pallas kernels: none -> 24.7 us  [the longest x2 20.2 us: conv_norm(): pl.pallas_call(kernel, out_shape=jax.ShapeDtypeStruct((rows, outputs), jn...]
    ppermute x2 -> x1, waiting for transfers between devices: 10.7 us -> 0.01 us  [body(): edge_video = lax.ppermute(frame, ('video', 'fsdp'), route)]
    conv_general_dilated x2 -> x0, matrix products: 5.71 us -> none  [the longest x1 3.72 us: spatial_conv(): lax.conv_general_dilated(channel_half(frames, 1 - side, span), other_weig...]
    dot_general x6 -> x0, matrix products: 5.49 us -> none  [the longest x3 4.59 us: body(): jnp.dot(channel_half(flat, 1 - side, span), other_time[tap], preferred_el...]
    unnamed x10 -> x6, local copies, waits for them, and re-layouts: 1.1 us -> 3.09 us
    ppermute x2 -> x1, starting transfers between devices: 5.43 us -> 3.5 us  [body(): edge_video = lax.ppermute(frame, ('video', 'fsdp'), route)]
    add x3 -> x0, local copies, waits for them, and re-layouts: 1.64 us -> none  [spatial_conv(): return mine + other]
    dynamic_slice x4 -> x0, local copies, waits for them, and re-layouts: 1.28 us -> none  [channel_half(): lax.dynamic_slice_in_dim(block, side * span, span, axis=block.ndim - 1)]
  transfers between devices with their start and end apart: 4 -> 4, of which waited for: 2 -> 1; matrix products, arithmetic and copies ran while one was open for 33% -> 2% of each run, Pallas kernels for 0% -> 60%
where the time goes in v2:
time: 34.3 us; the launch traced here: 33.9 us
  Pallas kernels  24.7 us (72%)
  starting transfers between devices  4.55 us (13%)
  local copies, waits for them, and re-layouts  3.09 us (9%)
  waiting for transfers between devices  0.86 us (3%)
  other arithmetic  0.64 us (2%)
    pallas_call x2, Pallas kernels, conv_norm(): pl.pallas_call(kernel, out_shape=jax.ShapeDtypeStruct((rows, outputs), jn...  20.2 us
    pallas_call x1, Pallas kernels, temporal(): pl.pallas_call(temporal_kernel, out_shape=jax.ShapeDtypeStruct((rows, out...  4.44 us
    ppermute x1, starting transfers between devices, body(): edge_video = lax.ppermute(frame, ('video', 'fsdp'), route)  3.5 us
    unnamed x6, local copies, waits for them, and re-layouts  3.09 us
    ppermute x3, starting transfers between devices, swap_pair(): return lax.ppermute(block, 'fsdp', [(0, 1), (1, 0)])  1.05 us
    ppermute x3, waiting for transfers between devices, swap_pair(): return lax.ppermute(block, 'fsdp', [(0, 1), (1, 0)])  0.86 us
  transfers between devices with their start and end apart: 4, of which 1 were waited for; matrix products, arithmetic and copies ran while one was open for 2% of the time, Pallas kernels for 60%

profile of v2, /device:TPU:17, one launch (start us, length us, event | category | flops | bytes accessed | tf_op | source)
XLA Modules:
  0.0 33.9 jit_solution(12742220102944661094)
XLA Ops:
  0.0 0.7 %collective-permute-start.1 = (bf16[3,3,256,512]{3,2,1,0:T(8,128)(2,1)}, bf16[3,3,256,512]{3,2,1,0:T(8,128)(2,1)S(1)}, u32[]{:S(2)}, u32[]{:S(2)}) collective-permute-start(bf16[3,3,256,512]{3,2,1,0:T(8,128)(2,1)} %wa_ref.3), channel_id=1, source_target_pairs={{0,1},{1,0},{2,3},{3,2},{4,5},{5,4},{6,7},{7,6},{8,9},{9,8},{10,11... | collective-permute-start | bytes 7077896 | tf_op jit(solution)/shard_map/ppermute | solution.py:16
  0.7 0.0 collective-permute-start.3
  0.7 3.5 %collective-permute-start = (bf16[512,512]{1,0:T(8,128)(2,1)}, bf16[512,512]{1,0:T(8,128)(2,1)}, u32[]{:S(2)}, u32[]{:S(2)}) collective-permute-start(bf16[512,512]{1,0:T(8,128)(2,1)} %bitcast.7), channel_id=1, source_target_pairs={{1,2},{2,1},{3,4},{4,3},{5,6},{6,5},{7,8},{8,7},{9,10},{10,9},{11,... | collective-permute-start | bytes 1572872 | tf_op jit(solution)/shard_map/ppermute | solution.py:160
  4.2 0.9 %collective-permute-done.1.wb_ref = bf16[3,3,256,512]{3,2,1,0:T(8,128)(2,1)S(1)} collective-permute-done((bf16[3,3,256,512]{3,2,1,0:T(8,128)(2,1)}, bf16[3,3,256,512]{3,2,1,0:T(8,128)(2,1)S(1)}, u32[]{:S(2)}, u32[]{:S(2)}) %collective-permute-start.1) | collective-permute-done | bytes 2359328 | tf_op jit(solution)/shard_map/ppermute | solution.py:16
  5.0 0.0 copy-start
  5.1 1.4 %copy-done = bf16[3,3,256,512]{3,2,1,0:T(8,128)(2,1)} copy-done((bf16[3,3,256,512]{3,2,1,0:T(8,128)(2,1)}, bf16[3,3,256,512]{3,2,1,0:T(8,128)(2,1)S(1)}, u32[]{:S(2)}) %copy-start) | copy-done | bytes 2359320
  6.5 10.1 %shard_map.56.ca.cb.cur_ref = bf16[512,512]{1,0:T(8,128)(2,1)} custom-call(s32[1]{0:T(128)} %bitcast.side_ref, bf16[512,512]{1,0:T(8,128)(2,1)} %bitcast.8, bf16[512,512]{1,0:T(8,128)(2,1)} %bitcast.9, bf16[3,3,256,512]{3,2,1,0:T(8,128)(2,1)} %wa_ref.3, bf16[3,3,256,512]{3,2,1,0:T(8,128)(2,1)} %copy-done, f32[1,512]{1,0:T(1,128)} %bitcast.10, f32[1,512]{1,0:T(1,128)} %bitcast.12), custom_call_target="tpu_custom_call" | custom-call | tf_op jit(solution)/shard_map/pallas_call | solution.py:79
  16.6 0.4 %collective-permute-start.2 = (bf16[512,512]{1,0:T(8,128)(2,1)}, bf16[512,512]{1,0:T(8,128)(2,1)S(1)}, u32[]{:S(2)}, u32[]{:S(2)}) collective-permute-start(bf16[512,512]{1,0:T(8,128)(2,1)} %shard_map.56.ca.cb.cur_ref), channel_id=1, source_target_pairs={{0,1},{1,0},{2,3},{3,2},{4,5},{5,4},{6,7},{7,6},{8,9},{9,8},{10,11... | collective-permute-start | bytes 1572872 | tf_op jit(solution)/shard_map/ppermute | solution.py:16
  16.9 0.6 %pad_add_fusion.s_ref = s32[3]{0:T(128)} fusion(s32[1]{0:T(128)} %bitcast.2, s32[1]{0:T(128)} %bitcast.1, s32[1]{0:T(128)} %bitcast.side_ref), kind=kLoop, calls=%fused_computation | loop fusion | flops 6 | bytes 24 | tf_op jit(solution)/shard_map/stack | solution.py:175
  17.6 0.0 collective-permute-done.xa_ref.xb_ref
  17.6 10.1 %shard_map.55.ea.eb = bf16[512,512]{1,0:T(8,128)(2,1)} custom-call(s32[1]{0:T(128)} %bitcast.side_ref, bf16[512,512]{1,0:T(8,128)(2,1)} %collective-permute-done.xa_ref.xb_ref, bf16[512,512]{1,0:T(8,128)(2,1)} %collective-permute-done.xa_ref.xb_ref, bf16[3,3,256,512]{3,2,1,0:T(8,128)(2,1)} %wa_ref.3, bf16[3,3,256,512]{3,2,1,0:T(8,128)(2,1)} %copy-done, ...), custom_call_target="tpu_custom_call" | custom-call | tf_op jit(solution)/shard_map/pallas_call | solution.py:79
  27.7 0.0 collective-permute-done.3.wo_e.wo_c.wo_p
  27.7 0.0 copy-start.1
  27.7 0.0 collective-permute-done.2.pa.pb
  27.7 0.9 %copy-done.1 = bf16[3,256,512]{2,1,0:T(8,128)(2,1)} copy-done((bf16[3,256,512]{2,1,0:T(8,128)(2,1)}, bf16[3,256,512]{2,1,0:T(8,128)(2,1)S(1)}, u32[]{:S(2)}) %copy-start.1) | copy-done | bytes 786456
  28.6 0.0 copy-start.2
  28.6 0.8 %copy-done.2 = bf16[512,512]{1,0:T(8,128)(2,1)} copy-done((bf16[512,512]{1,0:T(8,128)(2,1)}, bf16[512,512]{1,0:T(8,128)(2,1)S(1)}, u32[]{:S(2)}) %copy-start.2) | copy-done | bytes 524312
  29.4 4.4 %shard_map.57 = bf16[512,512]{1,0:T(8,128)(2,1)} custom-call(s32[3]{0:T(128)} %pad_add_fusion.s_ref, bf16[512,512]{1,0:T(8,128)(2,1)} %shard_map.55.ea.eb, bf16[512,512]{1,0:T(8,128)(2,1)} %shard_map.55.ea.eb, bf16[512,512]{1,0:T(8,128)(2,1)} %copy-done.2, bf16[512,512]{1,0:T(8,128)(2,1)} %copy-done.2, bf16[512,512]{1,0:T(8,128)(2,1)} %shard_map.56.ca.cb.cur_ref, ...), custom_call_target="tpu_custom_call" | custom-call | tf_op jit(solution)/shard_map/pallas_call | solution.py:129
Async XLA Ops:
  0.0 5.0 %collective-permute-start.1 = (bf16[3,3,256,512]{3,2,1,0:T(8,128)(2,1)}, bf16[3,3,256,512]{3,2,1,0:T(8,128)(2,1)S(1)}, u32[]{:S(2)}, u32[]{:S(2)}) collective-permute-start(bf16[3,3,256,512]{3,2,1,0:T(8,128)(2,1)} %wa_ref.3), channel_id=1, source_target_pairs={{0,1},{1,0},{2,3},{3,2},{4,5},{5,4},{6,7},{7,6},{8,9},{9,8},{10,11... | collective-permute-start | bytes 7077896 | tf_op jit(solution)/shard_map/ppermute | solution.py:16
  0.7 27.0 %collective-permute-start.3 = (bf16[3,256,512]{2,1,0:T(8,128)(2,1)}, bf16[3,256,512]{2,1,0:T(8,128)(2,1)S(1)}, u32[]{:S(2)}, u32[]{:S(2)}) collective-permute-start(bf16[3,256,512]{2,1,0:T(8,128)(2,1)} %wm_p.1), channel_id=1, source_target_pairs={{0,1},{1,0},{2,3},{3,2},{4,5},{5,4},{6,7},{7,6},{8,9},{9,8},{10,11... | collective-permute-start | bytes 2359304 | tf_op jit(solution)/shard_map/ppermute | solution.py:16
  0.7 16.9 %collective-permute-start = (bf16[512,512]{1,0:T(8,128)(2,1)}, bf16[512,512]{1,0:T(8,128)(2,1)}, u32[]{:S(2)}, u32[]{:S(2)}) collective-permute-start(bf16[512,512]{1,0:T(8,128)(2,1)} %bitcast.7), channel_id=1, source_target_pairs={{1,2},{2,1},{3,4},{4,3},{5,6},{6,5},{7,8},{8,7},{9,10},{10,9},{11,... | collective-permute-start | bytes 1572872 | tf_op jit(solution)/shard_map/ppermute | solution.py:160
  5.0 1.4 %copy-start = (bf16[3,3,256,512]{3,2,1,0:T(8,128)(2,1)}, bf16[3,3,256,512]{3,2,1,0:T(8,128)(2,1)S(1)}, u32[]{:S(2)}) copy-start(bf16[3,3,256,512]{3,2,1,0:T(8,128)(2,1)S(1)} %collective-permute-done.1.wb_ref) | copy-start | bytes 7077892
  16.6 11.2 %collective-permute-start.2 = (bf16[512,512]{1,0:T(8,128)(2,1)}, bf16[512,512]{1,0:T(8,128)(2,1)S(1)}, u32[]{:S(2)}, u32[]{:S(2)}) collective-permute-start(bf16[512,512]{1,0:T(8,128)(2,1)} %shard_map.56.ca.cb.cur_ref), channel_id=1, source_target_pairs={{0,1},{1,0},{2,3},{3,2},{4,5},{5,4},{6,7},{7,6},{8,9},{9,8},{10,11... | collective-permute-start | bytes 1572872 | tf_op jit(solution)/shard_map/ppermute | solution.py:16
  27.7 0.9 %copy-start.1 = (bf16[3,256,512]{2,1,0:T(8,128)(2,1)}, bf16[3,256,512]{2,1,0:T(8,128)(2,1)S(1)}, u32[]{:S(2)}) copy-start(bf16[3,256,512]{2,1,0:T(8,128)(2,1)S(1)} %collective-permute-done.3.wo_e.wo_c.wo_p) | copy-start | bytes 2359300
  28.6 0.8 %copy-start.2 = (bf16[512,512]{1,0:T(8,128)(2,1)}, bf16[512,512]{1,0:T(8,128)(2,1)S(1)}, u32[]{:S(2)}) copy-start(bf16[512,512]{1,0:T(8,128)(2,1)S(1)} %collective-permute-done.2.pa.pb) | copy-start | bytes 1572868

commit v3 on v2

v3 whole, which is shorter than its diff:
```python
import functools

import jax
import jax.numpy as jnp
from jax import lax
from jax.experimental import pallas as pl
from jax.experimental.pallas import tpu as pltpu
from jax.sharding import PartitionSpec as P

GROUPS = 32
CLIP = 16
EPS = 1e-05


def swap_pair(block):
    return lax.ppermute(block, "fsdp", [(0, 1), (1, 0)])


def group_sum(row, size):
    lanes = lax.broadcasted_iota(jnp.int32, row.shape, 1)
    width = row.shape[1]
    step = 1
    while step < size:
        up = pltpu.roll(row, width - step, 1)
        down = pltpu.roll(row, step, 1)
        row = row + jnp.where((lanes & step) == 0, up, down)
        step *= 2
    return row


def conv_norm_kernel(side_ref, xa_ref, xb_ref, wa_ref, wb_ref, gain_ref, shift_ref, o_ref,
                     lhs_ref, *, width, group):
    rows, half = xa_ref.shape

    @pl.when(pl.program_id(0) == 0)
    def _prepare():
        col = lax.broadcasted_iota(jnp.int32, (rows, half), 0) % width
        zeros = jnp.zeros((width, half), jnp.bfloat16)
        for h, x_ref in enumerate((xa_ref, xb_ref)):
            xf = x_ref[...].astype(jnp.float32)
            left = jnp.where(col == 0, 0.0, pltpu.roll(xf, 1, 0)).astype(jnp.bfloat16)
            right = jnp.where(col == width - 1, 0.0, pltpu.roll(xf, rows - 1, 0)).astype(jnp.bfloat16)
            for dx, v in enumerate((left, xf.astype(jnp.bfloat16), right)):
                for dy in range(3):
                    lo = (dy * 3 + dx) * half
                    cols = slice(lo, lo + half)
                    if dy == 0:
                        lhs_ref[h, :width, cols] = zeros
                        lhs_ref[h, width:, cols] = v[: rows - width]
                    elif dy == 1:
                        lhs_ref[h, :, cols] = v
                    else:
                        lhs_ref[h, : rows - width, cols] = v[width:]
                        lhs_ref[h, rows - width :, cols] = zeros

    acc = jnp.dot(lhs_ref[0], wa_ref[...], preferred_element_type=jnp.float32) + jnp.dot(
        lhs_ref[1], wb_ref[...], preferred_element_type=jnp.float32
    )
    count = rows * group
    total = jnp.broadcast_to(jnp.sum(acc, axis=0, keepdims=True), (8, acc.shape[1]))
    mean = group_sum(total, group)[0:1] / count
    d = acc - mean
    spread = jnp.broadcast_to(jnp.sum(d * d, axis=0, keepdims=True), (8, acc.shape[1]))
    variance = group_sum(spread, group)[0:1] / count
    v = d * lax.rsqrt(variance + EPS) * gain_ref[...] + shift_ref[...]
    o_ref[...] = (v / (1.0 + jnp.exp(-v))).astype(o_ref.dtype)


def conv_norm(frame, w_mine, w_other, gain, shift, side, width, split=2):
    rows, channels = frame.shape
    half = w_mine.shape[2]
    outputs = w_mine.shape[3]
    group = outputs // GROUPS
    block = outputs // split
    kernel = functools.partial(conv_norm_kernel, width=width, group=group)
    weight_block = pl.BlockSpec((9 * half, block), lambda n, s: (0, n))
    row_block = pl.BlockSpec((1, block), lambda n, s: (0, n))
    return pl.pallas_call(
        kernel,
        out_shape=jax.ShapeDtypeStruct((rows, outputs), jnp.bfloat16),
        grid_spec=pltpu.PrefetchScalarGridSpec(
            num_scalar_prefetch=1,
            grid=(split,),
            in_specs=[
                pl.BlockSpec((rows, half), lambda n, s: (0, s[0])),
                pl.BlockSpec((rows, half), lambda n, s: (0, 1 - s[0])),
                weight_block,
                weight_block,
                row_block,
                row_block,
            ],
            out_specs=pl.BlockSpec((rows, block), lambda n, s: (0, n)),
            scratch_shapes=[pltpu.VMEM((2, rows, 9 * half), jnp.bfloat16)],
        ),
        compiler_params=pltpu.CompilerParams(dimension_semantics=("arbitrary",)),
    )(side, frame, frame, w_mine.reshape(9 * half, outputs), w_other.reshape(9 * half, outputs),
      gain, shift)


def temporal_kernel(s_ref, ea, eb, pa, pb, ca, cb, cur_ref, wm_ref, wo_ref, o_ref, lhs_ref):
    half = ea.shape[1]

    @pl.when(pl.program_id(0) == 0)
    def _prepare():
        keep_edge = s_ref[1] != 0
        keep_partner = s_ref[2] != 0
        for h, (e, p, c) in enumerate(((ea, pa, ca), (eb, pb, cb))):
            edge = jnp.where(keep_edge, e[...], jnp.zeros_like(e[...]))
            partner = jnp.where(keep_partner, p[...], jnp.zeros_like(p[...]))
            lhs_ref[h, :, half : 2 * half] = c[...]

            @pl.when(s_ref[0] == 0)
            def _():
                lhs_ref[h, :, :half] = edge
                lhs_ref[h, :, 2 * half :] = partner

            @pl.when(s_ref[0] != 0)
            def _():
                lhs_ref[h, :, :half] = partner
                lhs_ref[h, :, 2 * half :] = edge

    f32 = jnp.float32
    total = jnp.dot(lhs_ref[0], wm_ref[...], preferred_element_type=f32) + jnp.dot(
        lhs_ref[1], wo_ref[...], preferred_element_type=f32
    )
    o_ref[...] = (cur_ref[...].astype(f32) + total).astype(o_ref.dtype)


def temporal(edge, partner, cur, w_mine, w_other, scalars, split=2):
    rows, channels = cur.shape
    half = w_mine.shape[1]
    outputs = w_mine.shape[2]
    block = outputs // split
    mine = pl.BlockSpec((rows, half), lambda n, s: (0, s[0]))
    other = pl.BlockSpec((rows, half), lambda n, s: (0, 1 - s[0]))
    weight_block = pl.BlockSpec((3 * half, block), lambda n, s: (0, n))
    return pl.pallas_call(
        temporal_kernel,
        out_shape=jax.ShapeDtypeStruct((rows, outputs), jnp.bfloat16),
        grid_spec=pltpu.PrefetchScalarGridSpec(
            num_scalar_prefetch=1,
            grid=(split,),
            in_specs=[
                mine, other, mine, other, mine, other,
                pl.BlockSpec((rows, block), lambda n, s: (0, n)),
                weight_block, weight_block,
            ],
            out_specs=pl.BlockSpec((rows, block), lambda n, s: (0, n)),
            scratch_shapes=[pltpu.VMEM((2, rows, 3 * half), jnp.bfloat16)],
        ),
        compiler_params=pltpu.CompilerParams(dimension_semantics=("arbitrary",)),
    )(scalars, edge, edge, partner, partner, cur, cur, cur,
      w_mine.reshape(3 * half, outputs), w_other.reshape(3 * half, outputs))


def body(video, w_spatial, norm_gain, norm_shift, w_time):
    count, height, width, channels = video.shape
    assert count == 1 and lax.axis_size("fsdp") == 2
    pixels = height * width
    side = lax.axis_index("fsdp")
    blocks = lax.axis_size("video") * 2
    position = lax.axis_index("video") * 2 + side

    route = []
    for j in range(blocks):
        target = j + 1 if j % 2 == 1 else j - 1
        if 0 <= target < blocks and min(j, target) % CLIP != CLIP - 1:
            route.append((j, target))
    frame = video.reshape(pixels, channels)
    edge_video = lax.ppermute(frame, ("video", "fsdp"), route)
    other_spatial = swap_pair(w_spatial)
    other_time = swap_pair(w_time)

    gain = norm_gain.reshape(1, channels)
    shift = norm_shift.reshape(1, channels)
    sides = side.reshape(1).astype(jnp.int32)
    hidden = conv_norm(frame, w_spatial, other_spatial, gain, shift, sides, width)
    partner = swap_pair(hidden)
    edge = conv_norm(edge_video, w_spatial, other_spatial, gain, shift, sides, width)

    keep_prev = (position % CLIP != 0).astype(jnp.int32)
    keep_next = (position % CLIP != CLIP - 1).astype(jnp.int32)
    keep_edge = jnp.where(side == 0, keep_prev, keep_next)
    keep_partner = jnp.where(side == 0, keep_next, keep_prev)
    scalars = jnp.stack([side.astype(jnp.int32), keep_edge, keep_partner])
    result = temporal(edge, partner, hidden, w_time, other_time, scalars)
    return result.reshape(count, height, width, channels)


def solution(mesh):
    placed = (
        P(("groups", "video", "fsdp"), None, None, None),
        P(None, None, "fsdp", None),
        P(),
        P(),
        P(None, "fsdp", None),
    )
    return jax.shard_map(
        body,
        mesh=mesh,
        in_specs=placed,
        out_specs=P(("groups", "video", "fsdp"), None, None, None),
        check_vma=False,
    )
```

time: 34.3 us -> 31.2 us (0.910)
  Pallas kernels: 24.7 us -> 20.2 us
  waiting for transfers between devices: 0.86 us -> 2.63 us
    pallas_call x2, Pallas kernels: 20.2 us -> 15.6 us  [conv_norm(): pl.pallas_call(kernel, out_shape=jax.ShapeDtypeStruct((rows, outputs), jn...]
    ppermute x3, waiting for transfers between devices: 0.86 us -> 1.99 us  [swap_pair(): return lax.ppermute(block, 'fsdp', [(0, 1), (1, 0)])]
    ppermute x1, waiting for transfers between devices: 0.01 us -> 0.65 us  [body(): edge_video = lax.ppermute(frame, ('video', 'fsdp'), route)]
  transfers between devices with their start and end apart: 4 -> 4, of which waited for: 1 -> 2; matrix products, arithmetic and copies ran while one was open for 2% -> 2% of each run, Pallas kernels for 60% -> 50%
where the time goes in v3:
time: 31.2 us; the launch traced here: 31 us
  Pallas kernels  20.2 us (65%)
  starting transfers between devices  4.55 us (15%)
  local copies, waits for them, and re-layouts  2.99 us (10%)
  waiting for transfers between devices  2.63 us (8%)
  other arithmetic  0.59 us (2%)
    pallas_call x2, Pallas kernels, conv_norm(): pl.pallas_call(kernel, out_shape=jax.ShapeDtypeStruct((rows, outputs), jn...  15.6 us
    pallas_call x1, Pallas kernels, temporal(): pl.pallas_call(temporal_kernel, out_shape=jax.ShapeDtypeStruct((rows, out...  4.56 us
    ppermute x1, starting transfers between devices, body(): edge_video = lax.ppermute(frame, ('video', 'fsdp'), route)  3.5 us
    unnamed x6, local copies, waits for them, and re-layouts  2.99 us
    ppermute x3, waiting for transfers between devices, swap_pair(): return lax.ppermute(block, 'fsdp', [(0, 1), (1, 0)])  1.99 us
    ppermute x3, starting transfers between devices, swap_pair(): return lax.ppermute(block, 'fsdp', [(0, 1), (1, 0)])  1.05 us
    ppermute x1, waiting for transfers between devices, body(): edge_video = lax.ppermute(frame, ('video', 'fsdp'), route)  0.65 us
  transfers between devices with their start and end apart: 4, of which 2 were waited for; matrix products, arithmetic and copies ran while one was open for 2% of the time, Pallas kernels for 50%

profile of v3, /device:TPU:17, one launch (start us, length us, event | category | flops | bytes accessed | tf_op | source)
XLA Modules:
  0.0 31.0 jit_solution(8362045902845529251)
XLA Ops:
  0.0 0.7 %collective-permute-start.1 = (bf16[3,3,256,512]{3,2,1,0:T(8,128)(2,1)}, bf16[3,3,256,512]{3,2,1,0:T(8,128)(2,1)S(1)}, u32[]{:S(2)}, u32[]{:S(2)}) collective-permute-start(bf16[3,3,256,512]{3,2,1,0:T(8,128)(2,1)} %param.6), channel_id=1, source_target_pairs={{0,1},{1,0},{2,3},{3,2},{4,5},{5,4},{6,7},{7,6},{8,9},{9,8},{10,11... | collective-permute-start | bytes 7077896 | tf_op jit(solution)/shard_map/ppermute | solution.py:16
  0.7 0.0 collective-permute-start.3
  0.7 3.5 %collective-permute-start = (bf16[512,512]{1,0:T(8,128)(2,1)}, bf16[512,512]{1,0:T(8,128)(2,1)S(1)}, u32[]{:S(2)}, u32[]{:S(2)}) collective-permute-start(bf16[512,512]{1,0:T(8,128)(2,1)} %bitcast.15), channel_id=1, source_target_pairs={{1,2},{2,1},{3,4},{4,3},{5,6},{6,5},{7,8},{8,7},{9,10},{10,9},{11,... | collective-permute-start | bytes 1572872 | tf_op jit(solution)/shard_map/ppermute | solution.py:170
  4.2 2.0 %collective-permute-done.1 = bf16[3,3,256,512]{3,2,1,0:T(8,128)(2,1)S(1)} collective-permute-done((bf16[3,3,256,512]{3,2,1,0:T(8,128)(2,1)}, bf16[3,3,256,512]{3,2,1,0:T(8,128)(2,1)S(1)}, u32[]{:S(2)}, u32[]{:S(2)}) %collective-permute-start.1) | collective-permute-done | bytes 2359328 | tf_op jit(solution)/shard_map/ppermute | solution.py:16
  6.2 0.0 copy-start
  6.2 1.4 %copy-done = bf16[3,3,256,512]{3,2,1,0:T(8,128)(2,1)} copy-done((bf16[3,3,256,512]{3,2,1,0:T(8,128)(2,1)}, bf16[3,3,256,512]{3,2,1,0:T(8,128)(2,1)S(1)}, u32[]{:S(2)}) %copy-start) | copy-done | bytes 2359320
  7.6 7.8 %shard_map.56.ca.cb.cur_ref = bf16[512,512]{1,0:T(8,128)(2,1)} custom-call(s32[1]{0:T(128)} %bitcast.side_ref, bf16[512,512]{1,0:T(8,128)(2,1)} %bitcast.16, bf16[512,512]{1,0:T(8,128)(2,1)} %bitcast.17, bf16[2304,512]{1,0:T(8,128)(2,1)} %bitcast.11, bf16[2304,512]{1,0:T(8,128)(2,1)} %bitcast.13, f32[1,512]{1,0:T(1,128)} %bitcast.19, f32[1,512]{1,0:T(1,128)} %bitcast.21), custom_call_target="tpu_custom_call" | custom-call | tf_op jit(solution)/shard_map/pallas_call | solution.py:78
  15.4 0.4 %collective-permute-start.2 = (bf16[512,512]{1,0:T(8,128)(2,1)}, bf16[512,512]{1,0:T(8,128)(2,1)S(1)}, u32[]{:S(2)}, u32[]{:S(2)}) collective-permute-start(bf16[512,512]{1,0:T(8,128)(2,1)} %shard_map.56.ca.cb.cur_ref), channel_id=1, source_target_pairs={{0,1},{1,0},{2,3},{3,2},{4,5},{5,4},{6,7},{7,6},{8,9},{9,8},{10,11... | collective-permute-start | bytes 1572872 | tf_op jit(solution)/shard_map/ppermute | solution.py:16
  15.8 0.6 %pad_add_fusion.s_ref = s32[3]{0:T(128)} fusion(s32[1]{0:T(128)} %bitcast.2, s32[1]{0:T(128)} %bitcast.1, s32[1]{0:T(128)} %bitcast.side_ref), kind=kLoop, calls=%fused_computation | loop fusion | flops 6 | bytes 24 | tf_op jit(solution)/shard_map/stack | solution.py:185
  16.3 0.6 %collective-permute-done.xa_ref.xb_ref = bf16[512,512]{1,0:T(8,128)(2,1)S(1)} collective-permute-done((bf16[512,512]{1,0:T(8,128)(2,1)}, bf16[512,512]{1,0:T(8,128)(2,1)S(1)}, u32[]{:S(2)}, u32[]{:S(2)}) %collective-permute-start) | collective-permute-done | bytes 524320 | tf_op jit(solution)/shard_map/ppermute | solution.py:170
  17.0 0.0 copy-start.1
  17.0 0.8 %copy-done.1 = bf16[512,512]{1,0:T(8,128)(2,1)} copy-done((bf16[512,512]{1,0:T(8,128)(2,1)}, bf16[512,512]{1,0:T(8,128)(2,1)S(1)}, u32[]{:S(2)}) %copy-start.1) | copy-done | bytes 524312
  17.8 7.8 %shard_map.55.ea.eb = bf16[512,512]{1,0:T(8,128)(2,1)} custom-call(s32[1]{0:T(128)} %bitcast.side_ref, bf16[512,512]{1,0:T(8,128)(2,1)} %copy-done.1, bf16[512,512]{1,0:T(8,128)(2,1)} %copy-done.1, bf16[2304,512]{1,0:T(8,128)(2,1)} %bitcast.12, bf16[2304,512]{1,0:T(8,128)(2,1)} %bitcast.14, f32[1,512]{1,0:T(1,128)} %bitcast.20, f32[1,512]{1,0:T(1,128)} %bitcast.22), custom_call_target="tpu_custom_call" | custom-call | tf_op jit(solution)/shard_map/pallas_call | solution.py:78
  25.6 0.0 collective-permute-done.3
  25.6 0.0 collective-permute-done.2.pa.pb
  25.6 0.0 copy-start.2
  25.6 0.8 %copy-done.2 = bf16[512,512]{1,0:T(8,128)(2,1)} copy-done((bf16[512,512]{1,0:T(8,128)(2,1)}, bf16[512,512]{1,0:T(8,128)(2,1)S(1)}, u32[]{:S(2)}) %copy-start.2) | copy-done | bytes 524312
  26.4 4.6 %shard_map.57 = bf16[512,512]{1,0:T(8,128)(2,1)} custom-call(s32[3]{0:T(128)} %pad_add_fusion.s_ref, bf16[512,512]{1,0:T(8,128)(2,1)} %shard_map.55.ea.eb, bf16[512,512]{1,0:T(8,128)(2,1)} %shard_map.55.ea.eb, bf16[512,512]{1,0:T(8,128)(2,1)} %copy-done.2, bf16[512,512]{1,0:T(8,128)(2,1)} %copy-done.2, bf16[512,512]{1,0:T(8,128)(2,1)} %shard_map.56.ca.cb.cur_ref, ...), custom_call_target="tpu_custom_call" | custom-call | tf_op jit(solution)/shard_map/pallas_call | solution.py:137
Async XLA Ops:
  0.0 6.2 %collective-permute-start.1 = (bf16[3,3,256,512]{3,2,1,0:T(8,128)(2,1)}, bf16[3,3,256,512]{3,2,1,0:T(8,128)(2,1)S(1)}, u32[]{:S(2)}, u32[]{:S(2)}) collective-permute-start(bf16[3,3,256,512]{3,2,1,0:T(8,128)(2,1)} %param.6), channel_id=1, source_target_pairs={{0,1},{1,0},{2,3},{3,2},{4,5},{5,4},{6,7},{7,6},{8,9},{9,8},{10,11... | collective-permute-start | bytes 7077896 | tf_op jit(solution)/shard_map/ppermute | solution.py:16
  0.7 24.9 %collective-permute-start.3 = (bf16[3,256,512]{2,1,0:T(8,128)(2,1)}, bf16[3,256,512]{2,1,0:T(8,128)(2,1)}, u32[]{:S(2)}, u32[]{:S(2)}) collective-permute-start(bf16[3,256,512]{2,1,0:T(8,128)(2,1)} %param.9), channel_id=1, source_target_pairs={{0,1},{1,0},{2,3},{3,2},{4,5},{5,4},{6,7},{7,6},{8,9},{9,8},{10,11... | collective-permute-start | bytes 2359304 | tf_op jit(solution)/shard_map/ppermute | solution.py:16
  0.7 16.3 %collective-permute-start = (bf16[512,512]{1,0:T(8,128)(2,1)}, bf16[512,512]{1,0:T(8,128)(2,1)S(1)}, u32[]{:S(2)}, u32[]{:S(2)}) collective-permute-start(bf16[512,512]{1,0:T(8,128)(2,1)} %bitcast.15), channel_id=1, source_target_pairs={{1,2},{2,1},{3,4},{4,3},{5,6},{6,5},{7,8},{8,7},{9,10},{10,9},{11,... | collective-permute-start | bytes 1572872 | tf_op jit(solution)/shard_map/ppermute | solution.py:170
  6.2 1.4 %copy-start = (bf16[3,3,256,512]{3,2,1,0:T(8,128)(2,1)}, bf16[3,3,256,512]{3,2,1,0:T(8,128)(2,1)S(1)}, u32[]{:S(2)}) copy-start(bf16[3,3,256,512]{3,2,1,0:T(8,128)(2,1)S(1)} %collective-permute-done.1) | copy-start | bytes 7077892
  15.4 10.2 %collective-permute-start.2 = (bf16[512,512]{1,0:T(8,128)(2,1)}, bf16[512,512]{1,0:T(8,128)(2,1)S(1)}, u32[]{:S(2)}, u32[]{:S(2)}) collective-permute-start(bf16[512,512]{1,0:T(8,128)(2,1)} %shard_map.56.ca.cb.cur_ref), channel_id=1, source_target_pairs={{0,1},{1,0},{2,3},{3,2},{4,5},{5,4},{6,7},{7,6},{8,9},{9,8},{10,11... | collective-permute-start | bytes 1572872 | tf_op jit(solution)/shard_map/ppermute | solution.py:16
  17.0 0.8 %copy-start.1 = (bf16[512,512]{1,0:T(8,128)(2,1)}, bf16[512,512]{1,0:T(8,128)(2,1)S(1)}, u32[]{:S(2)}) copy-start(bf16[512,512]{1,0:T(8,128)(2,1)S(1)} %collective-permute-done.xa_ref.xb_ref) | copy-start | bytes 1572868
  25.6 0.8 %copy-start.2 = (bf16[512,512]{1,0:T(8,128)(2,1)}, bf16[512,512]{1,0:T(8,128)(2,1)S(1)}, u32[]{:S(2)}) copy-start(bf16[512,512]{1,0:T(8,128)(2,1)S(1)} %collective-permute-done.2.pa.pb) | copy-start | bytes 1572868

commit v4 on v3

--- a/solution.py
+++ b/solution.py
@@ -66,21 +66,21 @@
     o_ref[...] = (v / (1.0 + jnp.exp(-v))).astype(o_ref.dtype)
 
 
-def conv_norm(frame, w_mine, w_other, gain, shift, side, width, split=2):
+def conv_norm(frame, w_mine, w_other, gain, shift, side, width, split, part):
     rows, channels = frame.shape
     half = w_mine.shape[2]
     outputs = w_mine.shape[3]
     group = outputs // GROUPS
     block = outputs // split
     kernel = functools.partial(conv_norm_kernel, width=width, group=group)
-    weight_block = pl.BlockSpec((9 * half, block), lambda n, s: (0, n))
-    row_block = pl.BlockSpec((1, block), lambda n, s: (0, n))
+    weight_block = pl.BlockSpec((9 * half, block), lambda n, s: (0, part))
+    row_block = pl.BlockSpec((1, block), lambda n, s: (0, part))
     return pl.pallas_call(
         kernel,
-        out_shape=jax.ShapeDtypeStruct((rows, outputs), jnp.bfloat16),
+        out_shape=jax.ShapeDtypeStruct((rows, block), jnp.bfloat16),
         grid_spec=pltpu.PrefetchScalarGridSpec(
             num_scalar_prefetch=1,
-            grid=(split,),
+            grid=(1,),
             in_specs=[
                 pl.BlockSpec((rows, half), lambda n, s: (0, s[0])),
                 pl.BlockSpec((rows, half), lambda n, s: (0, 1 - s[0])),
@@ -89,7 +89,7 @@
                 row_block,
                 row_block,
             ],
-            out_specs=pl.BlockSpec((rows, block), lambda n, s: (0, n)),
+            out_specs=pl.BlockSpec((rows, block), lambda n, s: (0, 0)),
             scratch_shapes=[pltpu.VMEM((2, rows, 9 * half), jnp.bfloat16)],
         ),
         compiler_params=pltpu.CompilerParams(dimension_semantics=("arbitrary",)),
@@ -167,16 +167,22 @@
         if 0 <= target < blocks and min(j, target) % CLIP != CLIP - 1:
             route.append((j, target))
     frame = video.reshape(pixels, channels)
-    edge_video = lax.ppermute(frame, ("video", "fsdp"), route)
     other_spatial = swap_pair(w_spatial)
     other_time = swap_pair(w_time)
 
     gain = norm_gain.reshape(1, channels)
     shift = norm_shift.reshape(1, channels)
     sides = side.reshape(1).astype(jnp.int32)
-    hidden = conv_norm(frame, w_spatial, other_spatial, gain, shift, sides, width)
-    partner = swap_pair(hidden)
-    edge = conv_norm(edge_video, w_spatial, other_spatial, gain, shift, sides, width)
+    split = 2
+    pieces, edges, partners = [], [], []
+    for part in range(split):
+        piece = conv_norm(frame, w_spatial, other_spatial, gain, shift, sides, width, split, part)
+        pieces.append(piece)
+        edges.append(lax.ppermute(piece, ("video", "fsdp"), route))
+        partners.append(swap_pair(piece))
+    hidden = jnp.concatenate(pieces, axis=1)
+    edge = jnp.concatenate(edges, axis=1)
+    partner = jnp.concatenate(partners, axis=1)
 
     keep_prev = (position % CLIP != 0).astype(jnp.int32)
     keep_next = (position % CLIP != CLIP - 1).astype(jnp.int32)

time: 31.2 us -> 39.4 us (1.26)
  waiting for transfers between devices: 2.63 us -> 11.9 us
  Pallas kernels: 20.2 us -> 14.2 us
  other arithmetic: 0.59 us -> 4.07 us
  starting transfers between devices: 4.55 us -> 6.74 us
  local copies, waits for them, and re-layouts: 2.99 us -> 2.31 us
    ppermute x1 -> x2, waiting for transfers between devices: 0.65 us -> 7.52 us  [body(): edges.append(lax.ppermute(piece, ('video', 'fsdp'), route))]
    pallas_call x2, Pallas kernels: 15.6 us -> 9.59 us  [conv_norm(): pl.pallas_call(kernel, out_shape=jax.ShapeDtypeStruct((rows, block), jnp....]
    concatenate x0 -> x3, other arithmetic: none -> 3.47 us  [the longest x1 1.78 us: body(): hidden = jnp.concatenate(pieces, axis=1)]
    ppermute x3 -> x4, waiting for transfers between devices: 1.99 us -> 4.38 us  [swap_pair(): return lax.ppermute(block, 'fsdp', [(0, 1), (1, 0)])]
    ppermute x1 -> x2, starting transfers between devices: 3.5 us -> 5.55 us  [body(): edges.append(lax.ppermute(piece, ('video', 'fsdp'), route))]
    unnamed x6, local copies, waits for them, and re-layouts: 2.99 us -> 2.31 us
    ppermute x3 -> x4, starting transfers between devices: 1.05 us -> 1.19 us  [swap_pair(): return lax.ppermute(block, 'fsdp', [(0, 1), (1, 0)])]
  transfers between devices with their start and end apart: 4 -> 6, of which waited for: 2 -> 3; matrix products, arithmetic and copies ran while one was open for 2% -> 10% of each run, Pallas kernels for 50% -> 24%
where the time goes in v4:
time: 39.4 us; the launch traced here: 39.2 us
  Pallas kernels  14.2 us (36%)
  waiting for transfers between devices  11.9 us (30%)
  starting transfers between devices  6.74 us (17%)
  other arithmetic  4.07 us (10%)
  local copies, waits for them, and re-layouts  2.31 us (6%)
    pallas_call x2, Pallas kernels, conv_norm(): pl.pallas_call(kernel, out_shape=jax.ShapeDtypeStruct((rows, block), jnp....  9.59 us
    ppermute x2, waiting for transfers between devices, body(): edges.append(lax.ppermute(piece, ('video', 'fsdp'), route))  7.52 us
    ppermute x2, starting transfers between devices, body(): edges.append(lax.ppermute(piece, ('video', 'fsdp'), route))  5.55 us
    pallas_call x1, Pallas kernels, temporal(): pl.pallas_call(temporal_kernel, out_shape=jax.ShapeDtypeStruct((rows, out...  4.56 us
    ppermute x4, waiting for transfers between devices, swap_pair(): return lax.ppermute(block, 'fsdp', [(0, 1), (1, 0)])  4.38 us
    unnamed x6, local copies, waits for them, and re-layouts  2.31 us
    concatenate x1, other arithmetic, body(): hidden = jnp.concatenate(pieces, axis=1)  1.78 us
    ppermute x4, starting transfers between devices, swap_pair(): return lax.ppermute(block, 'fsdp', [(0, 1), (1, 0)])  1.19 us
  transfers between devices with their start and end apart: 6, of which 3 were waited for; matrix products, arithmetic and copies ran while one was open for 10% of the time, Pallas kernels for 24%

profile of v4, /device:TPU:17, one launch (start us, length us, event | category | flops | bytes accessed | tf_op | source)
XLA Modules:
  0.0 39.2 jit_solution(13854614418265745075)
XLA Ops:
  0.0 0.7 %collective-permute-start = (bf16[3,3,256,512]{3,2,1,0:T(8,128)(2,1)}, bf16[3,3,256,512]{3,2,1,0:T(8,128)(2,1)S(1)}, u32[]{:S(2)}, u32[]{:S(2)}) collective-permute-start(bf16[3,3,256,512]{3,2,1,0:T(8,128)(2,1)} %param.6), channel_id=1, source_target_pairs={{0,1},{1,0},{2,3},{3,2},{4,5},{5,4},{6,7},{7,6},{8,9},{9,8},{10,11... | collective-permute-start | bytes 7077896 | tf_op jit(solution)/shard_map/ppermute | solution.py:16
  0.7 0.0 collective-permute-start.5
  0.7 4.4 %collective-permute-done = bf16[3,3,256,512]{3,2,1,0:T(8,128)(2,1)S(1)} collective-permute-done((bf16[3,3,256,512]{3,2,1,0:T(8,128)(2,1)}, bf16[3,3,256,512]{3,2,1,0:T(8,128)(2,1)S(1)}, u32[]{:S(2)}, u32[]{:S(2)}) %collective-permute-start) | collective-permute-done | bytes 2359328 | tf_op jit(solution)/shard_map/ppermute | solution.py:16
  5.1 1.4 %copy-done = bf16[3,3,256,512]{3,2,1,0:T(8,128)(2,1)} copy-done((bf16[3,3,256,512]{3,2,1,0:T(8,128)(2,1)}, bf16[3,3,256,512]{3,2,1,0:T(8,128)(2,1)S(1)}, u32[]{:S(2)}) %copy-start) | copy-done | bytes 2359320
  6.5 4.8 %shard_map.56 = bf16[512,256]{1,0:T(8,128)(2,1)} custom-call(s32[1]{0:T(128)} %bitcast.side_ref, bf16[512,512]{1,0:T(8,128)(2,1)} %bitcast.15, bf16[512,512]{1,0:T(8,128)(2,1)} %bitcast.16, bf16[2304,512]{1,0:T(8,128)(2,1)} %bitcast.11, bf16[2304,512]{1,0:T(8,128)(2,1)} %bitcast.13, f32[1,512]{1,0:T(1,128)} %bitcast.21, f32[1,512]{1,0:T(1,128)} %bitcast.23), custom_call_target="tpu_custom_call" | custom-call | tf_op jit(solution)/shard_map/pallas_call | solution.py:78
  11.2 0.0 copy-start.1
  11.2 4.8 %shard_map.55 = bf16[512,256]{1,0:T(8,128)(2,1)} custom-call(s32[1]{0:T(128)} %bitcast.side_ref, bf16[512,512]{1,0:T(8,128)(2,1)} %bitcast.17, bf16[512,512]{1,0:T(8,128)(2,1)} %bitcast.18, bf16[2304,512]{1,0:T(8,128)(2,1)} %bitcast.12, bf16[2304,512]{1,0:T(8,128)(2,1)} %bitcast.14, f32[1,512]{1,0:T(1,128)} %bitcast.22, f32[1,512]{1,0:T(1,128)} %bitcast.24), custom_call_target="tpu_custom_call" | custom-call | tf_op jit(solution)/shard_map/pallas_call | solution.py:78
  16.1 0.4 collective-permute-start.3
  16.4 0.0 copy-done.1
  16.4 0.1 collective-permute-start.4
  16.6 3.4 %collective-permute-start.1 = (bf16[512,256]{1,0:T(8,128)(2,1)}, bf16[512,256]{1,0:T(8,128)(2,1)S(1)}, u32[]{:S(2)}, u32[]{:S(2)}) collective-permute-start(bf16[512,256]{1,0:T(8,128)(2,1)} %shard_map.55), channel_id=1, source_target_pairs={{1,2},{2,1},{3,4},{4,3},{5,6},{6,5},{7,8},{8,7},{9,10},{10,9},{11,... | collective-permute-start | bytes 786440 | tf_op jit(solution)/shard_map/ppermute | solution.py:181
  19.9 2.2 %collective-permute-start.2 = (bf16[512,256]{1,0:T(8,128)(2,1)S(1)}, bf16[512,256]{1,0:T(8,128)(2,1)S(1)}, u32[]{:S(2)}, u32[]{:S(2)}) collective-permute-start(bf16[512,256]{1,0:T(8,128)(2,1)S(1)} %copy-done.1), channel_id=1, source_target_pairs={{1,2},{2,1},{3,4},{4,3},{5,6},{6,5},{7,8},{8,7},{9,10},{10,9},{11,... | collective-permute-start | bytes 786440 | tf_op jit(solution)/shard_map/ppermute | solution.py:181
  22.1 0.6 %pad_add_fusion.s_ref = s32[3]{0:T(128)} fusion(s32[1]{0:T(128)} %bitcast.2, s32[1]{0:T(128)} %bitcast.1, s32[1]{0:T(128)} %bitcast.side_ref), kind=kLoop, calls=%fused_computation.3 | loop fusion | flops 6 | bytes 24 | tf_op jit(solution)/shard_map/stack | solution.py:191
  22.7 1.8 %pad_maximum_fusion.2.ca.cb.cur_ref = bf16[512,512]{1,0:T(8,128)(2,1)} fusion(bf16[512,256]{1,0:T(8,128)(2,1)S(1)} %copy-done.1, bf16[512,256]{1,0:T(8,128)(2,1)} %shard_map.55), kind=kLoop, calls=%fused_computation.2 | loop fusion | flops 1048576 | bytes 1048576 | tf_op jit(solution)/shard_map/concatenate | solution.py:183
  24.5 0.0 collective-permute-done.3
  24.5 0.0 collective-permute-done.4
  24.5 0.9 %pad_maximum_fusion.1.pa.pb = bf16[512,512]{1,0:T(8,128)(2,1)} fusion(bf16[512,256]{1,0:T(8,128)(2,1)S(1)} %collective-permute-done.4, bf16[512,256]{1,0:T(8,128)(2,1)S(1)} %collective-permute-done.3), kind=kLoop, calls=%fused_computation.1 | loop fusion | flops 1048576 | bytes 1048576 | tf_op jit(solution)/shard_map/concatenate | solution.py:185
  25.4 4.7 %collective-permute-done.1 = bf16[512,256]{1,0:T(8,128)(2,1)S(1)} collective-permute-done((bf16[512,256]{1,0:T(8,128)(2,1)}, bf16[512,256]{1,0:T(8,128)(2,1)S(1)}, u32[]{:S(2)}, u32[]{:S(2)}) %collective-permute-start.1) | collective-permute-done | bytes 262176 | tf_op jit(solution)/shard_map/ppermute | solution.py:181
  30.1 2.8 %collective-permute-done.2 = bf16[512,256]{1,0:T(8,128)(2,1)S(1)} collective-permute-done((bf16[512,256]{1,0:T(8,128)(2,1)S(1)}, bf16[512,256]{1,0:T(8,128)(2,1)S(1)}, u32[]{:S(2)}, u32[]{:S(2)}) %collective-permute-start.2) | collective-permute-done | bytes 262176 | tf_op jit(solution)/shard_map/ppermute | solution.py:181
  32.9 0.8 %pad_maximum_fusion.ea.eb = bf16[512,512]{1,0:T(8,128)(2,1)} fusion(bf16[512,256]{1,0:T(8,128)(2,1)S(1)} %collective-permute-done.2, bf16[512,256]{1,0:T(8,128)(2,1)S(1)} %collective-permute-done.1), kind=kLoop, calls=%fused_computation | loop fusion | flops 1048576 | bytes 1048576 | tf_op jit(solution)/shard_map/concatenate | solution.py:184
  33.7 0.0 collective-permute-done.5
  33.7 0.0 copy-start.2
  33.7 0.9 %copy-done.2 = bf16[3,256,512]{2,1,0:T(8,128)(2,1)} copy-done((bf16[3,256,512]{2,1,0:T(8,128)(2,1)}, bf16[3,256,512]{2,1,0:T(8,128)(2,1)S(1)}, u32[]{:S(2)}) %copy-start.2) | copy-done | bytes 786456
  34.6 4.6 %shard_map.57 = bf16[512,512]{1,0:T(8,128)(2,1)} custom-call(s32[3]{0:T(128)} %pad_add_fusion.s_ref, bf16[512,512]{1,0:T(8,128)(2,1)} %pad_maximum_fusion.ea.eb, bf16[512,512]{1,0:T(8,128)(2,1)} %pad_maximum_fusion.ea.eb, bf16[512,512]{1,0:T(8,128)(2,1)} %pad_maximum_fusion.1.pa.pb, bf16[512,512]{1,0:T(8,128)(2,1)} %pad_maximum_fusion.1.pa.pb, ...), custom_call_target="tpu_custom_call" | custom-call | tf_op jit(solution)/shard_map/pallas_call | solution.py:137
  (1 shorter events, 0.0 us)
Async XLA Ops:
  0.0 5.0 %collective-permute-start = (bf16[3,3,256,512]{3,2,1,0:T(8,128)(2,1)}, bf16[3,3,256,512]{3,2,1,0:T(8,128)(2,1)S(1)}, u32[]{:S(2)}, u32[]{:S(2)}) collective-permute-start(bf16[3,3,256,512]{3,2,1,0:T(8,128)(2,1)} %param.6), channel_id=1, source_target_pairs={{0,1},{1,0},{2,3},{3,2},{4,5},{5,4},{6,7},{7,6},{8,9},{9,8},{10,11... | collective-permute-start | bytes 7077896 | tf_op jit(solution)/shard_map/ppermute | solution.py:16
  0.7 33.1 %collective-permute-start.5 = (bf16[3,256,512]{2,1,0:T(8,128)(2,1)}, bf16[3,256,512]{2,1,0:T(8,128)(2,1)S(1)}, u32[]{:S(2)}, u32[]{:S(2)}) collective-permute-start(bf16[3,256,512]{2,1,0:T(8,128)(2,1)} %param.9), channel_id=1, source_target_pairs={{0,1},{1,0},{2,3},{3,2},{4,5},{5,4},{6,7},{7,6},{8,9},{9,8},{10,11... | collective-permute-start | bytes 2359304 | tf_op jit(solution)/shard_map/ppermute | solution.py:16
  5.0 1.4 %copy-start = (bf16[3,3,256,512]{3,2,1,0:T(8,128)(2,1)}, bf16[3,3,256,512]{3,2,1,0:T(8,128)(2,1)S(1)}, u32[]{:S(2)}) copy-start(bf16[3,3,256,512]{3,2,1,0:T(8,128)(2,1)S(1)} %collective-permute-done) | copy-start | bytes 7077892
  11.2 5.2 %copy-start.1 = (bf16[512,256]{1,0:T(8,128)(2,1)S(1)}, bf16[512,256]{1,0:T(8,128)(2,1)}, u32[]{:S(2)}) copy-start(bf16[512,256]{1,0:T(8,128)(2,1)} %shard_map.56) | copy-start | bytes 786436
  16.1 8.5 %collective-permute-start.3 = (bf16[512,256]{1,0:T(8,128)(2,1)}, bf16[512,256]{1,0:T(8,128)(2,1)S(1)}, u32[]{:S(2)}, u32[]{:S(2)}) collective-permute-start(bf16[512,256]{1,0:T(8,128)(2,1)} %shard_map.55), channel_id=1, source_target_pairs={{0,1},{1,0},{2,3},{3,2},{4,5},{5,4},{6,7},{7,6},{8,9},{9,8},{10,11... | collective-permute-start | bytes 786440 | tf_op jit(solution)/shard_map/ppermute | solution.py:16
  16.4 8.1 %collective-permute-start.4 = (bf16[512,256]{1,0:T(8,128)(2,1)S(1)}, bf16[512,256]{1,0:T(8,128)(2,1)S(1)}, u32[]{:S(2)}, u32[]{:S(2)}) collective-permute-start(bf16[512,256]{1,0:T(8,128)(2,1)S(1)} %copy-done.1), channel_id=1, source_target_pairs={{0,1},{1,0},{2,3},{3,2},{4,5},{5,4},{6,7},{7,6},{8,9},{9,8},{10,11... | collective-permute-start | bytes 786440 | tf_op jit(solution)/shard_map/ppermute | solution.py:16
  16.6 13.5 %collective-permute-start.1 = (bf16[512,256]{1,0:T(8,128)(2,1)}, bf16[512,256]{1,0:T(8,128)(2,1)S(1)}, u32[]{:S(2)}, u32[]{:S(2)}) collective-permute-start(bf16[512,256]{1,0:T(8,128)(2,1)} %shard_map.55), channel_id=1, source_target_pairs={{1,2},{2,1},{3,4},{4,3},{5,6},{6,5},{7,8},{8,7},{9,10},{10,9},{11,... | collective-permute-start | bytes 786440 | tf_op jit(solution)/shard_map/ppermute | solution.py:181
  19.9 12.9 %collective-permute-start.2 = (bf16[512,256]{1,0:T(8,128)(2,1)S(1)}, bf16[512,256]{1,0:T(8,128)(2,1)S(1)}, u32[]{:S(2)}, u32[]{:S(2)}) collective-permute-start(bf16[512,256]{1,0:T(8,128)(2,1)S(1)} %copy-done.1), channel_id=1, source_target_pairs={{1,2},{2,1},{3,4},{4,3},{5,6},{6,5},{7,8},{8,7},{9,10},{10,9},{11,... | collective-permute-start | bytes 786440 | tf_op jit(solution)/shard_map/ppermute | solution.py:181
  33.7 0.9 %copy-start.2 = (bf16[3,256,512]{2,1,0:T(8,128)(2,1)}, bf16[3,256,512]{2,1,0:T(8,128)(2,1)S(1)}, u32[]{:S(2)}) copy-start(bf16[3,256,512]{2,1,0:T(8,128)(2,1)S(1)} %collective-permute-done.5) | copy-start | bytes 2359300

commit v5 on v3

--- a/solution.py
+++ b/solution.py
@@ -167,7 +167,6 @@
         if 0 <= target < blocks and min(j, target) % CLIP != CLIP - 1:
             route.append((j, target))
     frame = video.reshape(pixels, channels)
-    edge_video = lax.ppermute(frame, ("video", "fsdp"), route)
     other_spatial = swap_pair(w_spatial)
     other_time = swap_pair(w_time)
 
@@ -175,8 +174,8 @@
     shift = norm_shift.reshape(1, channels)
     sides = side.reshape(1).astype(jnp.int32)
     hidden = conv_norm(frame, w_spatial, other_spatial, gain, shift, sides, width)
+    edge = lax.ppermute(hidden, ("video", "fsdp"), route)
     partner = swap_pair(hidden)
-    edge = conv_norm(edge_video, w_spatial, other_spatial, gain, shift, sides, width)
 
     keep_prev = (position % CLIP != 0).astype(jnp.int32)
     keep_next = (position % CLIP != CLIP - 1).astype(jnp.int32)

time: 31.2 us -> 36.3 us (1.16)
  waiting for transfers between devices: 2.63 us -> 16.6 us
  Pallas kernels: 20.2 us -> 12.3 us
  local copies, waits for them, and re-layouts: 2.99 us -> 2.4 us
  starting transfers between devices: 4.55 us -> 4.13 us
    ppermute x1, waiting for transfers between devices: 0.65 us -> 12.2 us  [body(): edge = lax.ppermute(hidden, ('video', 'fsdp'), route)]
    pallas_call x2 -> x1, Pallas kernels: 15.6 us -> 7.78 us  [conv_norm(): pl.pallas_call(kernel, out_shape=jax.ShapeDtypeStruct((rows, outputs), jn...]
    ppermute x3, waiting for transfers between devices: 1.99 us -> 4.37 us  [swap_pair(): return lax.ppermute(block, 'fsdp', [(0, 1), (1, 0)])]
    unnamed x6 -> x8, local copies, waits for them, and re-layouts: 2.99 us -> 2.4 us
  transfers between devices with their start and end apart: 4 -> 4, of which waited for: 2 -> 2; matrix products, arithmetic and copies ran while one was open for 2% -> 2% of each run, Pallas kernels for 50% -> 22%
where the time goes in v5:
time: 36.3 us; the launch traced here: 36.1 us
  waiting for transfers between devices  16.6 us (46%)
  Pallas kernels  12.3 us (34%)
  starting transfers between devices  4.13 us (11%)
  local copies, waits for them, and re-layouts  2.4 us (7%)
  other arithmetic  0.61 us (2%)
    ppermute x1, waiting for transfers between devices, body(): edge = lax.ppermute(hidden, ('video', 'fsdp'), route)  12.2 us
    pallas_call x1, Pallas kernels, conv_norm(): pl.pallas_call(kernel, out_shape=jax.ShapeDtypeStruct((rows, outputs), jn...  7.78 us
    pallas_call x1, Pallas kernels, temporal(): pl.pallas_call(temporal_kernel, out_shape=jax.ShapeDtypeStruct((rows, out...  4.56 us
    ppermute x3, waiting for transfers between devices, swap_pair(): return lax.ppermute(block, 'fsdp', [(0, 1), (1, 0)])  4.37 us
    ppermute x1, starting transfers between devices, body(): edge = lax.ppermute(hidden, ('video', 'fsdp'), route)  3.37 us
    unnamed x8, local copies, waits for them, and re-layouts  2.4 us
    ppermute x3, starting transfers between devices, swap_pair(): return lax.ppermute(block, 'fsdp', [(0, 1), (1, 0)])  0.77 us
  transfers between devices with their start and end apart: 4, of which 2 were waited for; matrix products, arithmetic and copies ran while one was open for 2% of the time, Pallas kernels for 22%

profile of v5, /device:TPU:17, one launch (start us, length us, event | category | flops | bytes accessed | tf_op | source)
XLA Modules:
  0.0 36.1 jit_solution(14661049339681686598)
XLA Ops:
  0.0 0.7 %collective-permute-start = (bf16[3,3,256,512]{3,2,1,0:T(8,128)(2,1)}, bf16[3,3,256,512]{3,2,1,0:T(8,128)(2,1)S(1)}, u32[]{:S(2)}, u32[]{:S(2)}) collective-permute-start(bf16[3,3,256,512]{3,2,1,0:T(8,128)(2,1)} %param.6), channel_id=1, source_target_pairs={{0,1},{1,0},{2,3},{3,2},{4,5},{5,4},{6,7},{7,6},{8,9},{9,8},{10,11... | collective-permute-start | bytes 7077896 | tf_op jit(solution)/shard_map/ppermute | solution.py:16
  0.7 0.0 collective-permute-start.3
  0.7 4.4 %collective-permute-done = bf16[3,3,256,512]{3,2,1,0:T(8,128)(2,1)S(1)} collective-permute-done((bf16[3,3,256,512]{3,2,1,0:T(8,128)(2,1)}, bf16[3,3,256,512]{3,2,1,0:T(8,128)(2,1)S(1)}, u32[]{:S(2)}, u32[]{:S(2)}) %collective-permute-start) | collective-permute-done | bytes 2359328 | tf_op jit(solution)/shard_map/ppermute | solution.py:16
  5.0 0.0 copy-start
  5.1 1.4 %copy-done = bf16[3,3,256,512]{3,2,1,0:T(8,128)(2,1)} copy-done((bf16[3,3,256,512]{3,2,1,0:T(8,128)(2,1)}, bf16[3,3,256,512]{3,2,1,0:T(8,128)(2,1)S(1)}, u32[]{:S(2)}) %copy-start) | copy-done | bytes 2359320
  6.5 7.8 %shard_map.55.ca.cb.cur_ref = bf16[512,512]{1,0:T(8,128)(2,1)} custom-call(s32[1]{0:T(128)} %bitcast.side_ref, bf16[512,512]{1,0:T(8,128)(2,1)} %bitcast.13, bf16[512,512]{1,0:T(8,128)(2,1)} %bitcast.14, bf16[2304,512]{1,0:T(8,128)(2,1)} %bitcast.11, bf16[2304,512]{1,0:T(8,128)(2,1)} %bitcast.12, f32[1,512]{1,0:T(1,128)} %bitcast.17, f32[1,512]{1,0:T(1,128)} %bitcast.18), custom_call_target="tpu_custom_call" | custom-call | tf_op jit(solution)/shard_map/pallas_call | solution.py:78
  14.2 3.4 %collective-permute-start.1 = (bf16[512,512]{1,0:T(8,128)(2,1)}, bf16[512,512]{1,0:T(8,128)(2,1)S(1)}, u32[]{:S(2)}, u32[]{:S(2)}) collective-permute-start(bf16[512,512]{1,0:T(8,128)(2,1)} %shard_map.55.ca.cb.cur_ref), channel_id=1, source_target_pairs={{1,2},{2,1},{3,4},{4,3},{5,6},{6,5},{7,8},{8,7},{9,10},{10,9},{11,... | collective-permute-start | bytes 1572872 | tf_op jit(solution)/shard_map/ppermute | solution.py:177
  17.6 0.1 collective-permute-start.2
  17.7 0.6 %pad_add_fusion.s_ref = s32[3]{0:T(128)} fusion(s32[1]{0:T(128)} %bitcast.2, s32[1]{0:T(128)} %bitcast.1, s32[1]{0:T(128)} %bitcast.side_ref), kind=kLoop, calls=%fused_computation | loop fusion | flops 6 | bytes 24 | tf_op jit(solution)/shard_map/stack | solution.py:184
  18.3 0.0 collective-permute-done.3
  18.3 0.0 copy-start.3
  18.3 12.2 %collective-permute-done.1.ea.eb = bf16[512,512]{1,0:T(8,128)(2,1)S(1)} collective-permute-done((bf16[512,512]{1,0:T(8,128)(2,1)}, bf16[512,512]{1,0:T(8,128)(2,1)S(1)}, u32[]{:S(2)}, u32[]{:S(2)}) %collective-permute-start.1) | collective-permute-done | bytes 524320 | tf_op jit(solution)/shard_map/ppermute | solution.py:177
  30.6 0.0 copy-start.1
  30.6 0.0 collective-permute-done.2.pa.pb
  30.6 0.0 copy-start.2
  30.6 0.0 copy-done.3
  30.6 0.8 %copy-done.1 = bf16[512,512]{1,0:T(8,128)(2,1)} copy-done((bf16[512,512]{1,0:T(8,128)(2,1)}, bf16[512,512]{1,0:T(8,128)(2,1)S(1)}, u32[]{:S(2)}) %copy-start.1) | copy-done | bytes 524312
  31.3 0.2 copy-done.2
  31.6 4.6 %shard_map.56 = bf16[512,512]{1,0:T(8,128)(2,1)} custom-call(s32[3]{0:T(128)} %pad_add_fusion.s_ref, bf16[512,512]{1,0:T(8,128)(2,1)} %copy-done.1, bf16[512,512]{1,0:T(8,128)(2,1)} %copy-done.1, bf16[512,512]{1,0:T(8,128)(2,1)} %copy-done.2, bf16[512,512]{1,0:T(8,128)(2,1)} %copy-done.2, bf16[512,512]{1,0:T(8,128)(2,1)} %shard_map.55.ca.cb.cur_ref, ...), custom_call_target="tpu_custom_call" | custom-call | tf_op jit(solution)/shard_map/pallas_call | solution.py:137
Async XLA Ops:
  0.0 5.0 %collective-permute-start = (bf16[3,3,256,512]{3,2,1,0:T(8,128)(2,1)}, bf16[3,3,256,512]{3,2,1,0:T(8,128)(2,1)S(1)}, u32[]{:S(2)}, u32[]{:S(2)}) collective-permute-start(bf16[3,3,256,512]{3,2,1,0:T(8,128)(2,1)} %param.6), channel_id=1, source_target_pairs={{0,1},{1,0},{2,3},{3,2},{4,5},{5,4},{6,7},{7,6},{8,9},{9,8},{10,11... | collective-permute-start | bytes 7077896 | tf_op jit(solution)/shard_map/ppermute | solution.py:16
  0.7 17.7 %collective-permute-start.3 = (bf16[3,256,512]{2,1,0:T(8,128)(2,1)}, bf16[3,256,512]{2,1,0:T(8,128)(2,1)S(1)}, u32[]{:S(2)}, u32[]{:S(2)}) collective-permute-start(bf16[3,256,512]{2,1,0:T(8,128)(2,1)} %param.9), channel_id=1, source_target_pairs={{0,1},{1,0},{2,3},{3,2},{4,5},{5,4},{6,7},{7,6},{8,9},{9,8},{10,11... | collective-permute-start | bytes 2359304 | tf_op jit(solution)/shard_map/ppermute | solution.py:16
  5.0 1.4 %copy-start = (bf16[3,3,256,512]{3,2,1,0:T(8,128)(2,1)}, bf16[3,3,256,512]{3,2,1,0:T(8,128)(2,1)S(1)}, u32[]{:S(2)}) copy-start(bf16[3,3,256,512]{3,2,1,0:T(8,128)(2,1)S(1)} %collective-permute-done) | copy-start | bytes 7077892
  14.2 16.3 %collective-permute-start.1 = (bf16[512,512]{1,0:T(8,128)(2,1)}, bf16[512,512]{1,0:T(8,128)(2,1)S(1)}, u32[]{:S(2)}, u32[]{:S(2)}) collective-permute-start(bf16[512,512]{1,0:T(8,128)(2,1)} %shard_map.55.ca.cb.cur_ref), channel_id=1, source_target_pairs={{1,2},{2,1},{3,4},{4,3},{5,6},{6,5},{7,8},{8,7},{9,10},{10,9},{11,... | collective-permute-start | bytes 1572872 | tf_op jit(solution)/shard_map/ppermute | solution.py:177
  17.6 12.9 %collective-permute-start.2 = (bf16[512,512]{1,0:T(8,128)(2,1)}, bf16[512,512]{1,0:T(8,128)(2,1)S(1)}, u32[]{:S(2)}, u32[]{:S(2)}) collective-permute-start(bf16[512,512]{1,0:T(8,128)(2,1)} %shard_map.55.ca.cb.cur_ref), channel_id=1, source_target_pairs={{0,1},{1,0},{2,3},{3,2},{4,5},{5,4},{6,7},{7,6},{8,9},{9,8},{10,11... | collective-permute-start | bytes 1572872 | tf_op jit(solution)/shard_map/ppermute | solution.py:16
  18.3 12.2 %copy-start.3 = (bf16[3,256,512]{2,1,0:T(8,128)(2,1)}, bf16[3,256,512]{2,1,0:T(8,128)(2,1)S(1)}, u32[]{:S(2)}) copy-start(bf16[3,256,512]{2,1,0:T(8,128)(2,1)S(1)} %collective-permute-done.3) | copy-start | bytes 2359300
  30.6 0.8 %copy-start.1 = (bf16[512,512]{1,0:T(8,128)(2,1)}, bf16[512,512]{1,0:T(8,128)(2,1)S(1)}, u32[]{:S(2)}) copy-start(bf16[512,512]{1,0:T(8,128)(2,1)S(1)} %collective-permute-done.1.ea.eb) | copy-start | bytes 1572868
  30.6 1.0 %copy-start.2 = (bf16[512,512]{1,0:T(8,128)(2,1)}, bf16[512,512]{1,0:T(8,128)(2,1)S(1)}, u32[]{:S(2)}) copy-start(bf16[512,512]{1,0:T(8,128)(2,1)S(1)} %collective-permute-done.2.pa.pb) | copy-start | bytes 1572868

commit v6 on v5

--- a/solution.py
+++ b/solution.py
@@ -28,15 +28,16 @@
     return row
 
 
-def conv_norm_kernel(side_ref, xa_ref, xb_ref, wa_ref, wb_ref, gain_ref, shift_ref, o_ref,
+def conv_norm_kernel(side_ref, lo_ref, hi_ref, wa_ref, wb_ref, gain_ref, shift_ref, o_ref,
                      lhs_ref, *, width, group):
-    rows, half = xa_ref.shape
+    rows, half = lo_ref.shape
 
     @pl.when(pl.program_id(0) == 0)
     def _prepare():
         col = lax.broadcasted_iota(jnp.int32, (rows, half), 0) % width
         zeros = jnp.zeros((width, half), jnp.bfloat16)
-        for h, x_ref in enumerate((xa_ref, xb_ref)):
+        for h, x_ref in enumerate((lo_ref, hi_ref)):
+            slot = (h + side_ref[0]) % 2
             xf = x_ref[...].astype(jnp.float32)
             left = jnp.where(col == 0, 0.0, pltpu.roll(xf, 1, 0)).astype(jnp.bfloat16)
             right = jnp.where(col == width - 1, 0.0, pltpu.roll(xf, rows - 1, 0)).astype(jnp.bfloat16)
@@ -45,13 +46,13 @@
                     lo = (dy * 3 + dx) * half
                     cols = slice(lo, lo + half)
                     if dy == 0:
-                        lhs_ref[h, :width, cols] = zeros
-                        lhs_ref[h, width:, cols] = v[: rows - width]
+                        lhs_ref[slot, :width, cols] = zeros
+                        lhs_ref[slot, width:, cols] = v[: rows - width]
                     elif dy == 1:
-                        lhs_ref[h, :, cols] = v
+                        lhs_ref[slot, :, cols] = v
                     else:
-                        lhs_ref[h, : rows - width, cols] = v[width:]
-                        lhs_ref[h, rows - width :, cols] = zeros
+                        lhs_ref[slot, : rows - width, cols] = v[width:]
+                        lhs_ref[slot, rows - width :, cols] = zeros
 
     acc = jnp.dot(lhs_ref[0], wa_ref[...], preferred_element_type=jnp.float32) + jnp.dot(
         lhs_ref[1], wb_ref[...], preferred_element_type=jnp.float32
@@ -66,9 +67,10 @@
     o_ref[...] = (v / (1.0 + jnp.exp(-v))).astype(o_ref.dtype)
 
 
-def conv_norm(frame, w_mine, w_other, gain, shift, side, width, split=2):
-    rows, channels = frame.shape
+def conv_norm(lo, hi, w_mine, w_other, gain, shift, side, width, split=2):
+    rows = lo.shape[0]
     half = w_mine.shape[2]
+    hi_block = 1 if hi.shape[1] > half else 0
     outputs = w_mine.shape[3]
     group = outputs // GROUPS
     block = outputs // split
@@ -82,8 +84,8 @@
             num_scalar_prefetch=1,
             grid=(split,),
             in_specs=[
-                pl.BlockSpec((rows, half), lambda n, s: (0, s[0])),
-                pl.BlockSpec((rows, half), lambda n, s: (0, 1 - s[0])),
+                pl.BlockSpec((rows, half), lambda n, s: (0, 0)),
+                pl.BlockSpec((rows, half), lambda n, s: (0, hi_block)),
                 weight_block,
                 weight_block,
                 row_block,
@@ -93,7 +95,7 @@
             scratch_shapes=[pltpu.VMEM((2, rows, 9 * half), jnp.bfloat16)],
         ),
         compiler_params=pltpu.CompilerParams(dimension_semantics=("arbitrary",)),
-    )(side, frame, frame, w_mine.reshape(9 * half, outputs), w_other.reshape(9 * half, outputs),
+    )(side, lo, hi, w_mine.reshape(9 * half, outputs), w_other.reshape(9 * half, outputs),
       gain, shift)
 
 
@@ -167,15 +169,18 @@
         if 0 <= target < blocks and min(j, target) % CLIP != CLIP - 1:
             route.append((j, target))
     frame = video.reshape(pixels, channels)
+    half = channels // 2
+    edge_lo = lax.ppermute(frame[:, :half], ("video", "fsdp"), route)
+    edge_hi = lax.ppermute(frame[:, half:], ("video", "fsdp"), route)
     other_spatial = swap_pair(w_spatial)
     other_time = swap_pair(w_time)
 
     gain = norm_gain.reshape(1, channels)
     shift = norm_shift.reshape(1, channels)
     sides = side.reshape(1).astype(jnp.int32)
-    hidden = conv_norm(frame, w_spatial, other_spatial, gain, shift, sides, width)
-    edge = lax.ppermute(hidden, ("video", "fsdp"), route)
+    hidden = conv_norm(frame, frame, w_spatial, other_spatial, gain, shift, sides, width)
     partner = swap_pair(hidden)
+    edge = conv_norm(edge_lo, edge_hi, w_spatial, other_spatial, gain, shift, sides, width)
 
     keep_prev = (position % CLIP != 0).astype(jnp.int32)
     keep_next = (position % CLIP != CLIP - 1).astype(jnp.int32)

time: 36.3 us -> 46.7 us (1.29)
  Pallas kernels: 12.3 us -> 21 us
  starting transfers between devices: 4.13 us -> 6.62 us
  waiting for transfers between devices: 16.6 us -> 15.4 us
  local copies, waits for them, and re-layouts: 2.4 us -> 2.93 us
    pallas_call x1 -> x2, Pallas kernels: 7.78 us -> 16.4 us  [conv_norm(): pl.pallas_call(kernel, out_shape=jax.ShapeDtypeStruct((rows, outputs), jn...]
    ppermute x1 -> x2, waiting for transfers between devices: 12.2 us -> 9.87 us  [the longest x1 7.06 us: body(): edge_lo = lax.ppermute(frame[:, :half], ('video', 'fsdp'), route)]
    ppermute x1 -> x2, starting transfers between devices: 3.37 us -> 5.56 us  [the longest x1 3.14 us: body(): edge_lo = lax.ppermute(frame[:, :half], ('video', 'fsdp'), route)]
    ppermute x3, waiting for transfers between devices: 4.37 us -> 5.5 us  [swap_pair(): return lax.ppermute(block, 'fsdp', [(0, 1), (1, 0)])]
    unnamed x8 -> x10, local copies, waits for them, and re-layouts: 2.4 us -> 2.9 us
  transfers between devices with their start and end apart: 4 -> 5, of which waited for: 2 -> 3; matrix products, arithmetic and copies ran while one was open for 2% -> 1% of each run, Pallas kernels for 22% -> 35%
where the time goes in v6:
time: 46.7 us; the launch traced here: 46.6 us
  Pallas kernels  21 us (45%)
  waiting for transfers between devices  15.4 us (33%)
  starting transfers between devices  6.62 us (14%)
  local copies, waits for them, and re-layouts  2.93 us (6%)
  other arithmetic  0.64 us (1%)
    pallas_call x2, Pallas kernels, conv_norm(): pl.pallas_call(kernel, out_shape=jax.ShapeDtypeStruct((rows, outputs), jn...  16.4 us
    ppermute x1, waiting for transfers between devices, body(): edge_lo = lax.ppermute(frame[:, :half], ('video', 'fsdp'), route)  7.06 us
    ppermute x3, waiting for transfers between devices, swap_pair(): return lax.ppermute(block, 'fsdp', [(0, 1), (1, 0)])  5.5 us
    pallas_call x1, Pallas kernels, temporal(): pl.pallas_call(temporal_kernel, out_shape=jax.ShapeDtypeStruct((rows, out...  4.56 us
    ppermute x1, starting transfers between devices, body(): edge_lo = lax.ppermute(frame[:, :half], ('video', 'fsdp'), route)  3.14 us
    unnamed x10, local copies, waits for them, and re-layouts  2.9 us
    ppermute x1, waiting for transfers between devices, body(): edge_hi = lax.ppermute(frame[:, half:], ('video', 'fsdp'), route)  2.81 us
    ppermute x1, starting transfers between devices, body(): edge_hi = lax.ppermute(frame[:, half:], ('video', 'fsdp'), route)  2.42 us
  transfers between devices with their start and end apart: 5, of which 3 were waited for; matrix products, arithmetic and copies ran while one was open for 1% of the time, Pallas kernels for 35%

profile of v6, /device:TPU:17, one launch (start us, length us, event | category | flops | bytes accessed | tf_op | source)
XLA Modules:
  0.0 46.6 jit_solution(8107207309353525176)
XLA Ops:
  0.0 0.7 %collective-permute-start.2 = (bf16[3,3,256,512]{3,2,1,0:T(8,128)(2,1)}, bf16[3,3,256,512]{3,2,1,0:T(8,128)(2,1)S(1)}, u32[]{:S(2)}, u32[]{:S(2)}) collective-permute-start(bf16[3,3,256,512]{3,2,1,0:T(8,128)(2,1)} %param.6), channel_id=1, source_target_pairs={{0,1},{1,0},{2,3},{3,2},{4,5},{5,4},{6,7},{7,6},{8,9},{9,8},{10,11... | collective-permute-start | bytes 7077896 | tf_op jit(solution)/shard_map/ppermute | solution.py:16
  0.7 0.0 collective-permute-start.4
  0.7 5.5 %collective-permute-done.2 = bf16[3,3,256,512]{3,2,1,0:T(8,128)(2,1)S(1)} collective-permute-done((bf16[3,3,256,512]{3,2,1,0:T(8,128)(2,1)}, bf16[3,3,256,512]{3,2,1,0:T(8,128)(2,1)S(1)}, u32[]{:S(2)}, u32[]{:S(2)}) %collective-permute-start.2) | collective-permute-done | bytes 2359328 | tf_op jit(solution)/shard_map/ppermute | solution.py:16
  6.2 0.0 copy-start
  6.2 1.4 %copy-done = bf16[3,3,256,512]{3,2,1,0:T(8,128)(2,1)} copy-done((bf16[3,3,256,512]{3,2,1,0:T(8,128)(2,1)}, bf16[3,3,256,512]{3,2,1,0:T(8,128)(2,1)S(1)}, u32[]{:S(2)}) %copy-start) | copy-done | bytes 2359320
  7.6 0.0 copy-start.1
  7.6 8.2 %shard_map.56.ca.cb.cur_ref = bf16[512,512]{1,0:T(8,128)(2,1)} custom-call(s32[1]{0:T(128)} %bitcast.side_ref, bf16[512,512]{1,0:T(8,128)(2,1)} %bitcast.15, bf16[512,512]{1,0:T(8,128)(2,1)} %bitcast.16, bf16[2304,512]{1,0:T(8,128)(2,1)} %bitcast.11, bf16[2304,512]{1,0:T(8,128)(2,1)} %bitcast.13, f32[1,512]{1,0:T(1,128)} %bitcast.19, f32[1,512]{1,0:T(1,128)} %bitcast.21), custom_call_target="tpu_custom_call" | custom-call | tf_op jit(solution)/shard_map/pallas_call | solution.py:80
  15.8 0.4 collective-permute-start.3
  16.2 0.0 copy-done.1
  16.2 3.1 %collective-permute-start = (bf16[512,256]{1,0:T(8,128)(2,1)S(1)}, bf16[512,256]{1,0:T(8,128)(2,1)S(1)}, u32[]{:S(2)}, u32[]{:S(2)}) collective-permute-start(bf16[512,256]{1,0:T(8,128)(2,1)S(1)} %get-tuple-element.6), channel_id=1, source_target_pairs={{1,2},{2,1},{3,4},{4,3},{5,6},{6,5},{7,8},{8,7},{9,10},{10,9},{11,... | collective-permute-start | bytes 786440 | tf_op jit(solution)/shard_map/ppermute | solution.py:173
  19.4 2.4 %collective-permute-start.1 = (bf16[512,256]{1,0:T(8,128)(2,1)S(1)}, bf16[512,256]{1,0:T(8,128)(2,1)S(1)}, u32[]{:S(2)}, u32[]{:S(2)}) collective-permute-start(bf16[512,256]{1,0:T(8,128)(2,1)S(1)} %get-tuple-element.5), channel_id=1, source_target_pairs={{1,2},{2,1},{3,4},{4,3},{5,6},{6,5},{7,8},{8,7},{9,10},{10,9},{11,... | collective-permute-start | bytes 786440 | tf_op jit(solution)/shard_map/ppermute | solution.py:174
  21.8 0.6 %pad_add_fusion.s_ref = s32[3]{0:T(128)} fusion(s32[1]{0:T(128)} %bitcast.2, s32[1]{0:T(128)} %bitcast.1, s32[1]{0:T(128)} %bitcast.side_ref), kind=kLoop, calls=%fused_computation | loop fusion | flops 6 | bytes 24 | tf_op jit(solution)/shard_map/stack | solution.py:189
  22.5 7.1 %collective-permute-done.lo_ref = bf16[512,256]{1,0:T(8,128)(2,1)S(1)} collective-permute-done((bf16[512,256]{1,0:T(8,128)(2,1)S(1)}, bf16[512,256]{1,0:T(8,128)(2,1)S(1)}, u32[]{:S(2)}, u32[]{:S(2)}) %collective-permute-start) | collective-permute-done | bytes 262176 | tf_op jit(solution)/shard_map/ppermute | solution.py:173
  29.5 0.0 copy-start.3
  29.5 2.8 %collective-permute-done.1.hi_ref = bf16[512,256]{1,0:T(8,128)(2,1)S(1)} collective-permute-done((bf16[512,256]{1,0:T(8,128)(2,1)S(1)}, bf16[512,256]{1,0:T(8,128)(2,1)S(1)}, u32[]{:S(2)}, u32[]{:S(2)}) %collective-permute-start.1) | collective-permute-done | bytes 262176 | tf_op jit(solution)/shard_map/ppermute | solution.py:174
  32.3 0.0 copy-done.3
  32.3 0.0 copy-start.4
  32.3 0.7 %copy-done.4 = bf16[512,256]{1,0:T(8,128)(2,1)} copy-done((bf16[512,256]{1,0:T(8,128)(2,1)}, bf16[512,256]{1,0:T(8,128)(2,1)S(1)}, u32[]{:S(2)}) %copy-start.4) | copy-done | bytes 262168
  33.0 8.2 %shard_map.55.ea.eb = bf16[512,512]{1,0:T(8,128)(2,1)} custom-call(s32[1]{0:T(128)} %bitcast.side_ref, bf16[512,256]{1,0:T(8,128)(2,1)} %copy-done.3, bf16[512,256]{1,0:T(8,128)(2,1)} %copy-done.4, bf16[2304,512]{1,0:T(8,128)(2,1)} %bitcast.12, bf16[2304,512]{1,0:T(8,128)(2,1)} %bitcast.14, f32[1,512]{1,0:T(1,128)} %bitcast.20, f32[1,512]{1,0:T(1,128)} %bitcast.22), custom_call_target="tpu_custom_call" | custom-call | tf_op jit(solution)/shard_map/pallas_call | solution.py:80
  41.2 0.0 collective-permute-done.4
  41.2 0.0 collective-permute-done.3.pa.pb
  41.2 0.0 copy-start.2
  41.2 0.8 %copy-done.2 = bf16[512,512]{1,0:T(8,128)(2,1)} copy-done((bf16[512,512]{1,0:T(8,128)(2,1)}, bf16[512,512]{1,0:T(8,128)(2,1)S(1)}, u32[]{:S(2)}) %copy-start.2) | copy-done | bytes 524312
  42.0 4.6 %shard_map.57 = bf16[512,512]{1,0:T(8,128)(2,1)} custom-call(s32[3]{0:T(128)} %pad_add_fusion.s_ref, bf16[512,512]{1,0:T(8,128)(2,1)} %shard_map.55.ea.eb, bf16[512,512]{1,0:T(8,128)(2,1)} %shard_map.55.ea.eb, bf16[512,512]{1,0:T(8,128)(2,1)} %copy-done.2, bf16[512,512]{1,0:T(8,128)(2,1)} %copy-done.2, bf16[512,512]{1,0:T(8,128)(2,1)} %shard_map.56.ca.cb.cur_ref, ...), custom_call_target="tpu_custom_call" | custom-call | tf_op jit(solution)/shard_map/pallas_call | solution.py:139
  (1 shorter events, 0.0 us)
Async XLA Ops:
  0.0 6.2 %collective-permute-start.2 = (bf16[3,3,256,512]{3,2,1,0:T(8,128)(2,1)}, bf16[3,3,256,512]{3,2,1,0:T(8,128)(2,1)S(1)}, u32[]{:S(2)}, u32[]{:S(2)}) collective-permute-start(bf16[3,3,256,512]{3,2,1,0:T(8,128)(2,1)} %param.6), channel_id=1, source_target_pairs={{0,1},{1,0},{2,3},{3,2},{4,5},{5,4},{6,7},{7,6},{8,9},{9,8},{10,11... | collective-permute-start | bytes 7077896 | tf_op jit(solution)/shard_map/ppermute | solution.py:16
  0.7 40.5 %collective-permute-start.4 = (bf16[3,256,512]{2,1,0:T(8,128)(2,1)}, bf16[3,256,512]{2,1,0:T(8,128)(2,1)}, u32[]{:S(2)}, u32[]{:S(2)}) collective-permute-start(bf16[3,256,512]{2,1,0:T(8,128)(2,1)} %param.9), channel_id=1, source_target_pairs={{0,1},{1,0},{2,3},{3,2},{4,5},{5,4},{6,7},{7,6},{8,9},{9,8},{10,11... | collective-permute-start | bytes 2359304 | tf_op jit(solution)/shard_map/ppermute | solution.py:16
  6.2 1.4 %copy-start = (bf16[3,3,256,512]{3,2,1,0:T(8,128)(2,1)}, bf16[3,3,256,512]{3,2,1,0:T(8,128)(2,1)S(1)}, u32[]{:S(2)}) copy-start(bf16[3,3,256,512]{3,2,1,0:T(8,128)(2,1)S(1)} %collective-permute-done.2) | copy-start | bytes 7077892
  7.6 8.6 %copy-start.1 = (bf16[1,32,16,512]{3,2,1,0:T(8,128)(2,1)S(1)}, bf16[1,32,16,512]{3,2,1,0:T(8,128)(2,1)}, u32[]{:S(2)}) copy-start(bf16[1,32,16,512]{3,2,1,0:T(8,128)(2,1)} %param.5) | copy-start | bytes 1572868
  15.8 25.4 %collective-permute-start.3 = (bf16[512,512]{1,0:T(8,128)(2,1)}, bf16[512,512]{1,0:T(8,128)(2,1)S(1)}, u32[]{:S(2)}, u32[]{:S(2)}) collective-permute-start(bf16[512,512]{1,0:T(8,128)(2,1)} %shard_map.56.ca.cb.cur_ref), channel_id=1, source_target_pairs={{0,1},{1,0},{2,3},{3,2},{4,5},{5,4},{6,7},{7,6},{8,9},{9,8},{10,11... | collective-permute-start | bytes 1572872 | tf_op jit(solution)/shard_map/ppermute | solution.py:16
  16.2 13.3 %collective-permute-start = (bf16[512,256]{1,0:T(8,128)(2,1)S(1)}, bf16[512,256]{1,0:T(8,128)(2,1)S(1)}, u32[]{:S(2)}, u32[]{:S(2)}) collective-permute-start(bf16[512,256]{1,0:T(8,128)(2,1)S(1)} %get-tuple-element.6), channel_id=1, source_target_pairs={{1,2},{2,1},{3,4},{4,3},{5,6},{6,5},{7,8},{8,7},{9,10},{10,9},{11,... | collective-permute-start | bytes 786440 | tf_op jit(solution)/shard_map/ppermute | solution.py:173
  19.4 13.0 %collective-permute-start.1 = (bf16[512,256]{1,0:T(8,128)(2,1)S(1)}, bf16[512,256]{1,0:T(8,128)(2,1)S(1)}, u32[]{:S(2)}, u32[]{:S(2)}) collective-permute-start(bf16[512,256]{1,0:T(8,128)(2,1)S(1)} %get-tuple-element.5), channel_id=1, source_target_pairs={{1,2},{2,1},{3,4},{4,3},{5,6},{6,5},{7,8},{8,7},{9,10},{10,9},{11,... | collective-permute-start | bytes 786440 | tf_op jit(solution)/shard_map/ppermute | solution.py:174
  29.5 2.8 %copy-start.3 = (bf16[512,256]{1,0:T(8,128)(2,1)}, bf16[512,256]{1,0:T(8,128)(2,1)S(1)}, u32[]{:S(2)}) copy-start(bf16[512,256]{1,0:T(8,128)(2,1)S(1)} %collective-permute-done.lo_ref) | copy-start | bytes 786436
  32.3 0.7 %copy-start.4 = (bf16[512,256]{1,0:T(8,128)(2,1)}, bf16[512,256]{1,0:T(8,128)(2,1)S(1)}, u32[]{:S(2)}) copy-start(bf16[512,256]{1,0:T(8,128)(2,1)S(1)} %collective-permute-done.1.hi_ref) | copy-start | bytes 786436
  41.2 0.8 %copy-start.2 = (bf16[512,512]{1,0:T(8,128)(2,1)}, bf16[512,512]{1,0:T(8,128)(2,1)S(1)}, u32[]{:S(2)}) copy-start(bf16[512,512]{1,0:T(8,128)(2,1)S(1)} %collective-permute-done.3.pa.pb) | copy-start | bytes 1572868

commit v7 on v3

--- a/solution.py
+++ b/solution.py
@@ -66,7 +66,7 @@
     o_ref[...] = (v / (1.0 + jnp.exp(-v))).astype(o_ref.dtype)
 
 
-def conv_norm(frame, w_mine, w_other, gain, shift, side, width, split=2):
+def conv_norm(frame, w_mine, w_other, gain, shift, side, width, split=1):
     rows, channels = frame.shape
     half = w_mine.shape[2]
     outputs = w_mine.shape[3]

time: 31.2 us -> 30.5 us (0.978)
  Pallas kernels: 20.2 us -> 18.9 us
  waiting for transfers between devices: 2.63 us -> 3.28 us
    pallas_call x2, Pallas kernels: 15.6 us -> 14.3 us  [conv_norm(): pl.pallas_call(kernel, out_shape=jax.ShapeDtypeStruct((rows, outputs), jn...]
    ppermute x1, waiting for transfers between devices: 0.65 us -> 1.29 us  [body(): edge_video = lax.ppermute(frame, ('video', 'fsdp'), route)]
  transfers between devices with their start and end apart: 4 -> 4, of which waited for: 2 -> 2; matrix products, arithmetic and copies ran while one was open for 2% -> 2% of each run, Pallas kernels for 50% -> 47%
where the time goes in v7:
time: 30.5 us; the launch traced here: 30.3 us
  Pallas kernels  18.9 us (62%)
  starting transfers between devices  4.55 us (15%)
  waiting for transfers between devices  3.28 us (11%)
  local copies, waits for them, and re-layouts  2.99 us (10%)
  other arithmetic  0.59 us (2%)
    pallas_call x2, Pallas kernels, conv_norm(): pl.pallas_call(kernel, out_shape=jax.ShapeDtypeStruct((rows, outputs), jn...  14.3 us
    pallas_call x1, Pallas kernels, temporal(): pl.pallas_call(temporal_kernel, out_shape=jax.ShapeDtypeStruct((rows, out...  4.56 us
    ppermute x1, starting transfers between devices, body(): edge_video = lax.ppermute(frame, ('video', 'fsdp'), route)  3.5 us
    unnamed x6, local copies, waits for them, and re-layouts  2.99 us
    ppermute x3, waiting for transfers between devices, swap_pair(): return lax.ppermute(block, 'fsdp', [(0, 1), (1, 0)])  1.99 us
    ppermute x1, waiting for transfers between devices, body(): edge_video = lax.ppermute(frame, ('video', 'fsdp'), route)  1.29 us
    ppermute x3, starting transfers between devices, swap_pair(): return lax.ppermute(block, 'fsdp', [(0, 1), (1, 0)])  1.05 us
  transfers between devices with their start and end apart: 4, of which 2 were waited for; matrix products, arithmetic and copies ran while one was open for 2% of the time, Pallas kernels for 47%

profile of v7, /device:TPU:17, one launch (start us, length us, event | category | flops | bytes accessed | tf_op | source)
XLA Modules:
  0.0 30.3 jit_solution(17425718914664449404)
XLA Ops:
  0.0 0.7 %collective-permute-start.1 = (bf16[3,3,256,512]{3,2,1,0:T(8,128)(2,1)}, bf16[3,3,256,512]{3,2,1,0:T(8,128)(2,1)S(1)}, u32[]{:S(2)}, u32[]{:S(2)}) collective-permute-start(bf16[3,3,256,512]{3,2,1,0:T(8,128)(2,1)} %param.6), channel_id=1, source_target_pairs={{0,1},{1,0},{2,3},{3,2},{4,5},{5,4},{6,7},{7,6},{8,9},{9,8},{10,11... | collective-permute-start | bytes 7077896 | tf_op jit(solution)/shard_map/ppermute | solution.py:16
  0.7 0.0 collective-permute-start.3
  0.7 3.5 %collective-permute-start = (bf16[512,512]{1,0:T(8,128)(2,1)}, bf16[512,512]{1,0:T(8,128)(2,1)S(1)}, u32[]{:S(2)}, u32[]{:S(2)}) collective-permute-start(bf16[512,512]{1,0:T(8,128)(2,1)} %bitcast.15), channel_id=1, source_target_pairs={{1,2},{2,1},{3,4},{4,3},{5,6},{6,5},{7,8},{8,7},{9,10},{10,9},{11,... | collective-permute-start | bytes 1572872 | tf_op jit(solution)/shard_map/ppermute | solution.py:170
  4.2 2.0 %collective-permute-done.1 = bf16[3,3,256,512]{3,2,1,0:T(8,128)(2,1)S(1)} collective-permute-done((bf16[3,3,256,512]{3,2,1,0:T(8,128)(2,1)}, bf16[3,3,256,512]{3,2,1,0:T(8,128)(2,1)S(1)}, u32[]{:S(2)}, u32[]{:S(2)}) %collective-permute-start.1) | collective-permute-done | bytes 2359328 | tf_op jit(solution)/shard_map/ppermute | solution.py:16
  6.2 0.0 copy-start
  6.2 1.4 %copy-done = bf16[3,3,256,512]{3,2,1,0:T(8,128)(2,1)} copy-done((bf16[3,3,256,512]{3,2,1,0:T(8,128)(2,1)}, bf16[3,3,256,512]{3,2,1,0:T(8,128)(2,1)S(1)}, u32[]{:S(2)}) %copy-start) | copy-done | bytes 2359320
  7.6 7.2 %shard_map.56.ca.cb.cur_ref = bf16[512,512]{1,0:T(8,128)(2,1)} custom-call(s32[1]{0:T(128)} %bitcast.side_ref, bf16[512,512]{1,0:T(8,128)(2,1)} %bitcast.16, bf16[512,512]{1,0:T(8,128)(2,1)} %bitcast.17, bf16[2304,512]{1,0:T(8,128)(2,1)} %bitcast.11, bf16[2304,512]{1,0:T(8,128)(2,1)} %bitcast.13, f32[1,512]{1,0:T(1,128)} %bitcast.19, f32[1,512]{1,0:T(1,128)} %bitcast.21), custom_call_target="tpu_custom_call" | custom-call | tf_op jit(solution)/shard_map/pallas_call | solution.py:78
  14.7 0.4 %collective-permute-start.2 = (bf16[512,512]{1,0:T(8,128)(2,1)}, bf16[512,512]{1,0:T(8,128)(2,1)S(1)}, u32[]{:S(2)}, u32[]{:S(2)}) collective-permute-start(bf16[512,512]{1,0:T(8,128)(2,1)} %shard_map.56.ca.cb.cur_ref), channel_id=1, source_target_pairs={{0,1},{1,0},{2,3},{3,2},{4,5},{5,4},{6,7},{7,6},{8,9},{9,8},{10,11... | collective-permute-start | bytes 1572872 | tf_op jit(solution)/shard_map/ppermute | solution.py:16
  15.1 0.6 %pad_add_fusion.s_ref = s32[3]{0:T(128)} fusion(s32[1]{0:T(128)} %bitcast.2, s32[1]{0:T(128)} %bitcast.1, s32[1]{0:T(128)} %bitcast.side_ref), kind=kLoop, calls=%fused_computation | loop fusion | flops 6 | bytes 24 | tf_op jit(solution)/shard_map/stack | solution.py:185
  15.7 1.3 %collective-permute-done.xa_ref.xb_ref = bf16[512,512]{1,0:T(8,128)(2,1)S(1)} collective-permute-done((bf16[512,512]{1,0:T(8,128)(2,1)}, bf16[512,512]{1,0:T(8,128)(2,1)S(1)}, u32[]{:S(2)}, u32[]{:S(2)}) %collective-permute-start) | collective-permute-done | bytes 524320 | tf_op jit(solution)/shard_map/ppermute | solution.py:170
  17.0 0.0 copy-start.1
  17.0 0.8 %copy-done.1 = bf16[512,512]{1,0:T(8,128)(2,1)} copy-done((bf16[512,512]{1,0:T(8,128)(2,1)}, bf16[512,512]{1,0:T(8,128)(2,1)S(1)}, u32[]{:S(2)}) %copy-start.1) | copy-done | bytes 524312
  17.8 7.2 %shard_map.55.ea.eb = bf16[512,512]{1,0:T(8,128)(2,1)} custom-call(s32[1]{0:T(128)} %bitcast.side_ref, bf16[512,512]{1,0:T(8,128)(2,1)} %copy-done.1, bf16[512,512]{1,0:T(8,128)(2,1)} %copy-done.1, bf16[2304,512]{1,0:T(8,128)(2,1)} %bitcast.12, bf16[2304,512]{1,0:T(8,128)(2,1)} %bitcast.14, f32[1,512]{1,0:T(1,128)} %bitcast.20, f32[1,512]{1,0:T(1,128)} %bitcast.22), custom_call_target="tpu_custom_call" | custom-call | tf_op jit(solution)/shard_map/pallas_call | solution.py:78
  24.9 0.0 collective-permute-done.3
  25.0 0.0 collective-permute-done.2.pa.pb
  25.0 0.0 copy-start.2
  25.0 0.8 %copy-done.2 = bf16[512,512]{1,0:T(8,128)(2,1)} copy-done((bf16[512,512]{1,0:T(8,128)(2,1)}, bf16[512,512]{1,0:T(8,128)(2,1)S(1)}, u32[]{:S(2)}) %copy-start.2) | copy-done | bytes 524312
  25.8 4.6 %shard_map.57 = bf16[512,512]{1,0:T(8,128)(2,1)} custom-call(s32[3]{0:T(128)} %pad_add_fusion.s_ref, bf16[512,512]{1,0:T(8,128)(2,1)} %shard_map.55.ea.eb, bf16[512,512]{1,0:T(8,128)(2,1)} %shard_map.55.ea.eb, bf16[512,512]{1,0:T(8,128)(2,1)} %copy-done.2, bf16[512,512]{1,0:T(8,128)(2,1)} %copy-done.2, bf16[512,512]{1,0:T(8,128)(2,1)} %shard_map.56.ca.cb.cur_ref, ...), custom_call_target="tpu_custom_call" | custom-call | tf_op jit(solution)/shard_map/pallas_call | solution.py:137
Async XLA Ops:
  0.0 6.2 %collective-permute-start.1 = (bf16[3,3,256,512]{3,2,1,0:T(8,128)(2,1)}, bf16[3,3,256,512]{3,2,1,0:T(8,128)(2,1)S(1)}, u32[]{:S(2)}, u32[]{:S(2)}) collective-permute-start(bf16[3,3,256,512]{3,2,1,0:T(8,128)(2,1)} %param.6), channel_id=1, source_target_pairs={{0,1},{1,0},{2,3},{3,2},{4,5},{5,4},{6,7},{7,6},{8,9},{9,8},{10,11... | collective-permute-start | bytes 7077896 | tf_op jit(solution)/shard_map/ppermute | solution.py:16
  0.7 24.3 %collective-permute-start.3 = (bf16[3,256,512]{2,1,0:T(8,128)(2,1)}, bf16[3,256,512]{2,1,0:T(8,128)(2,1)}, u32[]{:S(2)}, u32[]{:S(2)}) collective-permute-start(bf16[3,256,512]{2,1,0:T(8,128)(2,1)} %param.9), channel_id=1, source_target_pairs={{0,1},{1,0},{2,3},{3,2},{4,5},{5,4},{6,7},{7,6},{8,9},{9,8},{10,11... | collective-permute-start | bytes 2359304 | tf_op jit(solution)/shard_map/ppermute | solution.py:16
  0.7 16.3 %collective-permute-start = (bf16[512,512]{1,0:T(8,128)(2,1)}, bf16[512,512]{1,0:T(8,128)(2,1)S(1)}, u32[]{:S(2)}, u32[]{:S(2)}) collective-permute-start(bf16[512,512]{1,0:T(8,128)(2,1)} %bitcast.15), channel_id=1, source_target_pairs={{1,2},{2,1},{3,4},{4,3},{5,6},{6,5},{7,8},{8,7},{9,10},{10,9},{11,... | collective-permute-start | bytes 1572872 | tf_op jit(solution)/shard_map/ppermute | solution.py:170
  6.2 1.4 %copy-start = (bf16[3,3,256,512]{3,2,1,0:T(8,128)(2,1)}, bf16[3,3,256,512]{3,2,1,0:T(8,128)(2,1)S(1)}, u32[]{:S(2)}) copy-start(bf16[3,3,256,512]{3,2,1,0:T(8,128)(2,1)S(1)} %collective-permute-done.1) | copy-start | bytes 7077892
  14.7 10.2 %collective-permute-start.2 = (bf16[512,512]{1,0:T(8,128)(2,1)}, bf16[512,512]{1,0:T(8,128)(2,1)S(1)}, u32[]{:S(2)}, u32[]{:S(2)}) collective-permute-start(bf16[512,512]{1,0:T(8,128)(2,1)} %shard_map.56.ca.cb.cur_ref), channel_id=1, source_target_pairs={{0,1},{1,0},{2,3},{3,2},{4,5},{5,4},{6,7},{7,6},{8,9},{9,8},{10,11... | collective-permute-start | bytes 1572872 | tf_op jit(solution)/shard_map/ppermute | solution.py:16
  17.0 0.8 %copy-start.1 = (bf16[512,512]{1,0:T(8,128)(2,1)}, bf16[512,512]{1,0:T(8,128)(2,1)S(1)}, u32[]{:S(2)}) copy-start(bf16[512,512]{1,0:T(8,128)(2,1)S(1)} %collective-permute-done.xa_ref.xb_ref) | copy-start | bytes 1572868
  25.0 0.8 %copy-start.2 = (bf16[512,512]{1,0:T(8,128)(2,1)}, bf16[512,512]{1,0:T(8,128)(2,1)S(1)}, u32[]{:S(2)}) copy-start(bf16[512,512]{1,0:T(8,128)(2,1)S(1)} %collective-permute-done.2.pa.pb) | copy-start | bytes 1572868

commit v8 on v7

--- a/solution.py
+++ b/solution.py
@@ -97,60 +97,92 @@
       gain, shift)
 
 
-def temporal_kernel(s_ref, ea, eb, pa, pb, ca, cb, cur_ref, wm_ref, wo_ref, o_ref, lhs_ref):
-    half = ea.shape[1]
-
-    @pl.when(pl.program_id(0) == 0)
-    def _prepare():
-        keep_edge = s_ref[1] != 0
-        keep_partner = s_ref[2] != 0
-        for h, (e, p, c) in enumerate(((ea, pa, ca), (eb, pb, cb))):
-            edge = jnp.where(keep_edge, e[...], jnp.zeros_like(e[...]))
-            partner = jnp.where(keep_partner, p[...], jnp.zeros_like(p[...]))
-            lhs_ref[h, :, half : 2 * half] = c[...]
-
-            @pl.when(s_ref[0] == 0)
-            def _():
-                lhs_ref[h, :, :half] = edge
-                lhs_ref[h, :, 2 * half :] = partner
-
-            @pl.when(s_ref[0] != 0)
-            def _():
-                lhs_ref[h, :, :half] = partner
-                lhs_ref[h, :, 2 * half :] = edge
+def edge_temporal_kernel(s_ref, xa_ref, xb_ref, wa_ref, wb_ref, gain_ref, shift_ref,
+                         cur_hbm, partner_hbm, wtm_hbm, wto_hbm, o_ref,
+                         lhs_ref, edge_v, cur_v, partner_v, wtm_v, wto_v, tl_ref, sem,
+                         *, width, group):
+    copies = [
+        pltpu.make_async_copy(src, dst, sem.at[i])
+        for i, (src, dst) in enumerate(
+            ((cur_hbm, cur_v), (partner_hbm, partner_v), (wtm_hbm, wtm_v), (wto_hbm, wto_v))
+        )
+    ]
+    for copy in copies:
+        copy.start()
+    conv_norm_kernel(s_ref, xa_ref, xb_ref, wa_ref, wb_ref, gain_ref, shift_ref, edge_v,
+                     lhs_ref, width=width, group=group)
+    for copy in copies:
+        copy.wait()
+
+    rows, half = xa_ref.shape
+    keep_edge = s_ref[1] != 0
+    keep_partner = s_ref[2] != 0
+    for side in range(2):
+        @pl.when(s_ref[0] == side)
+        def _fill():
+            mine = slice(side * half, (side + 1) * half)
+            other = slice((1 - side) * half, (2 - side) * half)
+            for h, cols in enumerate((mine, other)):
+                e = edge_v[:, cols]
+                p = partner_v[:, cols]
+                e = jnp.where(keep_edge, e, jnp.zeros_like(e))
+                p = jnp.where(keep_partner, p, jnp.zeros_like(p))
+                before, after = (e, p) if side == 0 else (p, e)
+                tl_ref[h, :, :half] = before
+                tl_ref[h, :, half : 2 * half] = cur_v[:, cols]
+                tl_ref[h, :, 2 * half :] = after
 
     f32 = jnp.float32
-    total = jnp.dot(lhs_ref[0], wm_ref[...], preferred_element_type=f32) + jnp.dot(
-        lhs_ref[1], wo_ref[...], preferred_element_type=f32
-    )
-    o_ref[...] = (cur_ref[...].astype(f32) + total).astype(o_ref.dtype)
-
-
-def temporal(edge, partner, cur, w_mine, w_other, scalars, split=2):
-    rows, channels = cur.shape
-    half = w_mine.shape[1]
-    outputs = w_mine.shape[2]
-    block = outputs // split
-    mine = pl.BlockSpec((rows, half), lambda n, s: (0, s[0]))
-    other = pl.BlockSpec((rows, half), lambda n, s: (0, 1 - s[0]))
-    weight_block = pl.BlockSpec((3 * half, block), lambda n, s: (0, n))
+    total = jnp.dot(tl_ref[0], wtm_v[...], preferred_element_type=f32) + jnp.dot(
+        tl_ref[1], wto_v[...], preferred_element_type=f32
+    )
+    o_ref[...] = (cur_v[...].astype(f32) + total).astype(o_ref.dtype)
+
+
+def edge_temporal(frame, w_mine, w_other, gain, shift, cur, partner, t_mine, t_other, scalars,
+                  width):
+    rows, channels = frame.shape
+    half = w_mine.shape[2]
+    outputs = w_mine.shape[3]
+    group = outputs // GROUPS
+    kernel = functools.partial(edge_temporal_kernel, width=width, group=group)
+    weight_block = pl.BlockSpec((9 * half, outputs), lambda n, s: (0, 0))
+    row_block = pl.BlockSpec((1, outputs), lambda n, s: (0, 0))
+    anywhere = pl.BlockSpec(memory_space=pl.ANY)
     return pl.pallas_call(
-        temporal_kernel,
+        kernel,
         out_shape=jax.ShapeDtypeStruct((rows, outputs), jnp.bfloat16),
         grid_spec=pltpu.PrefetchScalarGridSpec(
             num_scalar_prefetch=1,
-            grid=(split,),
+            grid=(1,),
             in_specs=[
-                mine, other, mine, other, mine, other,
-                pl.BlockSpec((rows, block), lambda n, s: (0, n)),
-                weight_block, weight_block,
+                pl.BlockSpec((rows, half), lambda n, s: (0, s[0])),
+                pl.BlockSpec((rows, half), lambda n, s: (0, 1 - s[0])),
+                weight_block,
+                weight_block,
+                row_block,
+                row_block,
+                anywhere,
+                anywhere,
+                anywhere,
+                anywhere,
             ],
-            out_specs=pl.BlockSpec((rows, block), lambda n, s: (0, n)),
-            scratch_shapes=[pltpu.VMEM((2, rows, 3 * half), jnp.bfloat16)],
+            out_specs=pl.BlockSpec((rows, outputs), lambda n, s: (0, 0)),
+            scratch_shapes=[
+                pltpu.VMEM((2, rows, 9 * half), jnp.bfloat16),
+                pltpu.VMEM((rows, outputs), jnp.bfloat16),
+                pltpu.VMEM((rows, channels), jnp.bfloat16),
+                pltpu.VMEM((rows, channels), jnp.bfloat16),
+                pltpu.VMEM((3 * half, outputs), jnp.bfloat16),
+                pltpu.VMEM((3 * half, outputs), jnp.bfloat16),
+                pltpu.VMEM((2, rows, 3 * half), jnp.bfloat16),
+                pltpu.SemaphoreType.DMA((4,)),
+            ],
         ),
         compiler_params=pltpu.CompilerParams(dimension_semantics=("arbitrary",)),
-    )(scalars, edge, edge, partner, partner, cur, cur, cur,
-      w_mine.reshape(3 * half, outputs), w_other.reshape(3 * half, outputs))
+    )(scalars, frame, frame, w_mine.reshape(9 * half, outputs), w_other.reshape(9 * half, outputs),
+      gain, shift, cur, partner, t_mine.reshape(3 * half, outputs),
+      t_other.reshape(3 * half, outputs))
 
 
 def body(video, w_spatial, norm_gain, norm_shift, w_time):
@@ -176,14 +208,13 @@
     sides = side.reshape(1).astype(jnp.int32)
     hidden = conv_norm(frame, w_spatial, other_spatial, gain, shift, sides, width)
     partner = swap_pair(hidden)
-    edge = conv_norm(edge_video, w_spatial, other_spatial, gain, shift, sides, width)
-
     keep_prev = (position % CLIP != 0).astype(jnp.int32)
     keep_next = (position % CLIP != CLIP - 1).astype(jnp.int32)
     keep_edge = jnp.where(side == 0, keep_prev, keep_next)
     keep_partner = jnp.where(side == 0, keep_next, keep_prev)
     scalars = jnp.stack([side.astype(jnp.int32), keep_edge, keep_partner])
-    result = temporal(edge, partner, hidden, w_time, other_time, scalars)
+    result = edge_temporal(edge_video, w_spatial, other_spatial, gain, shift, hidden, partner,
+                           w_time, other_time, scalars, width)
     return result.reshape(count, height, width, channels)
 
 

time: 30.5 us -> 27.1 us (0.89)
  Pallas kernels: 18.9 us -> 16.1 us
  local copies, waits for them, and re-layouts: 2.99 us -> 2.37 us
    pallas_call x2 -> x1, Pallas kernels: 14.3 us -> 7.16 us  [conv_norm(): pl.pallas_call(kernel, out_shape=jax.ShapeDtypeStruct((rows, outputs), jn...]
    pallas_call x1, Pallas kernels: 4.56 us -> 8.89 us  [edge_temporal(): pl.pallas_call(kernel, out_shape=jax.ShapeDtypeStruct((rows, outputs), jn...]
    unnamed x6, local copies, waits for them, and re-layouts: 2.99 us -> 2.37 us
  transfers between devices with their start and end apart: 4 -> 4, of which waited for: 2 -> 2; matrix products, arithmetic and copies ran while one was open for 2% -> 2% of each run, Pallas kernels for 47% -> 27%
where the time goes in v8:
time: 27.1 us; the launch traced here: 26.9 us
  Pallas kernels  16.1 us (59%)
  starting transfers between devices  4.55 us (17%)
  waiting for transfers between devices  3.22 us (12%)
  local copies, waits for them, and re-layouts  2.37 us (9%)
  other arithmetic  0.65 us (2%)
    pallas_call x1, Pallas kernels, edge_temporal(): pl.pallas_call(kernel, out_shape=jax.ShapeDtypeStruct((rows, outputs), jn...  8.89 us
    pallas_call x1, Pallas kernels, conv_norm(): pl.pallas_call(kernel, out_shape=jax.ShapeDtypeStruct((rows, outputs), jn...  7.16 us
    ppermute x1, starting transfers between devices, body(): edge_video = lax.ppermute(frame, ('video', 'fsdp'), route)  3.5 us
    unnamed x6, local copies, waits for them, and re-layouts  2.37 us
    ppermute x3, waiting for transfers between devices, swap_pair(): return lax.ppermute(block, 'fsdp', [(0, 1), (1, 0)])  1.99 us
    ppermute x1, waiting for transfers between devices, body(): edge_video = lax.ppermute(frame, ('video', 'fsdp'), route)  1.23 us
    ppermute x3, starting transfers between devices, swap_pair(): return lax.ppermute(block, 'fsdp', [(0, 1), (1, 0)])  1.05 us
    another operation x1, other arithmetic, body(): scalars = jnp.stack([side.astype(jnp.int32), keep_edge, keep_partner])  0.65 us
  transfers between devices with their start and end apart: 4, of which 2 were waited for; matrix products, arithmetic and copies ran while one was open for 2% of the time, Pallas kernels for 27%

profile of v8, /device:TPU:17, one launch (start us, length us, event | category | flops | bytes accessed | tf_op | source)
XLA Modules:
  0.0 26.9 jit_solution(16662084798224346720)
XLA Ops:
  0.0 0.7 %collective-permute-start.1 = (bf16[3,3,256,512]{3,2,1,0:T(8,128)(2,1)}, bf16[3,3,256,512]{3,2,1,0:T(8,128)(2,1)S(1)}, u32[]{:S(2)}, u32[]{:S(2)}) collective-permute-start(bf16[3,3,256,512]{3,2,1,0:T(8,128)(2,1)} %param.6), channel_id=1, source_target_pairs={{0,1},{1,0},{2,3},{3,2},{4,5},{5,4},{6,7},{7,6},{8,9},{9,8},{10,11... | collective-permute-start | bytes 7077896 | tf_op jit(solution)/shard_map/ppermute | solution.py:16
  0.7 0.0 collective-permute-start.3
  0.7 3.5 %collective-permute-start = (bf16[512,512]{1,0:T(8,128)(2,1)}, bf16[512,512]{1,0:T(8,128)(2,1)S(1)}, u32[]{:S(2)}, u32[]{:S(2)}) collective-permute-start(bf16[512,512]{1,0:T(8,128)(2,1)} %bitcast.15), channel_id=1, source_target_pairs={{1,2},{2,1},{3,4},{4,3},{5,6},{6,5},{7,8},{8,7},{9,10},{10,9},{11,... | collective-permute-start | bytes 1572872 | tf_op jit(solution)/shard_map/ppermute | solution.py:202
  4.2 2.0 %collective-permute-done.1 = bf16[3,3,256,512]{3,2,1,0:T(8,128)(2,1)S(1)} collective-permute-done((bf16[3,3,256,512]{3,2,1,0:T(8,128)(2,1)}, bf16[3,3,256,512]{3,2,1,0:T(8,128)(2,1)S(1)}, u32[]{:S(2)}, u32[]{:S(2)}) %collective-permute-start.1) | collective-permute-done | bytes 2359328 | tf_op jit(solution)/shard_map/ppermute | solution.py:16
  6.2 0.0 copy-start
  6.2 1.4 %copy-done = bf16[3,3,256,512]{3,2,1,0:T(8,128)(2,1)} copy-done((bf16[3,3,256,512]{3,2,1,0:T(8,128)(2,1)}, bf16[3,3,256,512]{3,2,1,0:T(8,128)(2,1)S(1)}, u32[]{:S(2)}) %copy-start) | copy-done | bytes 2359320
  7.6 7.2 %shard_map.55.cur_hbm = bf16[512,512]{1,0:T(8,128)(2,1)} custom-call(s32[1]{0:T(128)} %bitcast.side_ref, bf16[512,512]{1,0:T(8,128)(2,1)} %bitcast.16, bf16[512,512]{1,0:T(8,128)(2,1)} %bitcast.17, bf16[2304,512]{1,0:T(8,128)(2,1)} %bitcast.11, bf16[2304,512]{1,0:T(8,128)(2,1)} %bitcast.13, f32[1,512]{1,0:T(1,128)} %bitcast.19, f32[1,512]{1,0:T(1,128)} %bitcast.21), custom_call_target="tpu_custom_call" | custom-call | tf_op jit(solution)/shard_map/pallas_call | solution.py:78
  14.7 0.4 %collective-permute-start.2 = (bf16[512,512]{1,0:T(8,128)(2,1)}, bf16[512,512]{1,0:T(8,128)(2,1)S(1)}, u32[]{:S(2)}, u32[]{:S(2)}) collective-permute-start(bf16[512,512]{1,0:T(8,128)(2,1)} %shard_map.55.cur_hbm), channel_id=1, source_target_pairs={{0,1},{1,0},{2,3},{3,2},{4,5},{5,4},{6,7},{7,6},{8,9},{9,8},{10,11... | collective-permute-start | bytes 1572872 | tf_op jit(solution)/shard_map/ppermute | solution.py:16
  15.1 0.7 %pad_add_fusion.s_ref = s32[3]{0:T(128)} fusion(s32[1]{0:T(128)} %bitcast.2, s32[1]{0:T(128)} %bitcast.1, s32[1]{0:T(128)} %bitcast.side_ref), kind=kLoop, calls=%fused_computation | loop fusion | flops 6 | bytes 24 | tf_op jit(solution)/shard_map/stack | solution.py:215
  15.8 1.2 %collective-permute-done.xa_ref.xb_ref = bf16[512,512]{1,0:T(8,128)(2,1)S(1)} collective-permute-done((bf16[512,512]{1,0:T(8,128)(2,1)}, bf16[512,512]{1,0:T(8,128)(2,1)S(1)}, u32[]{:S(2)}, u32[]{:S(2)}) %collective-permute-start) | collective-permute-done | bytes 524320 | tf_op jit(solution)/shard_map/ppermute | solution.py:202
  17.0 0.0 copy-start.1
  17.0 0.0 collective-permute-done.3
  17.0 0.0 collective-permute-done.2.partner_hbm
  17.0 0.0 copy-start.2
  17.0 0.8 %copy-done.1 = bf16[512,512]{1,0:T(8,128)(2,1)} copy-done((bf16[512,512]{1,0:T(8,128)(2,1)}, bf16[512,512]{1,0:T(8,128)(2,1)S(1)}, u32[]{:S(2)}) %copy-start.1) | copy-done | bytes 524312
  17.8 0.2 copy-done.2
  18.0 8.9 %shard_map.56 = bf16[512,512]{1,0:T(8,128)(2,1)} custom-call(s32[3]{0:T(128)} %pad_add_fusion.s_ref, bf16[512,512]{1,0:T(8,128)(2,1)} %copy-done.1, bf16[512,512]{1,0:T(8,128)(2,1)} %copy-done.1, bf16[2304,512]{1,0:T(8,128)(2,1)} %bitcast.12, bf16[2304,512]{1,0:T(8,128)(2,1)} %bitcast.14, f32[1,512]{1,0:T(1,128)} %bitcast.20, f32[1,512]{1,0:T(1,128)} %bitcast.22, ...), custom_call_target="tpu_custom_call" | custom-call | tf_op jit(solution)/shard_map/pallas_call | solution.py:152
Async XLA Ops:
  0.0 6.2 %collective-permute-start.1 = (bf16[3,3,256,512]{3,2,1,0:T(8,128)(2,1)}, bf16[3,3,256,512]{3,2,1,0:T(8,128)(2,1)S(1)}, u32[]{:S(2)}, u32[]{:S(2)}) collective-permute-start(bf16[3,3,256,512]{3,2,1,0:T(8,128)(2,1)} %param.6), channel_id=1, source_target_pairs={{0,1},{1,0},{2,3},{3,2},{4,5},{5,4},{6,7},{7,6},{8,9},{9,8},{10,11... | collective-permute-start | bytes 7077896 | tf_op jit(solution)/shard_map/ppermute | solution.py:16
  0.7 16.3 %collective-permute-start.3 = (bf16[3,256,512]{2,1,0:T(8,128)(2,1)}, bf16[3,256,512]{2,1,0:T(8,128)(2,1)}, u32[]{:S(2)}, u32[]{:S(2)}) collective-permute-start(bf16[3,256,512]{2,1,0:T(8,128)(2,1)} %param.9), channel_id=1, source_target_pairs={{0,1},{1,0},{2,3},{3,2},{4,5},{5,4},{6,7},{7,6},{8,9},{9,8},{10,11... | collective-permute-start | bytes 2359304 | tf_op jit(solution)/shard_map/ppermute | solution.py:16
  0.7 16.3 %collective-permute-start = (bf16[512,512]{1,0:T(8,128)(2,1)}, bf16[512,512]{1,0:T(8,128)(2,1)S(1)}, u32[]{:S(2)}, u32[]{:S(2)}) collective-permute-start(bf16[512,512]{1,0:T(8,128)(2,1)} %bitcast.15), channel_id=1, source_target_pairs={{1,2},{2,1},{3,4},{4,3},{5,6},{6,5},{7,8},{8,7},{9,10},{10,9},{11,... | collective-permute-start | bytes 1572872 | tf_op jit(solution)/shard_map/ppermute | solution.py:202
  6.2 1.4 %copy-start = (bf16[3,3,256,512]{3,2,1,0:T(8,128)(2,1)}, bf16[3,3,256,512]{3,2,1,0:T(8,128)(2,1)S(1)}, u32[]{:S(2)}) copy-start(bf16[3,3,256,512]{3,2,1,0:T(8,128)(2,1)S(1)} %collective-permute-done.1) | copy-start | bytes 7077892
  14.7 2.3 %collective-permute-start.2 = (bf16[512,512]{1,0:T(8,128)(2,1)}, bf16[512,512]{1,0:T(8,128)(2,1)S(1)}, u32[]{:S(2)}, u32[]{:S(2)}) collective-permute-start(bf16[512,512]{1,0:T(8,128)(2,1)} %shard_map.55.cur_hbm), channel_id=1, source_target_pairs={{0,1},{1,0},{2,3},{3,2},{4,5},{5,4},{6,7},{7,6},{8,9},{9,8},{10,11... | collective-permute-start | bytes 1572872 | tf_op jit(solution)/shard_map/ppermute | solution.py:16
  17.0 0.8 %copy-start.1 = (bf16[512,512]{1,0:T(8,128)(2,1)}, bf16[512,512]{1,0:T(8,128)(2,1)S(1)}, u32[]{:S(2)}) copy-start(bf16[512,512]{1,0:T(8,128)(2,1)S(1)} %collective-permute-done.xa_ref.xb_ref) | copy-start | bytes 1572868
  17.0 1.0 %copy-start.2 = (bf16[512,512]{1,0:T(8,128)(2,1)}, bf16[512,512]{1,0:T(8,128)(2,1)S(1)}, u32[]{:S(2)}) copy-start(bf16[512,512]{1,0:T(8,128)(2,1)S(1)} %collective-permute-done.2.partner_hbm) | copy-start | bytes 1572868

commit v9 on v8

--- a/solution.py
+++ b/solution.py
@@ -28,31 +28,36 @@
     return row
 
 
+def build_lhs(halves, lhs_ref, width):
+    rows, half = halves[0][1].shape
+    col = lax.broadcasted_iota(jnp.int32, (rows, half), 0) % width
+    zeros = jnp.zeros((width, half), jnp.bfloat16)
+    for h, x in halves:
+        xf = x.astype(jnp.float32)
+        left = jnp.where(col == 0, 0.0, pltpu.roll(xf, 1, 0)).astype(jnp.bfloat16)
+        right = jnp.where(col == width - 1, 0.0, pltpu.roll(xf, rows - 1, 0)).astype(jnp.bfloat16)
+        for dx, v in enumerate((left, xf.astype(jnp.bfloat16), right)):
+            for dy in range(3):
+                lo = (dy * 3 + dx) * half
+                cols = slice(lo, lo + half)
+                if dy == 0:
+                    lhs_ref[h, :width, cols] = zeros
+                    lhs_ref[h, width:, cols] = v[: rows - width]
+                elif dy == 1:
+                    lhs_ref[h, :, cols] = v
+                else:
+                    lhs_ref[h, : rows - width, cols] = v[width:]
+                    lhs_ref[h, rows - width :, cols] = zeros
+
+
 def conv_norm_kernel(side_ref, xa_ref, xb_ref, wa_ref, wb_ref, gain_ref, shift_ref, o_ref,
                      lhs_ref, *, width, group):
-    rows, half = xa_ref.shape
-
-    @pl.when(pl.program_id(0) == 0)
-    def _prepare():
-        col = lax.broadcasted_iota(jnp.int32, (rows, half), 0) % width
-        zeros = jnp.zeros((width, half), jnp.bfloat16)
-        for h, x_ref in enumerate((xa_ref, xb_ref)):
-            xf = x_ref[...].astype(jnp.float32)
-            left = jnp.where(col == 0, 0.0, pltpu.roll(xf, 1, 0)).astype(jnp.bfloat16)
-            right = jnp.where(col == width - 1, 0.0, pltpu.roll(xf, rows - 1, 0)).astype(jnp.bfloat16)
-            for dx, v in enumerate((left, xf.astype(jnp.bfloat16), right)):
-                for dy in range(3):
-                    lo = (dy * 3 + dx) * half
-                    cols = slice(lo, lo + half)
-                    if dy == 0:
-                        lhs_ref[h, :width, cols] = zeros
-                        lhs_ref[h, width:, cols] = v[: rows - width]
-                    elif dy == 1:
-                        lhs_ref[h, :, cols] = v
-                    else:
-                        lhs_ref[h, : rows - width, cols] = v[width:]
-                        lhs_ref[h, rows - width :, cols] = zeros
-
+    build_lhs(((0, xa_ref[...]), (1, xb_ref[...])), lhs_ref, width)
+    dots_norm(lhs_ref, wa_ref, wb_ref, gain_ref, shift_ref, o_ref, group)
+
+
+def dots_norm(lhs_ref, wa_ref, wb_ref, gain_ref, shift_ref, o_ref, group):
+    rows = lhs_ref.shape[1]
     acc = jnp.dot(lhs_ref[0], wa_ref[...], preferred_element_type=jnp.float32) + jnp.dot(
         lhs_ref[1], wb_ref[...], preferred_element_type=jnp.float32
     )
@@ -97,24 +102,27 @@
       gain, shift)
 
 
-def edge_temporal_kernel(s_ref, xa_ref, xb_ref, wa_ref, wb_ref, gain_ref, shift_ref,
-                         cur_hbm, partner_hbm, wtm_hbm, wto_hbm, o_ref,
-                         lhs_ref, edge_v, cur_v, partner_v, wtm_v, wto_v, tl_ref, sem,
+def edge_temporal_kernel(s_ref, x_ref, wa_ref, wb_ref, gain_ref, shift_ref,
+                         cur_hbm, partner_v, wtm_hbm, wto_v, o_ref,
+                         lhs_ref, edge_v, cur_v, wtm_v, tl_ref, sem,
                          *, width, group):
     copies = [
         pltpu.make_async_copy(src, dst, sem.at[i])
         for i, (src, dst) in enumerate(
-            ((cur_hbm, cur_v), (partner_hbm, partner_v), (wtm_hbm, wtm_v), (wto_hbm, wto_v))
+            ((cur_hbm, cur_v), (wtm_hbm, wtm_v))
         )
     ]
     for copy in copies:
         copy.start()
-    conv_norm_kernel(s_ref, xa_ref, xb_ref, wa_ref, wb_ref, gain_ref, shift_ref, edge_v,
-                     lhs_ref, width=width, group=group)
+    half = x_ref.shape[1] // 2
+    build_lhs(
+        [((h + s_ref[0]) % 2, x_ref[:, h * half : (h + 1) * half]) for h in range(2)], lhs_ref, width
+    )
+    dots_norm(lhs_ref, wa_ref, wb_ref, gain_ref, shift_ref, edge_v, group)
     for copy in copies:
         copy.wait()
 
-    rows, half = xa_ref.shape
+    rows = x_ref.shape[0]
     keep_edge = s_ref[1] != 0
     keep_partner = s_ref[2] != 0
     for side in range(2):
@@ -149,6 +157,7 @@
     weight_block = pl.BlockSpec((9 * half, outputs), lambda n, s: (0, 0))
     row_block = pl.BlockSpec((1, outputs), lambda n, s: (0, 0))
     anywhere = pl.BlockSpec(memory_space=pl.ANY)
+    in_vmem = pl.BlockSpec(memory_space=pltpu.VMEM)
     return pl.pallas_call(
         kernel,
         out_shape=jax.ShapeDtypeStruct((rows, outputs), jnp.bfloat16),
@@ -156,31 +165,28 @@
             num_scalar_prefetch=1,
             grid=(1,),
             in_specs=[
-                pl.BlockSpec((rows, half), lambda n, s: (0, s[0])),
-                pl.BlockSpec((rows, half), lambda n, s: (0, 1 - s[0])),
+                in_vmem,
                 weight_block,
                 weight_block,
                 row_block,
                 row_block,
                 anywhere,
+                in_vmem,
                 anywhere,
-                anywhere,
-                anywhere,
+                in_vmem,
             ],
             out_specs=pl.BlockSpec((rows, outputs), lambda n, s: (0, 0)),
             scratch_shapes=[
                 pltpu.VMEM((2, rows, 9 * half), jnp.bfloat16),
                 pltpu.VMEM((rows, outputs), jnp.bfloat16),
                 pltpu.VMEM((rows, channels), jnp.bfloat16),
-                pltpu.VMEM((rows, channels), jnp.bfloat16),
-                pltpu.VMEM((3 * half, outputs), jnp.bfloat16),
                 pltpu.VMEM((3 * half, outputs), jnp.bfloat16),
                 pltpu.VMEM((2, rows, 3 * half), jnp.bfloat16),
-                pltpu.SemaphoreType.DMA((4,)),
+                pltpu.SemaphoreType.DMA((2,)),
             ],
         ),
         compiler_params=pltpu.CompilerParams(dimension_semantics=("arbitrary",)),
-    )(scalars, frame, frame, w_mine.reshape(9 * half, outputs), w_other.reshape(9 * half, outputs),
+    )(scalars, frame, w_mine.reshape(9 * half, outputs), w_other.reshape(9 * half, outputs),
       gain, shift, cur, partner, t_mine.reshape(3 * half, outputs),
       t_other.reshape(3 * half, outputs))
 

time: 27.1 us -> 27.9 us (1.030)
  Pallas kernels: 16.1 us -> 16.7 us
    ppermute x1, waiting for transfers between devices: 1.23 us -> 2.46 us  [body(): edge_video = lax.ppermute(frame, ('video', 'fsdp'), route)]
    ppermute x3, waiting for transfers between devices: 1.99 us -> 0.86 us  [swap_pair(): return lax.ppermute(block, 'fsdp', [(0, 1), (1, 0)])]
    pallas_call x1, Pallas kernels: 8.89 us -> 9.52 us  [edge_temporal(): pl.pallas_call(kernel, out_shape=jax.ShapeDtypeStruct((rows, outputs), jn...]
  transfers between devices with their start and end apart: 4 -> 4, of which waited for: 2 -> 2; matrix products, arithmetic and copies ran while one was open for 2% -> 2% of each run, Pallas kernels for 27% -> 26%
where the time goes in v9:
time: 27.9 us; the launch traced here: 27.7 us
  Pallas kernels  16.7 us (60%)
  starting transfers between devices  4.56 us (16%)
  waiting for transfers between devices  3.32 us (12%)
  local copies, waits for them, and re-layouts  2.51 us (9%)
  other arithmetic  0.65 us (2%)
    pallas_call x1, Pallas kernels, edge_temporal(): pl.pallas_call(kernel, out_shape=jax.ShapeDtypeStruct((rows, outputs), jn...  9.52 us
    pallas_call x1, Pallas kernels, conv_norm(): pl.pallas_call(kernel, out_shape=jax.ShapeDtypeStruct((rows, outputs), jn...  7.15 us
    ppermute x1, starting transfers between devices, body(): edge_video = lax.ppermute(frame, ('video', 'fsdp'), route)  3.5 us
    unnamed x6, local copies, waits for them, and re-layouts  2.51 us
    ppermute x1, waiting for transfers between devices, body(): edge_video = lax.ppermute(frame, ('video', 'fsdp'), route)  2.46 us
    ppermute x3, starting transfers between devices, swap_pair(): return lax.ppermute(block, 'fsdp', [(0, 1), (1, 0)])  1.06 us
    ppermute x3, waiting for transfers between devices, swap_pair(): return lax.ppermute(block, 'fsdp', [(0, 1), (1, 0)])  0.86 us
    another operation x1, other arithmetic, body(): scalars = jnp.stack([side.astype(jnp.int32), keep_edge, keep_partner])  0.65 us
  transfers between devices with their start and end apart: 4, of which 2 were waited for; matrix products, arithmetic and copies ran while one was open for 2% of the time, Pallas kernels for 26%

profile of v9, /device:TPU:17, one launch (start us, length us, event | category | flops | bytes accessed | tf_op | source)
XLA Modules:
  0.0 27.7 jit_solution(12313540247593115619)
XLA Ops:
  0.0 0.7 %collective-permute-start.1 = (bf16[3,3,256,512]{3,2,1,0:T(8,128)(2,1)}, bf16[3,3,256,512]{3,2,1,0:T(8,128)(2,1)S(1)}, u32[]{:S(2)}, u32[]{:S(2)}) collective-permute-start(bf16[3,3,256,512]{3,2,1,0:T(8,128)(2,1)} %param.6), channel_id=1, source_target_pairs={{0,1},{1,0},{2,3},{3,2},{4,5},{5,4},{6,7},{7,6},{8,9},{9,8},{10,11... | collective-permute-start | bytes 7077896 | tf_op jit(solution)/shard_map/ppermute | solution.py:16
  0.7 0.0 collective-permute-start.3
  0.7 3.5 %collective-permute-start = (bf16[512,512]{1,0:T(8,128)(2,1)}, bf16[512,512]{1,0:T(8,128)(2,1)}, u32[]{:S(2)}, u32[]{:S(2)}) collective-permute-start(bf16[512,512]{1,0:T(8,128)(2,1)} %bitcast.15), channel_id=1, source_target_pairs={{1,2},{2,1},{3,4},{4,3},{5,6},{6,5},{7,8},{8,7},{9,10},{10,9},{11,... | collective-permute-start | bytes 1572872 | tf_op jit(solution)/shard_map/ppermute | solution.py:208
  4.2 0.9 %collective-permute-done.1 = bf16[3,3,256,512]{3,2,1,0:T(8,128)(2,1)S(1)} collective-permute-done((bf16[3,3,256,512]{3,2,1,0:T(8,128)(2,1)}, bf16[3,3,256,512]{3,2,1,0:T(8,128)(2,1)S(1)}, u32[]{:S(2)}, u32[]{:S(2)}) %collective-permute-start.1) | collective-permute-done | bytes 2359328 | tf_op jit(solution)/shard_map/ppermute | solution.py:16
  5.0 0.0 copy-start
  5.1 1.4 %copy-done = bf16[3,3,256,512]{3,2,1,0:T(8,128)(2,1)} copy-done((bf16[3,3,256,512]{3,2,1,0:T(8,128)(2,1)}, bf16[3,3,256,512]{3,2,1,0:T(8,128)(2,1)S(1)}, u32[]{:S(2)}) %copy-start) | copy-done | bytes 2359320
  6.5 7.2 %shard_map.55.cur_hbm = bf16[512,512]{1,0:T(8,128)(2,1)} custom-call(s32[1]{0:T(128)} %bitcast.side_ref, bf16[512,512]{1,0:T(8,128)(2,1)} %bitcast.16, bf16[512,512]{1,0:T(8,128)(2,1)} %bitcast.17, bf16[2304,512]{1,0:T(8,128)(2,1)} %bitcast.11, bf16[2304,512]{1,0:T(8,128)(2,1)} %bitcast.13, f32[1,512]{1,0:T(1,128)} %bitcast.20, f32[1,512]{1,0:T(1,128)} %bitcast.22), custom_call_target="tpu_custom_call" | custom-call | tf_op jit(solution)/shard_map/pallas_call | solution.py:83
  13.6 0.4 %collective-permute-start.2 = (bf16[512,512]{1,0:T(8,128)(2,1)}, bf16[512,512]{1,0:T(8,128)(2,1)S(1)}, u32[]{:S(2)}, u32[]{:S(2)}) collective-permute-start(bf16[512,512]{1,0:T(8,128)(2,1)} %shard_map.55.cur_hbm), channel_id=1, source_target_pairs={{0,1},{1,0},{2,3},{3,2},{4,5},{5,4},{6,7},{7,6},{8,9},{9,8},{10,11... | collective-permute-start | bytes 1572872 | tf_op jit(solution)/shard_map/ppermute | solution.py:16
  14.0 0.7 %pad_add_fusion.s_ref = s32[3]{0:T(128)} fusion(s32[1]{0:T(128)} %bitcast.2, s32[1]{0:T(128)} %bitcast.1, s32[1]{0:T(128)} %bitcast.side_ref), kind=kLoop, calls=%fused_computation | loop fusion | flops 6 | bytes 24 | tf_op jit(solution)/shard_map/stack | solution.py:221
  14.6 2.5 %collective-permute-done.x_ref = bf16[512,512]{1,0:T(8,128)(2,1)} collective-permute-done((bf16[512,512]{1,0:T(8,128)(2,1)}, bf16[512,512]{1,0:T(8,128)(2,1)}, u32[]{:S(2)}, u32[]{:S(2)}) %collective-permute-start) | collective-permute-done | bytes 524320 | tf_op jit(solution)/shard_map/ppermute | solution.py:208
  17.1 0.0 collective-permute-done.3
  17.1 0.0 copy-start.1
  17.1 0.0 collective-permute-done.2.partner_v
  17.1 0.0 copy-start.2
  17.1 0.9 %copy-done.1 = bf16[3,256,512]{2,1,0:T(8,128)(2,1)} copy-done((bf16[3,256,512]{2,1,0:T(8,128)(2,1)}, bf16[3,256,512]{2,1,0:T(8,128)(2,1)S(1)}, u32[]{:S(2)}) %copy-start.1) | copy-done | bytes 786456
  18.0 0.2 copy-done.2
  18.2 9.5 %shard_map.56 = bf16[512,512]{1,0:T(8,128)(2,1)} custom-call(s32[3]{0:T(128)} %pad_add_fusion.s_ref, bf16[512,512]{1,0:T(8,128)(2,1)} %collective-permute-done.x_ref, bf16[2304,512]{1,0:T(8,128)(2,1)} %bitcast.12, bf16[2304,512]{1,0:T(8,128)(2,1)} %bitcast.14, f32[1,512]{1,0:T(1,128)} %bitcast.21, f32[1,512]{1,0:T(1,128)} %bitcast.23, ...), custom_call_target="tpu_custom_call" | custom-call | tf_op jit(solution)/shard_map/pallas_call | solution.py:161
Async XLA Ops:
  0.0 5.0 %collective-permute-start.1 = (bf16[3,3,256,512]{3,2,1,0:T(8,128)(2,1)}, bf16[3,3,256,512]{3,2,1,0:T(8,128)(2,1)S(1)}, u32[]{:S(2)}, u32[]{:S(2)}) collective-permute-start(bf16[3,3,256,512]{3,2,1,0:T(8,128)(2,1)} %param.6), channel_id=1, source_target_pairs={{0,1},{1,0},{2,3},{3,2},{4,5},{5,4},{6,7},{7,6},{8,9},{9,8},{10,11... | collective-permute-start | bytes 7077896 | tf_op jit(solution)/shard_map/ppermute | solution.py:16
  0.7 16.4 %collective-permute-start.3 = (bf16[3,256,512]{2,1,0:T(8,128)(2,1)}, bf16[3,256,512]{2,1,0:T(8,128)(2,1)S(1)}, u32[]{:S(2)}, u32[]{:S(2)}) collective-permute-start(bf16[3,256,512]{2,1,0:T(8,128)(2,1)} %param.9), channel_id=1, source_target_pairs={{0,1},{1,0},{2,3},{3,2},{4,5},{5,4},{6,7},{7,6},{8,9},{9,8},{10,11... | collective-permute-start | bytes 2359304 | tf_op jit(solution)/shard_map/ppermute | solution.py:16
  0.7 16.4 %collective-permute-start = (bf16[512,512]{1,0:T(8,128)(2,1)}, bf16[512,512]{1,0:T(8,128)(2,1)}, u32[]{:S(2)}, u32[]{:S(2)}) collective-permute-start(bf16[512,512]{1,0:T(8,128)(2,1)} %bitcast.15), channel_id=1, source_target_pairs={{1,2},{2,1},{3,4},{4,3},{5,6},{6,5},{7,8},{8,7},{9,10},{10,9},{11,... | collective-permute-start | bytes 1572872 | tf_op jit(solution)/shard_map/ppermute | solution.py:208
  5.0 1.4 %copy-start = (bf16[3,3,256,512]{3,2,1,0:T(8,128)(2,1)}, bf16[3,3,256,512]{3,2,1,0:T(8,128)(2,1)S(1)}, u32[]{:S(2)}) copy-start(bf16[3,3,256,512]{3,2,1,0:T(8,128)(2,1)S(1)} %collective-permute-done.1) | copy-start | bytes 7077892
  13.6 3.5 %collective-permute-start.2 = (bf16[512,512]{1,0:T(8,128)(2,1)}, bf16[512,512]{1,0:T(8,128)(2,1)S(1)}, u32[]{:S(2)}, u32[]{:S(2)}) collective-permute-start(bf16[512,512]{1,0:T(8,128)(2,1)} %shard_map.55.cur_hbm), channel_id=1, source_target_pairs={{0,1},{1,0},{2,3},{3,2},{4,5},{5,4},{6,7},{7,6},{8,9},{9,8},{10,11... | collective-permute-start | bytes 1572872 | tf_op jit(solution)/shard_map/ppermute | solution.py:16
  17.1 0.9 %copy-start.1 = (bf16[3,256,512]{2,1,0:T(8,128)(2,1)}, bf16[3,256,512]{2,1,0:T(8,128)(2,1)S(1)}, u32[]{:S(2)}) copy-start(bf16[3,256,512]{2,1,0:T(8,128)(2,1)S(1)} %collective-permute-done.3) | copy-start | bytes 2359300
  17.1 1.1 %copy-start.2 = (bf16[512,512]{1,0:T(8,128)(2,1)}, bf16[512,512]{1,0:T(8,128)(2,1)S(1)}, u32[]{:S(2)}) copy-start(bf16[512,512]{1,0:T(8,128)(2,1)S(1)} %collective-permute-done.2.partner_v) | copy-start | bytes 1572868

commit v10 on v8

--- a/solution.py
+++ b/solution.py
@@ -66,6 +66,57 @@
     o_ref[...] = (v / (1.0 + jnp.exp(-v))).astype(o_ref.dtype)
 
 
+def own_conv_kernel(side_ref, xa_ref, xb_ref, wa_ref, wb_ref, gain_ref, shift_ref, tm_ref, to_ref,
+                    o_ref, p_ref, lhs_ref, *, width, group):
+    conv_norm_kernel(side_ref, xa_ref, xb_ref, wa_ref, wb_ref, gain_ref, shift_ref, o_ref,
+                     lhs_ref, width=width, group=group)
+    half = xa_ref.shape[1]
+    for side in range(2):
+        @pl.when(side_ref[0] == side)
+        def _tap():
+            mine = slice(side * half, (side + 1) * half)
+            other = slice((1 - side) * half, (2 - side) * half)
+            p_ref[...] = jnp.dot(o_ref[:, mine], tm_ref[0], preferred_element_type=jnp.float32) + jnp.dot(
+                o_ref[:, other], to_ref[0], preferred_element_type=jnp.float32
+            )
+
+
+def own_conv(frame, w_mine, w_other, gain, shift, t_mine, t_other, side, width):
+    rows, channels = frame.shape
+    half = w_mine.shape[2]
+    outputs = w_mine.shape[3]
+    group = outputs // GROUPS
+    kernel = functools.partial(own_conv_kernel, width=width, group=group)
+    weight_block = pl.BlockSpec((9 * half, outputs), lambda n, s: (0, 0))
+    row_block = pl.BlockSpec((1, outputs), lambda n, s: (0, 0))
+    tap_block = pl.BlockSpec((1, half, outputs), lambda n, s: (1, 0, 0))
+    whole = pl.BlockSpec((rows, outputs), lambda n, s: (0, 0))
+    return pl.pallas_call(
+        kernel,
+        out_shape=(
+            jax.ShapeDtypeStruct((rows, outputs), jnp.bfloat16),
+            jax.ShapeDtypeStruct((rows, outputs), jnp.float32),
+        ),
+        grid_spec=pltpu.PrefetchScalarGridSpec(
+            num_scalar_prefetch=1,
+            grid=(1,),
+            in_specs=[
+                pl.BlockSpec((rows, half), lambda n, s: (0, s[0])),
+                pl.BlockSpec((rows, half), lambda n, s: (0, 1 - s[0])),
+                weight_block,
+                weight_block,
+                row_block,
+                row_block,
+                tap_block,
+                tap_block,
+            ],
+            out_specs=(whole, whole),
+            scratch_shapes=[pltpu.VMEM((2, rows, 9 * half), jnp.bfloat16)],
+        ),
+    )(side, frame, frame, w_mine.reshape(9 * half, outputs), w_other.reshape(9 * half, outputs),
+      gain, shift, t_mine, t_other)
+
+
 def conv_norm(frame, w_mine, w_other, gain, shift, side, width, split=1):
     rows, channels = frame.shape
     half = w_mine.shape[2]
@@ -98,13 +149,15 @@
 
 
 def edge_temporal_kernel(s_ref, xa_ref, xb_ref, wa_ref, wb_ref, gain_ref, shift_ref,
-                         cur_hbm, partner_hbm, wtm_hbm, wto_hbm, o_ref,
-                         lhs_ref, edge_v, cur_v, partner_v, wtm_v, wto_v, tl_ref, sem,
+                         cur_hbm, own_hbm, partner_hbm, wtm_hbm, wto_hbm, o_ref,
+                         lhs_ref, edge_v, cur_v, own_v, partner_v, wtm_v, wto_v, tl_ref, sem,
                          *, width, group):
     copies = [
         pltpu.make_async_copy(src, dst, sem.at[i])
         for i, (src, dst) in enumerate(
-            ((cur_hbm, cur_v), (partner_hbm, partner_v), (wtm_hbm, wtm_v), (wto_hbm, wto_v))
+            ((cur_hbm, cur_v), (own_hbm, own_v), (partner_hbm, partner_v),
+             (wtm_hbm.at[0], wtm_v.at[0]), (wtm_hbm.at[2], wtm_v.at[1]),
+             (wto_hbm.at[0], wto_v.at[0]), (wto_hbm.at[2], wto_v.at[1]))
         )
     ]
     for copy in copies:
@@ -129,18 +182,19 @@
                 p = jnp.where(keep_partner, p, jnp.zeros_like(p))
                 before, after = (e, p) if side == 0 else (p, e)
                 tl_ref[h, :, :half] = before
-                tl_ref[h, :, half : 2 * half] = cur_v[:, cols]
-                tl_ref[h, :, 2 * half :] = after
+                tl_ref[h, :, half:] = after
 
     f32 = jnp.float32
-    total = jnp.dot(tl_ref[0], wtm_v[...], preferred_element_type=f32) + jnp.dot(
-        tl_ref[1], wto_v[...], preferred_element_type=f32
-    )
+    taps = wtm_v.shape[0] * wtm_v.shape[1]
+    total = jnp.dot(tl_ref[0], wtm_v[...].reshape(taps, -1), preferred_element_type=f32) + jnp.dot(
+        tl_ref[1], wto_v[...].reshape(taps, -1), preferred_element_type=f32
+    )
+    total = total + own_v[...]
     o_ref[...] = (cur_v[...].astype(f32) + total).astype(o_ref.dtype)
 
 
-def edge_temporal(frame, w_mine, w_other, gain, shift, cur, partner, t_mine, t_other, scalars,
-                  width):
+def edge_temporal(frame, w_mine, w_other, gain, shift, cur, own, partner, t_mine, t_other,
+                  scalars, width):
     rows, channels = frame.shape
     half = w_mine.shape[2]
     outputs = w_mine.shape[3]
@@ -166,23 +220,24 @@
                 anywhere,
                 anywhere,
                 anywhere,
+                anywhere,
             ],
             out_specs=pl.BlockSpec((rows, outputs), lambda n, s: (0, 0)),
             scratch_shapes=[
                 pltpu.VMEM((2, rows, 9 * half), jnp.bfloat16),
                 pltpu.VMEM((rows, outputs), jnp.bfloat16),
                 pltpu.VMEM((rows, channels), jnp.bfloat16),
+                pltpu.VMEM((rows, outputs), jnp.float32),
                 pltpu.VMEM((rows, channels), jnp.bfloat16),
-                pltpu.VMEM((3 * half, outputs), jnp.bfloat16),
-                pltpu.VMEM((3 * half, outputs), jnp.bfloat16),
-                pltpu.VMEM((2, rows, 3 * half), jnp.bfloat16),
-                pltpu.SemaphoreType.DMA((4,)),
+                pltpu.VMEM((2, half, outputs), jnp.bfloat16),
+                pltpu.VMEM((2, half, outputs), jnp.bfloat16),
+                pltpu.VMEM((2, rows, 2 * half), jnp.bfloat16),
+                pltpu.SemaphoreType.DMA((7,)),
             ],
         ),
         compiler_params=pltpu.CompilerParams(dimension_semantics=("arbitrary",)),
     )(scalars, frame, frame, w_mine.reshape(9 * half, outputs), w_other.reshape(9 * half, outputs),
-      gain, shift, cur, partner, t_mine.reshape(3 * half, outputs),
-      t_other.reshape(3 * half, outputs))
+      gain, shift, cur, own, partner, t_mine, t_other)
 
 
 def body(video, w_spatial, norm_gain, norm_shift, w_time):
@@ -206,15 +261,16 @@
     gain = norm_gain.reshape(1, channels)
     shift = norm_shift.reshape(1, channels)
     sides = side.reshape(1).astype(jnp.int32)
-    hidden = conv_norm(frame, w_spatial, other_spatial, gain, shift, sides, width)
+    hidden, own_tap = own_conv(frame, w_spatial, other_spatial, gain, shift, w_time, other_time,
+                               sides, width)
     partner = swap_pair(hidden)
     keep_prev = (position % CLIP != 0).astype(jnp.int32)
     keep_next = (position % CLIP != CLIP - 1).astype(jnp.int32)
     keep_edge = jnp.where(side == 0, keep_prev, keep_next)
     keep_partner = jnp.where(side == 0, keep_next, keep_prev)
     scalars = jnp.stack([side.astype(jnp.int32), keep_edge, keep_partner])
-    result = edge_temporal(edge_video, w_spatial, other_spatial, gain, shift, hidden, partner,
-                           w_time, other_time, scalars, width)
+    result = edge_temporal(edge_video, w_spatial, other_spatial, gain, shift, hidden, own_tap,
+                           partner, w_time, other_time, scalars, width)
     return result.reshape(count, height, width, channels)
 
 

time: 27.1 us -> 28.8 us (1.063)
  Pallas kernels: 16.1 us -> 17.9 us
    pallas_call x1, Pallas kernels: 8.89 us -> 9.94 us  [edge_temporal(): pl.pallas_call(kernel, out_shape=jax.ShapeDtypeStruct((rows, outputs), jn...]
    ppermute x1, waiting for transfers between devices: 1.23 us -> 0.26 us  [body(): edge_video = lax.ppermute(frame, ('video', 'fsdp'), route)]
    pallas_call x1, Pallas kernels: 7.16 us -> 8 us  [own_conv(): pl.pallas_call(kernel, out_shape=(jax.ShapeDtypeStruct((rows, outputs), j...]
    ppermute x3, waiting for transfers between devices: 1.99 us -> 2.82 us  [swap_pair(): return lax.ppermute(block, 'fsdp', [(0, 1), (1, 0)])]
  transfers between devices with their start and end apart: 4 -> 4, of which waited for: 2 -> 3; matrix products, arithmetic and copies ran while one was open for 2% -> 2% of each run, Pallas kernels for 27% -> 28%
where the time goes in v10:
time: 28.8 us; the launch traced here: 28.7 us
  Pallas kernels  17.9 us (62%)
  starting transfers between devices  4.54 us (16%)
  waiting for transfers between devices  3.07 us (11%)
  local copies, waits for them, and re-layouts  2.45 us (9%)
  other arithmetic  0.66 us (2%)
    pallas_call x1, Pallas kernels, edge_temporal(): pl.pallas_call(kernel, out_shape=jax.ShapeDtypeStruct((rows, outputs), jn...  9.94 us
    pallas_call x1, Pallas kernels, own_conv(): pl.pallas_call(kernel, out_shape=(jax.ShapeDtypeStruct((rows, outputs), j...  8 us
    ppermute x1, starting transfers between devices, body(): edge_video = lax.ppermute(frame, ('video', 'fsdp'), route)  3.5 us
    ppermute x3, waiting for transfers between devices, swap_pair(): return lax.ppermute(block, 'fsdp', [(0, 1), (1, 0)])  2.82 us
    unnamed x6, local copies, waits for them, and re-layouts  2.45 us
    ppermute x3, starting transfers between devices, swap_pair(): return lax.ppermute(block, 'fsdp', [(0, 1), (1, 0)])  1.04 us
    another operation x1, other arithmetic, body(): scalars = jnp.stack([side.astype(jnp.int32), keep_edge, keep_partner])  0.66 us
  transfers between devices with their start and end apart: 4, of which 3 were waited for; matrix products, arithmetic and copies ran while one was open for 2% of the time, Pallas kernels for 28%

profile of v10, /device:TPU:17, one launch (start us, length us, event | category | flops | bytes accessed | tf_op | source)
XLA Modules:
  0.0 28.7 jit_solution(17847684984032316077)
XLA Ops:
  0.0 0.7 %collective-permute-start.1 = (bf16[3,3,256,512]{3,2,1,0:T(8,128)(2,1)}, bf16[3,3,256,512]{3,2,1,0:T(8,128)(2,1)S(1)}, u32[]{:S(2)}, u32[]{:S(2)}) collective-permute-start(bf16[3,3,256,512]{3,2,1,0:T(8,128)(2,1)} %param.6), channel_id=1, source_target_pairs={{0,1},{1,0},{2,3},{3,2},{4,5},{5,4},{6,7},{7,6},{8,9},{9,8},{10,11... | collective-permute-start | bytes 7077896 | tf_op jit(solution)/shard_map/ppermute | solution.py:16
  0.7 0.0 collective-permute-start.2
  0.7 3.5 %collective-permute-start = (bf16[512,512]{1,0:T(8,128)(2,1)}, bf16[512,512]{1,0:T(8,128)(2,1)}, u32[]{:S(2)}, u32[]{:S(2)}) collective-permute-start(bf16[512,512]{1,0:T(8,128)(2,1)} %bitcast.13), channel_id=1, source_target_pairs={{1,2},{2,1},{3,4},{4,3},{5,6},{6,5},{7,8},{8,7},{9,10},{10,9},{11,... | collective-permute-start | bytes 1572872 | tf_op jit(solution)/shard_map/ppermute | solution.py:257
  4.2 2.0 %collective-permute-done.2.to_ref.wto_hbm = bf16[3,256,512]{2,1,0:T(8,128)(2,1)S(1)} collective-permute-done((bf16[3,256,512]{2,1,0:T(8,128)(2,1)}, bf16[3,256,512]{2,1,0:T(8,128)(2,1)S(1)}, u32[]{:S(2)}, u32[]{:S(2)}) %collective-permute-start.2) | collective-permute-done | bytes 786464 | tf_op jit(solution)/shard_map/ppermute | solution.py:16
  6.2 0.0 copy-start.1
  6.2 0.0 collective-permute-done.1
  6.2 0.0 copy-start
  6.2 0.9 %copy-done.1 = bf16[3,256,512]{2,1,0:T(8,128)(2,1)} copy-done((bf16[3,256,512]{2,1,0:T(8,128)(2,1)}, bf16[3,256,512]{2,1,0:T(8,128)(2,1)S(1)}, u32[]{:S(2)}) %copy-start.1) | copy-done | bytes 786456
  7.1 0.8 %copy-done = bf16[3,3,256,512]{3,2,1,0:T(8,128)(2,1)} copy-done((bf16[3,3,256,512]{3,2,1,0:T(8,128)(2,1)}, bf16[3,3,256,512]{3,2,1,0:T(8,128)(2,1)S(1)}, u32[]{:S(2)}) %copy-start) | copy-done | bytes 2359320
  7.8 8.0 %shard_map.55 = (bf16[512,512]{1,0:T(8,128)(2,1)}, f32[512,512]{1,0:T(8,128)}) custom-call(s32[1]{0:T(128)} %bitcast.side_ref, bf16[512,512]{1,0:T(8,128)(2,1)} %bitcast.14, bf16[512,512]{1,0:T(8,128)(2,1)} %bitcast.15, bf16[2304,512]{1,0:T(8,128)(2,1)} %bitcast.9, bf16[2304,512]{1,0:T(8,128)(2,1)} %bitcast.11, f32[1,512]{1,0:T(1,128)} %bitcast.16, ...), custom_call_target="tpu_custom_call" | custom-call | tf_op jit(solution)/shard_map/pallas_call | solution.py:94
  15.8 0.4 %collective-permute-start.3 = (bf16[512,512]{1,0:T(8,128)(2,1)}, bf16[512,512]{1,0:T(8,128)(2,1)S(1)}, u32[]{:S(2)}, u32[]{:S(2)}) collective-permute-start(bf16[512,512]{1,0:T(8,128)(2,1)} %get-tuple-element.7.cur_hbm), channel_id=1, source_target_pairs={{0,1},{1,0},{2,3},{3,2},{4,5},{5,4},{6,7},{7,6},{8,9},{9,8},{10,11... | collective-permute-start | bytes 1572872 | tf_op jit(solution)/shard_map/ppermute | solution.py:16
  16.2 0.7 %pad_add_fusion.s_ref = s32[3]{0:T(128)} fusion(s32[1]{0:T(128)} %bitcast.2, s32[1]{0:T(128)} %bitcast.1, s32[1]{0:T(128)} %bitcast.side_ref), kind=kLoop, calls=%fused_computation | loop fusion | flops 6 | bytes 24 | tf_op jit(solution)/shard_map/stack | solution.py:271
  16.8 0.3 collective-permute-done.xa_ref.xb_ref
  17.1 0.8 %collective-permute-done.3.partner_hbm = bf16[512,512]{1,0:T(8,128)(2,1)S(1)} collective-permute-done((bf16[512,512]{1,0:T(8,128)(2,1)}, bf16[512,512]{1,0:T(8,128)(2,1)S(1)}, u32[]{:S(2)}, u32[]{:S(2)}) %collective-permute-start.3) | collective-permute-done | bytes 524320 | tf_op jit(solution)/shard_map/ppermute | solution.py:16
  17.9 0.0 copy-start.2
  17.9 0.8 %copy-done.2 = bf16[512,512]{1,0:T(8,128)(2,1)} copy-done((bf16[512,512]{1,0:T(8,128)(2,1)}, bf16[512,512]{1,0:T(8,128)(2,1)S(1)}, u32[]{:S(2)}) %copy-start.2) | copy-done | bytes 524312
  18.8 9.9 %shard_map.56 = bf16[512,512]{1,0:T(8,128)(2,1)} custom-call(s32[3]{0:T(128)} %pad_add_fusion.s_ref, bf16[512,512]{1,0:T(8,128)(2,1)} %collective-permute-done.xa_ref.xb_ref, bf16[512,512]{1,0:T(8,128)(2,1)} %collective-permute-done.xa_ref.xb_ref, bf16[2304,512]{1,0:T(8,128)(2,1)} %bitcast.10, bf16[2304,512]{1,0:T(8,128)(2,1)} %bitcast.12, ...), custom_call_target="tpu_custom_call" | custom-call | tf_op jit(solution)/shard_map/pallas_call | solution.py:206
Async XLA Ops:
  0.0 6.2 %collective-permute-start.1 = (bf16[3,3,256,512]{3,2,1,0:T(8,128)(2,1)}, bf16[3,3,256,512]{3,2,1,0:T(8,128)(2,1)S(1)}, u32[]{:S(2)}, u32[]{:S(2)}) collective-permute-start(bf16[3,3,256,512]{3,2,1,0:T(8,128)(2,1)} %param.6), channel_id=1, source_target_pairs={{0,1},{1,0},{2,3},{3,2},{4,5},{5,4},{6,7},{7,6},{8,9},{9,8},{10,11... | collective-permute-start | bytes 7077896 | tf_op jit(solution)/shard_map/ppermute | solution.py:16
  0.7 5.5 %collective-permute-start.2 = (bf16[3,256,512]{2,1,0:T(8,128)(2,1)}, bf16[3,256,512]{2,1,0:T(8,128)(2,1)S(1)}, u32[]{:S(2)}, u32[]{:S(2)}) collective-permute-start(bf16[3,256,512]{2,1,0:T(8,128)(2,1)} %wtm_hbm.1), channel_id=1, source_target_pairs={{0,1},{1,0},{2,3},{3,2},{4,5},{5,4},{6,7},{7,6},{8,9},{9,8},{10,11... | collective-permute-start | bytes 2359304 | tf_op jit(solution)/shard_map/ppermute | solution.py:16
  0.7 16.4 %collective-permute-start = (bf16[512,512]{1,0:T(8,128)(2,1)}, bf16[512,512]{1,0:T(8,128)(2,1)}, u32[]{:S(2)}, u32[]{:S(2)}) collective-permute-start(bf16[512,512]{1,0:T(8,128)(2,1)} %bitcast.13), channel_id=1, source_target_pairs={{1,2},{2,1},{3,4},{4,3},{5,6},{6,5},{7,8},{8,7},{9,10},{10,9},{11,... | collective-permute-start | bytes 1572872 | tf_op jit(solution)/shard_map/ppermute | solution.py:257
  6.2 0.9 %copy-start.1 = (bf16[3,256,512]{2,1,0:T(8,128)(2,1)}, bf16[3,256,512]{2,1,0:T(8,128)(2,1)S(1)}, u32[]{:S(2)}) copy-start(bf16[3,256,512]{2,1,0:T(8,128)(2,1)S(1)} %collective-permute-done.2.to_ref.wto_hbm) | copy-start | bytes 2359300
  6.2 1.6 %copy-start = (bf16[3,3,256,512]{3,2,1,0:T(8,128)(2,1)}, bf16[3,3,256,512]{3,2,1,0:T(8,128)(2,1)S(1)}, u32[]{:S(2)}) copy-start(bf16[3,3,256,512]{3,2,1,0:T(8,128)(2,1)S(1)} %collective-permute-done.1) | copy-start | bytes 7077892
  15.8 2.1 %collective-permute-start.3 = (bf16[512,512]{1,0:T(8,128)(2,1)}, bf16[512,512]{1,0:T(8,128)(2,1)S(1)}, u32[]{:S(2)}, u32[]{:S(2)}) collective-permute-start(bf16[512,512]{1,0:T(8,128)(2,1)} %get-tuple-element.7.cur_hbm), channel_id=1, source_target_pairs={{0,1},{1,0},{2,3},{3,2},{4,5},{5,4},{6,7},{7,6},{8,9},{9,8},{10,11... | collective-permute-start | bytes 1572872 | tf_op jit(solution)/shard_map/ppermute | solution.py:16
  17.9 0.8 %copy-start.2 = (bf16[512,512]{1,0:T(8,128)(2,1)}, bf16[512,512]{1,0:T(8,128)(2,1)S(1)}, u32[]{:S(2)}) copy-start(bf16[512,512]{1,0:T(8,128)(2,1)S(1)} %collective-permute-done.3.partner_hbm) | copy-start | bytes 1572868

commit v11 on v9

--- a/solution.py
+++ b/solution.py
@@ -50,17 +50,7 @@
                     lhs_ref[h, rows - width :, cols] = zeros
 
 
-def conv_norm_kernel(side_ref, xa_ref, xb_ref, wa_ref, wb_ref, gain_ref, shift_ref, o_ref,
-                     lhs_ref, *, width, group):
-    build_lhs(((0, xa_ref[...]), (1, xb_ref[...])), lhs_ref, width)
-    dots_norm(lhs_ref, wa_ref, wb_ref, gain_ref, shift_ref, o_ref, group)
-
-
-def dots_norm(lhs_ref, wa_ref, wb_ref, gain_ref, shift_ref, o_ref, group):
-    rows = lhs_ref.shape[1]
-    acc = jnp.dot(lhs_ref[0], wa_ref[...], preferred_element_type=jnp.float32) + jnp.dot(
-        lhs_ref[1], wb_ref[...], preferred_element_type=jnp.float32
-    )
+def norm_silu(acc, gain_ref, shift_ref, o_ref, rows, group):
     count = rows * group
     total = jnp.broadcast_to(jnp.sum(acc, axis=0, keepdims=True), (8, acc.shape[1]))
     mean = group_sum(total, group)[0:1] / count
@@ -69,6 +59,20 @@
     variance = group_sum(spread, group)[0:1] / count
     v = d * lax.rsqrt(variance + EPS) * gain_ref[...] + shift_ref[...]
     o_ref[...] = (v / (1.0 + jnp.exp(-v))).astype(o_ref.dtype)
+
+
+def conv_norm_kernel(side_ref, xa_ref, xb_ref, wa_ref, wb_ref, gain_ref, shift_ref, o_ref,
+                     lhs_ref, *, width, group):
+    rows = xa_ref.shape[0]
+
+    @pl.when(pl.program_id(0) == 0)
+    def _prepare():
+        build_lhs(((0, xa_ref[...]), (1, xb_ref[...])), lhs_ref, width)
+
+    acc = jnp.dot(lhs_ref[0], wa_ref[...], preferred_element_type=jnp.float32) + jnp.dot(
+        lhs_ref[1], wb_ref[...], preferred_element_type=jnp.float32
+    )
+    norm_silu(acc, gain_ref, shift_ref, o_ref, rows, group)
 
 
 def conv_norm(frame, w_mine, w_other, gain, shift, side, width, split=1):
@@ -102,27 +106,50 @@
       gain, shift)
 
 
-def edge_temporal_kernel(s_ref, x_ref, wa_ref, wb_ref, gain_ref, shift_ref,
-                         cur_hbm, partner_v, wtm_hbm, wto_v, o_ref,
-                         lhs_ref, edge_v, cur_v, wtm_v, tl_ref, sem,
-                         *, width, group):
+def edge_temporal_kernel(s_ref, xa_ref, xb_ref, wa_hbm, wb_hbm, gain_ref, shift_ref,
+                         cur_hbm, partner_hbm, wtm_hbm, wto_hbm, o_ref,
+                         lhs_ref, wa_v, wb_v, edge_v, cur_v, partner_v, wtm_v, wto_v, tl_ref, sem,
+                         wsem, *, width, group, chunks=2):
     copies = [
         pltpu.make_async_copy(src, dst, sem.at[i])
         for i, (src, dst) in enumerate(
-            ((cur_hbm, cur_v), (wtm_hbm, wtm_v))
+            ((cur_hbm, cur_v), (partner_hbm, partner_v), (wtm_hbm, wtm_v), (wto_hbm, wto_v))
         )
     ]
+    size = wa_hbm.shape[0] // chunks
+    weight_copies = [
+        [
+            pltpu.make_async_copy(w_hbm.at[pl.ds(k * size, size)], w_v.at[pl.ds(k * size, size)],
+                                  wsem.at[2 * k + i])
+            for i, (w_hbm, w_v) in enumerate(((wa_hbm, wa_v), (wb_hbm, wb_v)))
+        ]
+        for k in range(chunks)
+    ]
+    for pair in weight_copies:
+        for copy in pair:
+            copy.start()
     for copy in copies:
         copy.start()
-    half = x_ref.shape[1] // 2
-    build_lhs(
-        [((h + s_ref[0]) % 2, x_ref[:, h * half : (h + 1) * half]) for h in range(2)], lhs_ref, width
-    )
-    dots_norm(lhs_ref, wa_ref, wb_ref, gain_ref, shift_ref, edge_v, group)
+    rows = xa_ref.shape[0]
+
+    @pl.when(pl.program_id(0) == 0)
+    def _prepare():
+        build_lhs(((0, xa_ref[...]), (1, xb_ref[...])), lhs_ref, width)
+
+    acc = None
+    for k, pair in enumerate(weight_copies):
+        for copy in pair:
+            copy.wait()
+        cols = pl.ds(k * size, size)
+        term = jnp.dot(lhs_ref[0, :, cols], wa_v[cols, :], preferred_element_type=jnp.float32) + jnp.dot(
+            lhs_ref[1, :, cols], wb_v[cols, :], preferred_element_type=jnp.float32
+        )
+        acc = term if acc is None else acc + term
+    norm_silu(acc, gain_ref, shift_ref, edge_v, rows, group)
     for copy in copies:
         copy.wait()
 
-    rows = x_ref.shape[0]
+    rows, half = xa_ref.shape
     keep_edge = s_ref[1] != 0
     keep_partner = s_ref[2] != 0
     for side in range(2):
@@ -157,7 +184,6 @@
     weight_block = pl.BlockSpec((9 * half, outputs), lambda n, s: (0, 0))
     row_block = pl.BlockSpec((1, outputs), lambda n, s: (0, 0))
     anywhere = pl.BlockSpec(memory_space=pl.ANY)
-    in_vmem = pl.BlockSpec(memory_space=pltpu.VMEM)
     return pl.pallas_call(
         kernel,
         out_shape=jax.ShapeDtypeStruct((rows, outputs), jnp.bfloat16),
@@ -165,28 +191,34 @@
             num_scalar_prefetch=1,
             grid=(1,),
             in_specs=[
-                in_vmem,
-                weight_block,
-                weight_block,
-                row_block,
-                row_block,
-                anywhere,
-                in_vmem,
-                anywhere,
-                in_vmem,
+                pl.BlockSpec((rows, half), lambda n, s: (0, s[0])),
+                pl.BlockSpec((rows, half), lambda n, s: (0, 1 - s[0])),
+                anywhere,
+                anywhere,
+                row_block,
+                row_block,
+                anywhere,
+                anywhere,
+                anywhere,
+                anywhere,
             ],
             out_specs=pl.BlockSpec((rows, outputs), lambda n, s: (0, 0)),
             scratch_shapes=[
                 pltpu.VMEM((2, rows, 9 * half), jnp.bfloat16),
+                pltpu.VMEM((9 * half, outputs), jnp.bfloat16),
+                pltpu.VMEM((9 * half, outputs), jnp.bfloat16),
                 pltpu.VMEM((rows, outputs), jnp.bfloat16),
                 pltpu.VMEM((rows, channels), jnp.bfloat16),
+                pltpu.VMEM((rows, channels), jnp.bfloat16),
+                pltpu.VMEM((3 * half, outputs), jnp.bfloat16),
                 pltpu.VMEM((3 * half, outputs), jnp.bfloat16),
                 pltpu.VMEM((2, rows, 3 * half), jnp.bfloat16),
-                pltpu.SemaphoreType.DMA((2,)),
+                pltpu.SemaphoreType.DMA((4,)),
+                pltpu.SemaphoreType.DMA((4,)),
             ],
         ),
         compiler_params=pltpu.CompilerParams(dimension_semantics=("arbitrary",)),
-    )(scalars, frame, w_mine.reshape(9 * half, outputs), w_other.reshape(9 * half, outputs),
+    )(scalars, frame, frame, w_mine.reshape(9 * half, outputs), w_other.reshape(9 * half, outputs),
       gain, shift, cur, partner, t_mine.reshape(3 * half, outputs),
       t_other.reshape(3 * half, outputs))
 

time: 27.9 us -> 27.7 us (level)
    ppermute x1, waiting for transfers between devices: 2.46 us -> 1.23 us  [body(): edge_video = lax.ppermute(frame, ('video', 'fsdp'), route)]
    ppermute x3, waiting for transfers between devices: 0.86 us -> 1.99 us  [swap_pair(): return lax.ppermute(block, 'fsdp', [(0, 1), (1, 0)])]
where the time goes in v11:
time: 27.7 us; the launch traced here: 27.5 us
  Pallas kernels  16.7 us (60%)
  starting transfers between devices  4.55 us (16%)
  waiting for transfers between devices  3.22 us (12%)
  local copies, waits for them, and re-layouts  2.37 us (9%)
  other arithmetic  0.65 us (2%)
    pallas_call x1, Pallas kernels, edge_temporal(): pl.pallas_call(kernel, out_shape=jax.ShapeDtypeStruct((rows, outputs), jn...  9.52 us
    pallas_call x1, Pallas kernels, conv_norm(): pl.pallas_call(kernel, out_shape=jax.ShapeDtypeStruct((rows, outputs), jn...  7.16 us
    ppermute x1, starting transfers between devices, body(): edge_video = lax.ppermute(frame, ('video', 'fsdp'), route)  3.5 us
    unnamed x6, local copies, waits for them, and re-layouts  2.37 us
    ppermute x3, waiting for transfers between devices, swap_pair(): return lax.ppermute(block, 'fsdp', [(0, 1), (1, 0)])  1.99 us
    ppermute x1, waiting for transfers between devices, body(): edge_video = lax.ppermute(frame, ('video', 'fsdp'), route)  1.23 us
    ppermute x3, starting transfers between devices, swap_pair(): return lax.ppermute(block, 'fsdp', [(0, 1), (1, 0)])  1.05 us
    another operation x1, other arithmetic, body(): scalars = jnp.stack([side.astype(jnp.int32), keep_edge, keep_partner])  0.65 us
  transfers between devices with their start and end apart: 4, of which 2 were waited for; matrix products, arithmetic and copies ran while one was open for 2% of the time, Pallas kernels for 26%

profile of v11, /device:TPU:17, one launch (start us, length us, event | category | flops | bytes accessed | tf_op | source)
XLA Modules:
  0.0 27.5 jit_solution(40566075894916573)
XLA Ops:
  0.0 0.7 %collective-permute-start.1 = (bf16[3,3,256,512]{3,2,1,0:T(8,128)(2,1)}, bf16[3,3,256,512]{3,2,1,0:T(8,128)(2,1)S(1)}, u32[]{:S(2)}, u32[]{:S(2)}) collective-permute-start(bf16[3,3,256,512]{3,2,1,0:T(8,128)(2,1)} %param.6), channel_id=1, source_target_pairs={{0,1},{1,0},{2,3},{3,2},{4,5},{5,4},{6,7},{7,6},{8,9},{9,8},{10,11... | collective-permute-start | bytes 7077896 | tf_op jit(solution)/shard_map/ppermute | solution.py:16
  0.7 0.0 collective-permute-start.3
  0.7 3.5 %collective-permute-start = (bf16[512,512]{1,0:T(8,128)(2,1)}, bf16[512,512]{1,0:T(8,128)(2,1)S(1)}, u32[]{:S(2)}, u32[]{:S(2)}) collective-permute-start(bf16[512,512]{1,0:T(8,128)(2,1)} %bitcast.15), channel_id=1, source_target_pairs={{1,2},{2,1},{3,4},{4,3},{5,6},{6,5},{7,8},{8,7},{9,10},{10,9},{11,... | collective-permute-start | bytes 1572872 | tf_op jit(solution)/shard_map/ppermute | solution.py:240
  4.2 2.0 %collective-permute-done.1 = bf16[3,3,256,512]{3,2,1,0:T(8,128)(2,1)S(1)} collective-permute-done((bf16[3,3,256,512]{3,2,1,0:T(8,128)(2,1)}, bf16[3,3,256,512]{3,2,1,0:T(8,128)(2,1)S(1)}, u32[]{:S(2)}, u32[]{:S(2)}) %collective-permute-start.1) | collective-permute-done | bytes 2359328 | tf_op jit(solution)/shard_map/ppermute | solution.py:16
  6.2 0.0 copy-start
  6.2 1.4 %copy-done = bf16[3,3,256,512]{3,2,1,0:T(8,128)(2,1)} copy-done((bf16[3,3,256,512]{3,2,1,0:T(8,128)(2,1)}, bf16[3,3,256,512]{3,2,1,0:T(8,128)(2,1)S(1)}, u32[]{:S(2)}) %copy-start) | copy-done | bytes 2359320
  7.6 7.2 %shard_map.55.cur_hbm = bf16[512,512]{1,0:T(8,128)(2,1)} custom-call(s32[1]{0:T(128)} %bitcast.side_ref, bf16[512,512]{1,0:T(8,128)(2,1)} %bitcast.16, bf16[512,512]{1,0:T(8,128)(2,1)} %bitcast.17, bf16[2304,512]{1,0:T(8,128)(2,1)} %bitcast.11, bf16[2304,512]{1,0:T(8,128)(2,1)} %bitcast.13, f32[1,512]{1,0:T(1,128)} %bitcast.19, f32[1,512]{1,0:T(1,128)} %bitcast.21), custom_call_target="tpu_custom_call" | custom-call | tf_op jit(solution)/shard_map/pallas_call | solution.py:87
  14.7 0.4 %collective-permute-start.2 = (bf16[512,512]{1,0:T(8,128)(2,1)}, bf16[512,512]{1,0:T(8,128)(2,1)S(1)}, u32[]{:S(2)}, u32[]{:S(2)}) collective-permute-start(bf16[512,512]{1,0:T(8,128)(2,1)} %shard_map.55.cur_hbm), channel_id=1, source_target_pairs={{0,1},{1,0},{2,3},{3,2},{4,5},{5,4},{6,7},{7,6},{8,9},{9,8},{10,11... | collective-permute-start | bytes 1572872 | tf_op jit(solution)/shard_map/ppermute | solution.py:16
  15.1 0.7 %pad_add_fusion.s_ref = s32[3]{0:T(128)} fusion(s32[1]{0:T(128)} %bitcast.2, s32[1]{0:T(128)} %bitcast.1, s32[1]{0:T(128)} %bitcast.side_ref), kind=kLoop, calls=%fused_computation | loop fusion | flops 6 | bytes 24 | tf_op jit(solution)/shard_map/stack | solution.py:253
  15.8 1.2 %collective-permute-done.xa_ref.xb_ref = bf16[512,512]{1,0:T(8,128)(2,1)S(1)} collective-permute-done((bf16[512,512]{1,0:T(8,128)(2,1)}, bf16[512,512]{1,0:T(8,128)(2,1)S(1)}, u32[]{:S(2)}, u32[]{:S(2)}) %collective-permute-start) | collective-permute-done | bytes 524320 | tf_op jit(solution)/shard_map/ppermute | solution.py:240
  17.0 0.0 copy-start.1
  17.0 0.0 collective-permute-done.3
  17.0 0.0 collective-permute-done.2.partner_hbm
  17.0 0.0 copy-start.2
  17.0 0.8 %copy-done.1 = bf16[512,512]{1,0:T(8,128)(2,1)} copy-done((bf16[512,512]{1,0:T(8,128)(2,1)}, bf16[512,512]{1,0:T(8,128)(2,1)S(1)}, u32[]{:S(2)}) %copy-start.1) | copy-done | bytes 524312
  17.8 0.2 copy-done.2
  18.0 9.5 %shard_map.56 = bf16[512,512]{1,0:T(8,128)(2,1)} custom-call(s32[3]{0:T(128)} %pad_add_fusion.s_ref, bf16[512,512]{1,0:T(8,128)(2,1)} %copy-done.1, bf16[512,512]{1,0:T(8,128)(2,1)} %copy-done.1, bf16[2304,512]{1,0:T(8,128)(2,1)} %bitcast.12, bf16[2304,512]{1,0:T(8,128)(2,1)} %bitcast.14, f32[1,512]{1,0:T(1,128)} %bitcast.20, f32[1,512]{1,0:T(1,128)} %bitcast.22, ...), custom_call_target="tpu_custom_call" | custom-call | tf_op jit(solution)/shard_map/pallas_call | solution.py:187
Async XLA Ops:
  0.0 6.2 %collective-permute-start.1 = (bf16[3,3,256,512]{3,2,1,0:T(8,128)(2,1)}, bf16[3,3,256,512]{3,2,1,0:T(8,128)(2,1)S(1)}, u32[]{:S(2)}, u32[]{:S(2)}) collective-permute-start(bf16[3,3,256,512]{3,2,1,0:T(8,128)(2,1)} %param.6), channel_id=1, source_target_pairs={{0,1},{1,0},{2,3},{3,2},{4,5},{5,4},{6,7},{7,6},{8,9},{9,8},{10,11... | collective-permute-start | bytes 7077896 | tf_op jit(solution)/shard_map/ppermute | solution.py:16
  0.7 16.3 %collective-permute-start.3 = (bf16[3,256,512]{2,1,0:T(8,128)(2,1)}, bf16[3,256,512]{2,1,0:T(8,128)(2,1)}, u32[]{:S(2)}, u32[]{:S(2)}) collective-permute-start(bf16[3,256,512]{2,1,0:T(8,128)(2,1)} %param.9), channel_id=1, source_target_pairs={{0,1},{1,0},{2,3},{3,2},{4,5},{5,4},{6,7},{7,6},{8,9},{9,8},{10,11... | collective-permute-start | bytes 2359304 | tf_op jit(solution)/shard_map/ppermute | solution.py:16
  0.7 16.3 %collective-permute-start = (bf16[512,512]{1,0:T(8,128)(2,1)}, bf16[512,512]{1,0:T(8,128)(2,1)S(1)}, u32[]{:S(2)}, u32[]{:S(2)}) collective-permute-start(bf16[512,512]{1,0:T(8,128)(2,1)} %bitcast.15), channel_id=1, source_target_pairs={{1,2},{2,1},{3,4},{4,3},{5,6},{6,5},{7,8},{8,7},{9,10},{10,9},{11,... | collective-permute-start | bytes 1572872 | tf_op jit(solution)/shard_map/ppermute | solution.py:240
  6.2 1.4 %copy-start = (bf16[3,3,256,512]{3,2,1,0:T(8,128)(2,1)}, bf16[3,3,256,512]{3,2,1,0:T(8,128)(2,1)S(1)}, u32[]{:S(2)}) copy-start(bf16[3,3,256,512]{3,2,1,0:T(8,128)(2,1)S(1)} %collective-permute-done.1) | copy-start | bytes 7077892
  14.7 2.3 %collective-permute-start.2 = (bf16[512,512]{1,0:T(8,128)(2,1)}, bf16[512,512]{1,0:T(8,128)(2,1)S(1)}, u32[]{:S(2)}, u32[]{:S(2)}) collective-permute-start(bf16[512,512]{1,0:T(8,128)(2,1)} %shard_map.55.cur_hbm), channel_id=1, source_target_pairs={{0,1},{1,0},{2,3},{3,2},{4,5},{5,4},{6,7},{7,6},{8,9},{9,8},{10,11... | collective-permute-start | bytes 1572872 | tf_op jit(solution)/shard_map/ppermute | solution.py:16
  17.0 0.8 %copy-start.1 = (bf16[512,512]{1,0:T(8,128)(2,1)}, bf16[512,512]{1,0:T(8,128)(2,1)S(1)}, u32[]{:S(2)}) copy-start(bf16[512,512]{1,0:T(8,128)(2,1)S(1)} %collective-permute-done.xa_ref.xb_ref) | copy-start | bytes 1572868
  17.0 1.0 %copy-start.2 = (bf16[512,512]{1,0:T(8,128)(2,1)}, bf16[512,512]{1,0:T(8,128)(2,1)S(1)}, u32[]{:S(2)}) copy-start(bf16[512,512]{1,0:T(8,128)(2,1)S(1)} %collective-permute-done.2.partner_hbm) | copy-start | bytes 1572868

commit v12 on v8

--- a/solution.py
+++ b/solution.py
@@ -99,14 +99,20 @@
 
 def edge_temporal_kernel(s_ref, xa_ref, xb_ref, wa_ref, wb_ref, gain_ref, shift_ref,
                          cur_hbm, partner_hbm, wtm_hbm, wto_hbm, o_ref,
-                         lhs_ref, edge_v, cur_v, partner_v, wtm_v, wto_v, tl_ref, sem,
-                         *, width, group):
+                         lhs_ref, edge_v, cur_v, partner_v, wt_v, sem, *, width, group):
+    side = s_ref[0]
+    half = wtm_hbm.shape[1]
+    edge_tap = 2 * side
+    taps = (edge_tap, 1, 2 - edge_tap)
     copies = [
-        pltpu.make_async_copy(src, dst, sem.at[i])
-        for i, (src, dst) in enumerate(
-            ((cur_hbm, cur_v), (partner_hbm, partner_v), (wtm_hbm, wtm_v), (wto_hbm, wto_v))
-        )
+        pltpu.make_async_copy(cur_hbm, cur_v, sem.at[0]),
+        pltpu.make_async_copy(partner_hbm, partner_v, sem.at[1]),
     ]
+    for slot, tap in enumerate(taps):
+        copies.append(pltpu.make_async_copy(
+            wtm_hbm.at[tap], wt_v.at[slot, pl.ds(side * half, half)], sem.at[2 + 2 * slot]))
+        copies.append(pltpu.make_async_copy(
+            wto_hbm.at[tap], wt_v.at[slot, pl.ds((1 - side) * half, half)], sem.at[3 + 2 * slot]))
     for copy in copies:
         copy.start()
     conv_norm_kernel(s_ref, xa_ref, xb_ref, wa_ref, wb_ref, gain_ref, shift_ref, edge_v,
@@ -114,28 +120,13 @@
     for copy in copies:
         copy.wait()
 
-    rows, half = xa_ref.shape
-    keep_edge = s_ref[1] != 0
-    keep_partner = s_ref[2] != 0
-    for side in range(2):
-        @pl.when(s_ref[0] == side)
-        def _fill():
-            mine = slice(side * half, (side + 1) * half)
-            other = slice((1 - side) * half, (2 - side) * half)
-            for h, cols in enumerate((mine, other)):
-                e = edge_v[:, cols]
-                p = partner_v[:, cols]
-                e = jnp.where(keep_edge, e, jnp.zeros_like(e))
-                p = jnp.where(keep_partner, p, jnp.zeros_like(p))
-                before, after = (e, p) if side == 0 else (p, e)
-                tl_ref[h, :, :half] = before
-                tl_ref[h, :, half : 2 * half] = cur_v[:, cols]
-                tl_ref[h, :, 2 * half :] = after
-
     f32 = jnp.float32
-    total = jnp.dot(tl_ref[0], wtm_v[...], preferred_element_type=f32) + jnp.dot(
-        tl_ref[1], wto_v[...], preferred_element_type=f32
-    )
+    keep_edge = s_ref[1].astype(f32)
+    keep_partner = s_ref[2].astype(f32)
+    own = jnp.dot(cur_v[...], wt_v[1], preferred_element_type=f32)
+    edge = jnp.dot(edge_v[...], wt_v[0], preferred_element_type=f32)
+    partner = jnp.dot(partner_v[...], wt_v[2], preferred_element_type=f32)
+    total = own + keep_edge * edge + keep_partner * partner
     o_ref[...] = (cur_v[...].astype(f32) + total).astype(o_ref.dtype)
 
 
@@ -173,16 +164,13 @@
                 pltpu.VMEM((rows, outputs), jnp.bfloat16),
                 pltpu.VMEM((rows, channels), jnp.bfloat16),
                 pltpu.VMEM((rows, channels), jnp.bfloat16),
-                pltpu.VMEM((3 * half, outputs), jnp.bfloat16),
-                pltpu.VMEM((3 * half, outputs), jnp.bfloat16),
-                pltpu.VMEM((2, rows, 3 * half), jnp.bfloat16),
-                pltpu.SemaphoreType.DMA((4,)),
+                pltpu.VMEM((3, channels, outputs), jnp.bfloat16),
+                pltpu.SemaphoreType.DMA((8,)),
             ],
         ),
         compiler_params=pltpu.CompilerParams(dimension_semantics=("arbitrary",)),
     )(scalars, frame, frame, w_mine.reshape(9 * half, outputs), w_other.reshape(9 * half, outputs),
-      gain, shift, cur, partner, t_mine.reshape(3 * half, outputs),
-      t_other.reshape(3 * half, outputs))
+      gain, shift, cur, partner, t_mine, t_other)
 
 
 def body(video, w_spatial, norm_gain, norm_shift, w_time):

time: 27.1 us -> 28.9 us (1.066)
  Pallas kernels: 16.1 us -> 17.2 us
  local copies, waits for them, and re-layouts: 2.37 us -> 2.99 us
    pallas_call x1, Pallas kernels: 8.89 us -> 10.1 us  [edge_temporal(): pl.pallas_call(kernel, out_shape=jax.ShapeDtypeStruct((rows, outputs), jn...]
    unnamed x6, local copies, waits for them, and re-layouts: 2.37 us -> 2.99 us
  transfers between devices with their start and end apart: 4 -> 4, of which waited for: 2 -> 2; matrix products, arithmetic and copies ran while one was open for 2% -> 2% of each run, Pallas kernels for 27% -> 25%
where the time goes in v12:
time: 28.9 us; the launch traced here: 28.7 us
  Pallas kernels  17.2 us (60%)
  starting transfers between devices  4.55 us (16%)
  waiting for transfers between devices  3.22 us (11%)
  local copies, waits for them, and re-layouts  2.99 us (10%)
  other arithmetic  0.65 us (2%)
    pallas_call x1, Pallas kernels, edge_temporal(): pl.pallas_call(kernel, out_shape=jax.ShapeDtypeStruct((rows, outputs), jn...  10.1 us
    pallas_call x1, Pallas kernels, conv_norm(): pl.pallas_call(kernel, out_shape=jax.ShapeDtypeStruct((rows, outputs), jn...  7.16 us
    ppermute x1, starting transfers between devices, body(): edge_video = lax.ppermute(frame, ('video', 'fsdp'), route)  3.5 us
    unnamed x6, local copies, waits for them, and re-layouts  2.99 us
    ppermute x3, waiting for transfers between devices, swap_pair(): return lax.ppermute(block, 'fsdp', [(0, 1), (1, 0)])  1.99 us
    ppermute x1, waiting for transfers between devices, body(): edge_video = lax.ppermute(frame, ('video', 'fsdp'), route)  1.23 us
    ppermute x3, starting transfers between devices, swap_pair(): return lax.ppermute(block, 'fsdp', [(0, 1), (1, 0)])  1.05 us
    another operation x1, other arithmetic, body(): scalars = jnp.stack([side.astype(jnp.int32), keep_edge, keep_partner])  0.65 us
  transfers between devices with their start and end apart: 4, of which 2 were waited for; matrix products, arithmetic and copies ran while one was open for 2% of the time, Pallas kernels for 25%

profile of v12, /device:TPU:17, one launch (start us, length us, event | category | flops | bytes accessed | tf_op | source)
XLA Modules:
  0.0 28.7 jit_solution(6871934673881790744)
XLA Ops:
  0.0 0.7 %collective-permute-start.1 = (bf16[3,3,256,512]{3,2,1,0:T(8,128)(2,1)}, bf16[3,3,256,512]{3,2,1,0:T(8,128)(2,1)S(1)}, u32[]{:S(2)}, u32[]{:S(2)}) collective-permute-start(bf16[3,3,256,512]{3,2,1,0:T(8,128)(2,1)} %param.6), channel_id=1, source_target_pairs={{0,1},{1,0},{2,3},{3,2},{4,5},{5,4},{6,7},{7,6},{8,9},{9,8},{10,11... | collective-permute-start | bytes 7077896 | tf_op jit(solution)/shard_map/ppermute | solution.py:16
  0.7 0.0 collective-permute-start.3
  0.7 3.5 %collective-permute-start = (bf16[512,512]{1,0:T(8,128)(2,1)}, bf16[512,512]{1,0:T(8,128)(2,1)S(1)}, u32[]{:S(2)}, u32[]{:S(2)}) collective-permute-start(bf16[512,512]{1,0:T(8,128)(2,1)} %bitcast.13), channel_id=1, source_target_pairs={{1,2},{2,1},{3,4},{4,3},{5,6},{6,5},{7,8},{8,7},{9,10},{10,9},{11,... | collective-permute-start | bytes 1572872 | tf_op jit(solution)/shard_map/ppermute | solution.py:190
  4.2 2.0 %collective-permute-done.1 = bf16[3,3,256,512]{3,2,1,0:T(8,128)(2,1)S(1)} collective-permute-done((bf16[3,3,256,512]{3,2,1,0:T(8,128)(2,1)}, bf16[3,3,256,512]{3,2,1,0:T(8,128)(2,1)S(1)}, u32[]{:S(2)}, u32[]{:S(2)}) %collective-permute-start.1) | collective-permute-done | bytes 2359328 | tf_op jit(solution)/shard_map/ppermute | solution.py:16
  6.2 0.0 copy-start
  6.2 1.4 %copy-done = bf16[3,3,256,512]{3,2,1,0:T(8,128)(2,1)} copy-done((bf16[3,3,256,512]{3,2,1,0:T(8,128)(2,1)}, bf16[3,3,256,512]{3,2,1,0:T(8,128)(2,1)S(1)}, u32[]{:S(2)}) %copy-start) | copy-done | bytes 2359320
  7.6 7.2 %shard_map.55.cur_hbm = bf16[512,512]{1,0:T(8,128)(2,1)} custom-call(s32[1]{0:T(128)} %bitcast.side_ref, bf16[512,512]{1,0:T(8,128)(2,1)} %bitcast.14, bf16[512,512]{1,0:T(8,128)(2,1)} %bitcast.15, bf16[2304,512]{1,0:T(8,128)(2,1)} %bitcast.9, bf16[2304,512]{1,0:T(8,128)(2,1)} %bitcast.11, f32[1,512]{1,0:T(1,128)} %bitcast.16, f32[1,512]{1,0:T(1,128)} %bitcast.18), custom_call_target="tpu_custom_call" | custom-call | tf_op jit(solution)/shard_map/pallas_call | solution.py:78
  14.7 0.4 %collective-permute-start.2 = (bf16[512,512]{1,0:T(8,128)(2,1)}, bf16[512,512]{1,0:T(8,128)(2,1)S(1)}, u32[]{:S(2)}, u32[]{:S(2)}) collective-permute-start(bf16[512,512]{1,0:T(8,128)(2,1)} %shard_map.55.cur_hbm), channel_id=1, source_target_pairs={{0,1},{1,0},{2,3},{3,2},{4,5},{5,4},{6,7},{7,6},{8,9},{9,8},{10,11... | collective-permute-start | bytes 1572872 | tf_op jit(solution)/shard_map/ppermute | solution.py:16
  15.1 0.7 %pad_add_fusion.s_ref = s32[3]{0:T(128)} fusion(s32[1]{0:T(128)} %bitcast.2, s32[1]{0:T(128)} %bitcast.1, s32[1]{0:T(128)} %bitcast.side_ref), kind=kLoop, calls=%fused_computation | loop fusion | flops 6 | bytes 24 | tf_op jit(solution)/shard_map/stack | solution.py:203
  15.8 1.2 %collective-permute-done.xa_ref.xb_ref = bf16[512,512]{1,0:T(8,128)(2,1)S(1)} collective-permute-done((bf16[512,512]{1,0:T(8,128)(2,1)}, bf16[512,512]{1,0:T(8,128)(2,1)S(1)}, u32[]{:S(2)}, u32[]{:S(2)}) %collective-permute-start) | collective-permute-done | bytes 524320 | tf_op jit(solution)/shard_map/ppermute | solution.py:190
  17.0 0.0 copy-start.1
  17.0 0.0 collective-permute-done.3.wto_hbm
  17.0 0.0 collective-permute-done.2.partner_hbm
  17.0 0.8 %copy-done.1 = bf16[512,512]{1,0:T(8,128)(2,1)} copy-done((bf16[512,512]{1,0:T(8,128)(2,1)}, bf16[512,512]{1,0:T(8,128)(2,1)S(1)}, u32[]{:S(2)}) %copy-start.1) | copy-done | bytes 524312
  17.8 0.0 copy-start.2
  17.8 0.8 %copy-done.2 = bf16[512,512]{1,0:T(8,128)(2,1)} copy-done((bf16[512,512]{1,0:T(8,128)(2,1)}, bf16[512,512]{1,0:T(8,128)(2,1)S(1)}, u32[]{:S(2)}) %copy-start.2) | copy-done | bytes 524312
  18.6 10.1 %shard_map.56 = bf16[512,512]{1,0:T(8,128)(2,1)} custom-call(s32[3]{0:T(128)} %pad_add_fusion.s_ref, bf16[512,512]{1,0:T(8,128)(2,1)} %copy-done.1, bf16[512,512]{1,0:T(8,128)(2,1)} %copy-done.1, bf16[2304,512]{1,0:T(8,128)(2,1)} %bitcast.10, bf16[2304,512]{1,0:T(8,128)(2,1)} %bitcast.12, f32[1,512]{1,0:T(1,128)} %bitcast.17, f32[1,512]{1,0:T(1,128)} %bitcast.19, ...), custom_call_target="tpu_custom_call" | custom-call | tf_op jit(solution)/shard_map/pallas_call | solution.py:143
Async XLA Ops:
  0.0 6.2 %collective-permute-start.1 = (bf16[3,3,256,512]{3,2,1,0:T(8,128)(2,1)}, bf16[3,3,256,512]{3,2,1,0:T(8,128)(2,1)S(1)}, u32[]{:S(2)}, u32[]{:S(2)}) collective-permute-start(bf16[3,3,256,512]{3,2,1,0:T(8,128)(2,1)} %param.6), channel_id=1, source_target_pairs={{0,1},{1,0},{2,3},{3,2},{4,5},{5,4},{6,7},{7,6},{8,9},{9,8},{10,11... | collective-permute-start | bytes 7077896 | tf_op jit(solution)/shard_map/ppermute | solution.py:16
  0.7 16.3 %collective-permute-start.3 = (bf16[3,256,512]{2,1,0:T(8,128)(2,1)}, bf16[3,256,512]{2,1,0:T(8,128)(2,1)}, u32[]{:S(2)}, u32[]{:S(2)}) collective-permute-start(bf16[3,256,512]{2,1,0:T(8,128)(2,1)} %wtm_hbm.1), channel_id=1, source_target_pairs={{0,1},{1,0},{2,3},{3,2},{4,5},{5,4},{6,7},{7,6},{8,9},{9,8},{10,11... | collective-permute-start | bytes 2359304 | tf_op jit(solution)/shard_map/ppermute | solution.py:16
  0.7 16.3 %collective-permute-start = (bf16[512,512]{1,0:T(8,128)(2,1)}, bf16[512,512]{1,0:T(8,128)(2,1)S(1)}, u32[]{:S(2)}, u32[]{:S(2)}) collective-permute-start(bf16[512,512]{1,0:T(8,128)(2,1)} %bitcast.13), channel_id=1, source_target_pairs={{1,2},{2,1},{3,4},{4,3},{5,6},{6,5},{7,8},{8,7},{9,10},{10,9},{11,... | collective-permute-start | bytes 1572872 | tf_op jit(solution)/shard_map/ppermute | solution.py:190
  6.2 1.4 %copy-start = (bf16[3,3,256,512]{3,2,1,0:T(8,128)(2,1)}, bf16[3,3,256,512]{3,2,1,0:T(8,128)(2,1)S(1)}, u32[]{:S(2)}) copy-start(bf16[3,3,256,512]{3,2,1,0:T(8,128)(2,1)S(1)} %collective-permute-done.1) | copy-start | bytes 7077892
  14.7 2.3 %collective-permute-start.2 = (bf16[512,512]{1,0:T(8,128)(2,1)}, bf16[512,512]{1,0:T(8,128)(2,1)S(1)}, u32[]{:S(2)}, u32[]{:S(2)}) collective-permute-start(bf16[512,512]{1,0:T(8,128)(2,1)} %shard_map.55.cur_hbm), channel_id=1, source_target_pairs={{0,1},{1,0},{2,3},{3,2},{4,5},{5,4},{6,7},{7,6},{8,9},{9,8},{10,11... | collective-permute-start | bytes 1572872 | tf_op jit(solution)/shard_map/ppermute | solution.py:16
  17.0 0.8 %copy-start.1 = (bf16[512,512]{1,0:T(8,128)(2,1)}, bf16[512,512]{1,0:T(8,128)(2,1)S(1)}, u32[]{:S(2)}) copy-start(bf16[512,512]{1,0:T(8,128)(2,1)S(1)} %collective-permute-done.xa_ref.xb_ref) | copy-start | bytes 1572868
  17.8 0.8 %copy-start.2 = (bf16[512,512]{1,0:T(8,128)(2,1)}, bf16[512,512]{1,0:T(8,128)(2,1)S(1)}, u32[]{:S(2)}) copy-start(bf16[512,512]{1,0:T(8,128)(2,1)S(1)} %collective-permute-done.2.partner_hbm) | copy-start | bytes 1572868

commit v13 on v8

--- a/solution.py
+++ b/solution.py
@@ -107,10 +107,10 @@
             ((cur_hbm, cur_v), (partner_hbm, partner_v), (wtm_hbm, wtm_v), (wto_hbm, wto_v))
         )
     ]
+    conv_norm_kernel(s_ref, xa_ref, xb_ref, wa_ref, wb_ref, gain_ref, shift_ref, edge_v,
+                     lhs_ref, width=width, group=group)
     for copy in copies:
         copy.start()
-    conv_norm_kernel(s_ref, xa_ref, xb_ref, wa_ref, wb_ref, gain_ref, shift_ref, edge_v,
-                     lhs_ref, width=width, group=group)
     for copy in copies:
         copy.wait()
 

time: 27.1 us -> 27.1 us (level)
  no operation moved by 1% of the time
where the time goes in v13:
time: 27.1 us; the launch traced here: 26.9 us
  Pallas kernels  16.1 us (59%)
  starting transfers between devices  4.55 us (17%)
  waiting for transfers between devices  3.22 us (12%)
  local copies, waits for them, and re-layouts  2.37 us (9%)
  other arithmetic  0.65 us (2%)
    pallas_call x1, Pallas kernels, edge_temporal(): pl.pallas_call(kernel, out_shape=jax.ShapeDtypeStruct((rows, outputs), jn...  8.89 us
    pallas_call x1, Pallas kernels, conv_norm(): pl.pallas_call(kernel, out_shape=jax.ShapeDtypeStruct((rows, outputs), jn...  7.16 us
    ppermute x1, starting transfers between devices, body(): edge_video = lax.ppermute(frame, ('video', 'fsdp'), route)  3.5 us
    unnamed x6, local copies, waits for them, and re-layouts  2.37 us
    ppermute x3, waiting for transfers between devices, swap_pair(): return lax.ppermute(block, 'fsdp', [(0, 1), (1, 0)])  1.99 us
    ppermute x1, waiting for transfers between devices, body(): edge_video = lax.ppermute(frame, ('video', 'fsdp'), route)  1.23 us
    ppermute x3, starting transfers between devices, swap_pair(): return lax.ppermute(block, 'fsdp', [(0, 1), (1, 0)])  1.05 us
    another operation x1, other arithmetic, body(): scalars = jnp.stack([side.astype(jnp.int32), keep_edge, keep_partner])  0.65 us
  transfers between devices with their start and end apart: 4, of which 2 were waited for; matrix products, arithmetic and copies ran while one was open for 2% of the time, Pallas kernels for 27%

profile of v13, /device:TPU:17, one launch (start us, length us, event | category | flops | bytes accessed | tf_op | source)
XLA Modules:
  0.0 26.9 jit_solution(16662084798224346720)
XLA Ops:
  0.0 0.7 %collective-permute-start.1 = (bf16[3,3,256,512]{3,2,1,0:T(8,128)(2,1)}, bf16[3,3,256,512]{3,2,1,0:T(8,128)(2,1)S(1)}, u32[]{:S(2)}, u32[]{:S(2)}) collective-permute-start(bf16[3,3,256,512]{3,2,1,0:T(8,128)(2,1)} %param.6), channel_id=1, source_target_pairs={{0,1},{1,0},{2,3},{3,2},{4,5},{5,4},{6,7},{7,6},{8,9},{9,8},{10,11... | collective-permute-start | bytes 7077896 | tf_op jit(solution)/shard_map/ppermute | solution.py:16
  0.7 0.0 collective-permute-start.3
  0.7 3.5 %collective-permute-start = (bf16[512,512]{1,0:T(8,128)(2,1)}, bf16[512,512]{1,0:T(8,128)(2,1)S(1)}, u32[]{:S(2)}, u32[]{:S(2)}) collective-permute-start(bf16[512,512]{1,0:T(8,128)(2,1)} %bitcast.15), channel_id=1, source_target_pairs={{1,2},{2,1},{3,4},{4,3},{5,6},{6,5},{7,8},{8,7},{9,10},{10,9},{11,... | collective-permute-start | bytes 1572872 | tf_op jit(solution)/shard_map/ppermute | solution.py:202
  4.2 2.0 %collective-permute-done.1 = bf16[3,3,256,512]{3,2,1,0:T(8,128)(2,1)S(1)} collective-permute-done((bf16[3,3,256,512]{3,2,1,0:T(8,128)(2,1)}, bf16[3,3,256,512]{3,2,1,0:T(8,128)(2,1)S(1)}, u32[]{:S(2)}, u32[]{:S(2)}) %collective-permute-start.1) | collective-permute-done | bytes 2359328 | tf_op jit(solution)/shard_map/ppermute | solution.py:16
  6.2 0.0 copy-start
  6.2 1.4 %copy-done = bf16[3,3,256,512]{3,2,1,0:T(8,128)(2,1)} copy-done((bf16[3,3,256,512]{3,2,1,0:T(8,128)(2,1)}, bf16[3,3,256,512]{3,2,1,0:T(8,128)(2,1)S(1)}, u32[]{:S(2)}) %copy-start) | copy-done | bytes 2359320
  7.6 7.2 %shard_map.55.cur_hbm = bf16[512,512]{1,0:T(8,128)(2,1)} custom-call(s32[1]{0:T(128)} %bitcast.side_ref, bf16[512,512]{1,0:T(8,128)(2,1)} %bitcast.16, bf16[512,512]{1,0:T(8,128)(2,1)} %bitcast.17, bf16[2304,512]{1,0:T(8,128)(2,1)} %bitcast.11, bf16[2304,512]{1,0:T(8,128)(2,1)} %bitcast.13, f32[1,512]{1,0:T(1,128)} %bitcast.19, f32[1,512]{1,0:T(1,128)} %bitcast.21), custom_call_target="tpu_custom_call" | custom-call | tf_op jit(solution)/shard_map/pallas_call | solution.py:78
  14.7 0.4 %collective-permute-start.2 = (bf16[512,512]{1,0:T(8,128)(2,1)}, bf16[512,512]{1,0:T(8,128)(2,1)S(1)}, u32[]{:S(2)}, u32[]{:S(2)}) collective-permute-start(bf16[512,512]{1,0:T(8,128)(2,1)} %shard_map.55.cur_hbm), channel_id=1, source_target_pairs={{0,1},{1,0},{2,3},{3,2},{4,5},{5,4},{6,7},{7,6},{8,9},{9,8},{10,11... | collective-permute-start | bytes 1572872 | tf_op jit(solution)/shard_map/ppermute | solution.py:16
  15.1 0.7 %pad_add_fusion.s_ref = s32[3]{0:T(128)} fusion(s32[1]{0:T(128)} %bitcast.2, s32[1]{0:T(128)} %bitcast.1, s32[1]{0:T(128)} %bitcast.side_ref), kind=kLoop, calls=%fused_computation | loop fusion | flops 6 | bytes 24 | tf_op jit(solution)/shard_map/stack | solution.py:215
  15.8 1.2 %collective-permute-done.xa_ref.xb_ref = bf16[512,512]{1,0:T(8,128)(2,1)S(1)} collective-permute-done((bf16[512,512]{1,0:T(8,128)(2,1)}, bf16[512,512]{1,0:T(8,128)(2,1)S(1)}, u32[]{:S(2)}, u32[]{:S(2)}) %collective-permute-start) | collective-permute-done | bytes 524320 | tf_op jit(solution)/shard_map/ppermute | solution.py:202
  17.0 0.0 copy-start.1
  17.0 0.0 collective-permute-done.3
  17.0 0.0 collective-permute-done.2.partner_hbm
  17.0 0.0 copy-start.2
  17.0 0.8 %copy-done.1 = bf16[512,512]{1,0:T(8,128)(2,1)} copy-done((bf16[512,512]{1,0:T(8,128)(2,1)}, bf16[512,512]{1,0:T(8,128)(2,1)S(1)}, u32[]{:S(2)}) %copy-start.1) | copy-done | bytes 524312
  17.8 0.2 copy-done.2
  18.0 8.9 %shard_map.56 = bf16[512,512]{1,0:T(8,128)(2,1)} custom-call(s32[3]{0:T(128)} %pad_add_fusion.s_ref, bf16[512,512]{1,0:T(8,128)(2,1)} %copy-done.1, bf16[512,512]{1,0:T(8,128)(2,1)} %copy-done.1, bf16[2304,512]{1,0:T(8,128)(2,1)} %bitcast.12, bf16[2304,512]{1,0:T(8,128)(2,1)} %bitcast.14, f32[1,512]{1,0:T(1,128)} %bitcast.20, f32[1,512]{1,0:T(1,128)} %bitcast.22, ...), custom_call_target="tpu_custom_call" | custom-call | tf_op jit(solution)/shard_map/pallas_call | solution.py:152
Async XLA Ops:
  0.0 6.2 %collective-permute-start.1 = (bf16[3,3,256,512]{3,2,1,0:T(8,128)(2,1)}, bf16[3,3,256,512]{3,2,1,0:T(8,128)(2,1)S(1)}, u32[]{:S(2)}, u32[]{:S(2)}) collective-permute-start(bf16[3,3,256,512]{3,2,1,0:T(8,128)(2,1)} %param.6), channel_id=1, source_target_pairs={{0,1},{1,0},{2,3},{3,2},{4,5},{5,4},{6,7},{7,6},{8,9},{9,8},{10,11... | collective-permute-start | bytes 7077896 | tf_op jit(solution)/shard_map/ppermute | solution.py:16
  0.7 16.3 %collective-permute-start.3 = (bf16[3,256,512]{2,1,0:T(8,128)(2,1)}, bf16[3,256,512]{2,1,0:T(8,128)(2,1)}, u32[]{:S(2)}, u32[]{:S(2)}) collective-permute-start(bf16[3,256,512]{2,1,0:T(8,128)(2,1)} %param.9), channel_id=1, source_target_pairs={{0,1},{1,0},{2,3},{3,2},{4,5},{5,4},{6,7},{7,6},{8,9},{9,8},{10,11... | collective-permute-start | bytes 2359304 | tf_op jit(solution)/shard_map/ppermute | solution.py:16
  0.7 16.3 %collective-permute-start = (bf16[512,512]{1,0:T(8,128)(2,1)}, bf16[512,512]{1,0:T(8,128)(2,1)S(1)}, u32[]{:S(2)}, u32[]{:S(2)}) collective-permute-start(bf16[512,512]{1,0:T(8,128)(2,1)} %bitcast.15), channel_id=1, source_target_pairs={{1,2},{2,1},{3,4},{4,3},{5,6},{6,5},{7,8},{8,7},{9,10},{10,9},{11,... | collective-permute-start | bytes 1572872 | tf_op jit(solution)/shard_map/ppermute | solution.py:202
  6.2 1.4 %copy-start = (bf16[3,3,256,512]{3,2,1,0:T(8,128)(2,1)}, bf16[3,3,256,512]{3,2,1,0:T(8,128)(2,1)S(1)}, u32[]{:S(2)}) copy-start(bf16[3,3,256,512]{3,2,1,0:T(8,128)(2,1)S(1)} %collective-permute-done.1) | copy-start | bytes 7077892
  14.7 2.3 %collective-permute-start.2 = (bf16[512,512]{1,0:T(8,128)(2,1)}, bf16[512,512]{1,0:T(8,128)(2,1)S(1)}, u32[]{:S(2)}, u32[]{:S(2)}) collective-permute-start(bf16[512,512]{1,0:T(8,128)(2,1)} %shard_map.55.cur_hbm), channel_id=1, source_target_pairs={{0,1},{1,0},{2,3},{3,2},{4,5},{5,4},{6,7},{7,6},{8,9},{9,8},{10,11... | collective-permute-start | bytes 1572872 | tf_op jit(solution)/shard_map/ppermute | solution.py:16
  17.0 0.8 %copy-start.1 = (bf16[512,512]{1,0:T(8,128)(2,1)}, bf16[512,512]{1,0:T(8,128)(2,1)S(1)}, u32[]{:S(2)}) copy-start(bf16[512,512]{1,0:T(8,128)(2,1)S(1)} %collective-permute-done.xa_ref.xb_ref) | copy-start | bytes 1572868
  17.0 1.0 %copy-start.2 = (bf16[512,512]{1,0:T(8,128)(2,1)}, bf16[512,512]{1,0:T(8,128)(2,1)S(1)}, u32[]{:S(2)}) copy-start(bf16[512,512]{1,0:T(8,128)(2,1)S(1)} %collective-permute-done.2.partner_hbm) | copy-start | bytes 1572868

commit v14 on v8

--- a/solution.py
+++ b/solution.py
@@ -73,7 +73,7 @@
     group = outputs // GROUPS
     block = outputs // split
     kernel = functools.partial(conv_norm_kernel, width=width, group=group)
-    weight_block = pl.BlockSpec((9 * half, block), lambda n, s: (0, n))
+    weight_block = pl.BlockSpec(memory_space=pltpu.VMEM)
     row_block = pl.BlockSpec((1, block), lambda n, s: (0, n))
     return pl.pallas_call(
         kernel,
@@ -146,7 +146,7 @@
     outputs = w_mine.shape[3]
     group = outputs // GROUPS
     kernel = functools.partial(edge_temporal_kernel, width=width, group=group)
-    weight_block = pl.BlockSpec((9 * half, outputs), lambda n, s: (0, 0))
+    weight_block = pl.BlockSpec(memory_space=pltpu.VMEM)
     row_block = pl.BlockSpec((1, outputs), lambda n, s: (0, 0))
     anywhere = pl.BlockSpec(memory_space=pl.ANY)
     return pl.pallas_call(

time: 27.1 us -> 27.1 us (level)
  no operation moved by 1% of the time
where the time goes in v14:
time: 27.1 us; the launch traced here: 26.9 us
  Pallas kernels  16.1 us (59%)
  starting transfers between devices  4.55 us (17%)
  waiting for transfers between devices  3.22 us (12%)
  local copies, waits for them, and re-layouts  2.37 us (9%)
  other arithmetic  0.65 us (2%)
    pallas_call x1, Pallas kernels, edge_temporal(): pl.pallas_call(kernel, out_shape=jax.ShapeDtypeStruct((rows, outputs), jn...  8.89 us
    pallas_call x1, Pallas kernels, conv_norm(): pl.pallas_call(kernel, out_shape=jax.ShapeDtypeStruct((rows, outputs), jn...  7.16 us
    ppermute x1, starting transfers between devices, body(): edge_video = lax.ppermute(frame, ('video', 'fsdp'), route)  3.5 us
    unnamed x6, local copies, waits for them, and re-layouts  2.37 us
    ppermute x3, waiting for transfers between devices, swap_pair(): return lax.ppermute(block, 'fsdp', [(0, 1), (1, 0)])  1.99 us
    ppermute x1, waiting for transfers between devices, body(): edge_video = lax.ppermute(frame, ('video', 'fsdp'), route)  1.23 us
    ppermute x3, starting transfers between devices, swap_pair(): return lax.ppermute(block, 'fsdp', [(0, 1), (1, 0)])  1.05 us
    another operation x1, other arithmetic, body(): scalars = jnp.stack([side.astype(jnp.int32), keep_edge, keep_partner])  0.65 us
  transfers between devices with their start and end apart: 4, of which 2 were waited for; matrix products, arithmetic and copies ran while one was open for 2% of the time, Pallas kernels for 27%

profile of v14, /device:TPU:17, one launch (start us, length us, event | category | flops | bytes accessed | tf_op | source)
XLA Modules:
  0.0 26.9 jit_solution(16662084798224346720)
XLA Ops:
  0.0 0.7 %collective-permute-start.1 = (bf16[3,3,256,512]{3,2,1,0:T(8,128)(2,1)}, bf16[3,3,256,512]{3,2,1,0:T(8,128)(2,1)S(1)}, u32[]{:S(2)}, u32[]{:S(2)}) collective-permute-start(bf16[3,3,256,512]{3,2,1,0:T(8,128)(2,1)} %param.6), channel_id=1, source_target_pairs={{0,1},{1,0},{2,3},{3,2},{4,5},{5,4},{6,7},{7,6},{8,9},{9,8},{10,11... | collective-permute-start | bytes 7077896 | tf_op jit(solution)/shard_map/ppermute | solution.py:16
  0.7 0.0 collective-permute-start.3
  0.7 3.5 %collective-permute-start = (bf16[512,512]{1,0:T(8,128)(2,1)}, bf16[512,512]{1,0:T(8,128)(2,1)S(1)}, u32[]{:S(2)}, u32[]{:S(2)}) collective-permute-start(bf16[512,512]{1,0:T(8,128)(2,1)} %bitcast.15), channel_id=1, source_target_pairs={{1,2},{2,1},{3,4},{4,3},{5,6},{6,5},{7,8},{8,7},{9,10},{10,9},{11,... | collective-permute-start | bytes 1572872 | tf_op jit(solution)/shard_map/ppermute | solution.py:202
  4.2 2.0 %collective-permute-done.1 = bf16[3,3,256,512]{3,2,1,0:T(8,128)(2,1)S(1)} collective-permute-done((bf16[3,3,256,512]{3,2,1,0:T(8,128)(2,1)}, bf16[3,3,256,512]{3,2,1,0:T(8,128)(2,1)S(1)}, u32[]{:S(2)}, u32[]{:S(2)}) %collective-permute-start.1) | collective-permute-done | bytes 2359328 | tf_op jit(solution)/shard_map/ppermute | solution.py:16
  6.2 0.0 copy-start
  6.2 1.4 %copy-done = bf16[3,3,256,512]{3,2,1,0:T(8,128)(2,1)} copy-done((bf16[3,3,256,512]{3,2,1,0:T(8,128)(2,1)}, bf16[3,3,256,512]{3,2,1,0:T(8,128)(2,1)S(1)}, u32[]{:S(2)}) %copy-start) | copy-done | bytes 2359320
  7.6 7.2 %shard_map.55.cur_hbm = bf16[512,512]{1,0:T(8,128)(2,1)} custom-call(s32[1]{0:T(128)} %bitcast.side_ref, bf16[512,512]{1,0:T(8,128)(2,1)} %bitcast.16, bf16[512,512]{1,0:T(8,128)(2,1)} %bitcast.17, bf16[2304,512]{1,0:T(8,128)(2,1)} %bitcast.11, bf16[2304,512]{1,0:T(8,128)(2,1)} %bitcast.13, f32[1,512]{1,0:T(1,128)} %bitcast.19, f32[1,512]{1,0:T(1,128)} %bitcast.21), custom_call_target="tpu_custom_call" | custom-call | tf_op jit(solution)/shard_map/pallas_call | solution.py:78
  14.7 0.4 %collective-permute-start.2 = (bf16[512,512]{1,0:T(8,128)(2,1)}, bf16[512,512]{1,0:T(8,128)(2,1)S(1)}, u32[]{:S(2)}, u32[]{:S(2)}) collective-permute-start(bf16[512,512]{1,0:T(8,128)(2,1)} %shard_map.55.cur_hbm), channel_id=1, source_target_pairs={{0,1},{1,0},{2,3},{3,2},{4,5},{5,4},{6,7},{7,6},{8,9},{9,8},{10,11... | collective-permute-start | bytes 1572872 | tf_op jit(solution)/shard_map/ppermute | solution.py:16
  15.1 0.7 %pad_add_fusion.s_ref = s32[3]{0:T(128)} fusion(s32[1]{0:T(128)} %bitcast.2, s32[1]{0:T(128)} %bitcast.1, s32[1]{0:T(128)} %bitcast.side_ref), kind=kLoop, calls=%fused_computation | loop fusion | flops 6 | bytes 24 | tf_op jit(solution)/shard_map/stack | solution.py:215
  15.8 1.2 %collective-permute-done.xa_ref.xb_ref = bf16[512,512]{1,0:T(8,128)(2,1)S(1)} collective-permute-done((bf16[512,512]{1,0:T(8,128)(2,1)}, bf16[512,512]{1,0:T(8,128)(2,1)S(1)}, u32[]{:S(2)}, u32[]{:S(2)}) %collective-permute-start) | collective-permute-done | bytes 524320 | tf_op jit(solution)/shard_map/ppermute | solution.py:202
  17.0 0.0 copy-start.1
  17.0 0.0 collective-permute-done.3
  17.0 0.0 collective-permute-done.2.partner_hbm
  17.0 0.0 copy-start.2
  17.0 0.8 %copy-done.1 = bf16[512,512]{1,0:T(8,128)(2,1)} copy-done((bf16[512,512]{1,0:T(8,128)(2,1)}, bf16[512,512]{1,0:T(8,128)(2,1)S(1)}, u32[]{:S(2)}) %copy-start.1) | copy-done | bytes 524312
  17.8 0.2 copy-done.2
  18.0 8.9 %shard_map.56 = bf16[512,512]{1,0:T(8,128)(2,1)} custom-call(s32[3]{0:T(128)} %pad_add_fusion.s_ref, bf16[512,512]{1,0:T(8,128)(2,1)} %copy-done.1, bf16[512,512]{1,0:T(8,128)(2,1)} %copy-done.1, bf16[2304,512]{1,0:T(8,128)(2,1)} %bitcast.12, bf16[2304,512]{1,0:T(8,128)(2,1)} %bitcast.14, f32[1,512]{1,0:T(1,128)} %bitcast.20, f32[1,512]{1,0:T(1,128)} %bitcast.22, ...), custom_call_target="tpu_custom_call" | custom-call | tf_op jit(solution)/shard_map/pallas_call | solution.py:152
Async XLA Ops:
  0.0 6.2 %collective-permute-start.1 = (bf16[3,3,256,512]{3,2,1,0:T(8,128)(2,1)}, bf16[3,3,256,512]{3,2,1,0:T(8,128)(2,1)S(1)}, u32[]{:S(2)}, u32[]{:S(2)}) collective-permute-start(bf16[3,3,256,512]{3,2,1,0:T(8,128)(2,1)} %param.6), channel_id=1, source_target_pairs={{0,1},{1,0},{2,3},{3,2},{4,5},{5,4},{6,7},{7,6},{8,9},{9,8},{10,11... | collective-permute-start | bytes 7077896 | tf_op jit(solution)/shard_map/ppermute | solution.py:16
  0.7 16.3 %collective-permute-start.3 = (bf16[3,256,512]{2,1,0:T(8,128)(2,1)}, bf16[3,256,512]{2,1,0:T(8,128)(2,1)}, u32[]{:S(2)}, u32[]{:S(2)}) collective-permute-start(bf16[3,256,512]{2,1,0:T(8,128)(2,1)} %param.9), channel_id=1, source_target_pairs={{0,1},{1,0},{2,3},{3,2},{4,5},{5,4},{6,7},{7,6},{8,9},{9,8},{10,11... | collective-permute-start | bytes 2359304 | tf_op jit(solution)/shard_map/ppermute | solution.py:16
  0.7 16.3 %collective-permute-start = (bf16[512,512]{1,0:T(8,128)(2,1)}, bf16[512,512]{1,0:T(8,128)(2,1)S(1)}, u32[]{:S(2)}, u32[]{:S(2)}) collective-permute-start(bf16[512,512]{1,0:T(8,128)(2,1)} %bitcast.15), channel_id=1, source_target_pairs={{1,2},{2,1},{3,4},{4,3},{5,6},{6,5},{7,8},{8,7},{9,10},{10,9},{11,... | collective-permute-start | bytes 1572872 | tf_op jit(solution)/shard_map/ppermute | solution.py:202
  6.2 1.4 %copy-start = (bf16[3,3,256,512]{3,2,1,0:T(8,128)(2,1)}, bf16[3,3,256,512]{3,2,1,0:T(8,128)(2,1)S(1)}, u32[]{:S(2)}) copy-start(bf16[3,3,256,512]{3,2,1,0:T(8,128)(2,1)S(1)} %collective-permute-done.1) | copy-start | bytes 7077892
  14.7 2.3 %collective-permute-start.2 = (bf16[512,512]{1,0:T(8,128)(2,1)}, bf16[512,512]{1,0:T(8,128)(2,1)S(1)}, u32[]{:S(2)}, u32[]{:S(2)}) collective-permute-start(bf16[512,512]{1,0:T(8,128)(2,1)} %shard_map.55.cur_hbm), channel_id=1, source_target_pairs={{0,1},{1,0},{2,3},{3,2},{4,5},{5,4},{6,7},{7,6},{8,9},{9,8},{10,11... | collective-permute-start | bytes 1572872 | tf_op jit(solution)/shard_map/ppermute | solution.py:16
  17.0 0.8 %copy-start.1 = (bf16[512,512]{1,0:T(8,128)(2,1)}, bf16[512,512]{1,0:T(8,128)(2,1)S(1)}, u32[]{:S(2)}) copy-start(bf16[512,512]{1,0:T(8,128)(2,1)S(1)} %collective-permute-done.xa_ref.xb_ref) | copy-start | bytes 1572868
  17.0 1.0 %copy-start.2 = (bf16[512,512]{1,0:T(8,128)(2,1)}, bf16[512,512]{1,0:T(8,128)(2,1)S(1)}, u32[]{:S(2)}) copy-start(bf16[512,512]{1,0:T(8,128)(2,1)S(1)} %collective-permute-done.2.partner_hbm) | copy-start | bytes 1572868

commit v15 on v9

--- a/solution.py
+++ b/solution.py
@@ -50,6 +50,12 @@
                     lhs_ref[h, rows - width :, cols] = zeros
 
 
+def own_conv_kernel(side_ref, xa_ref, xb_ref, wa_ref, wb_ref, gain_ref, shift_ref, later_hbm,
+                    o_ref, lhs_ref, *, width, group):
+    conv_norm_kernel(side_ref, xa_ref, xb_ref, wa_ref, wb_ref, gain_ref, shift_ref, o_ref,
+                     lhs_ref, width=width, group=group)
+
+
 def conv_norm_kernel(side_ref, xa_ref, xb_ref, wa_ref, wb_ref, gain_ref, shift_ref, o_ref,
                      lhs_ref, *, width, group):
     build_lhs(((0, xa_ref[...]), (1, xb_ref[...])), lhs_ref, width)
@@ -71,13 +77,13 @@
     o_ref[...] = (v / (1.0 + jnp.exp(-v))).astype(o_ref.dtype)
 
 
-def conv_norm(frame, w_mine, w_other, gain, shift, side, width, split=1):
+def conv_norm(frame, w_mine, w_other, gain, shift, side, width, later, split=1):
     rows, channels = frame.shape
     half = w_mine.shape[2]
     outputs = w_mine.shape[3]
     group = outputs // GROUPS
     block = outputs // split
-    kernel = functools.partial(conv_norm_kernel, width=width, group=group)
+    kernel = functools.partial(own_conv_kernel, width=width, group=group)
     weight_block = pl.BlockSpec((9 * half, block), lambda n, s: (0, n))
     row_block = pl.BlockSpec((1, block), lambda n, s: (0, n))
     return pl.pallas_call(
@@ -93,23 +99,24 @@
                 weight_block,
                 row_block,
                 row_block,
+                pl.BlockSpec(memory_space=pl.ANY),
             ],
             out_specs=pl.BlockSpec((rows, block), lambda n, s: (0, n)),
             scratch_shapes=[pltpu.VMEM((2, rows, 9 * half), jnp.bfloat16)],
         ),
         compiler_params=pltpu.CompilerParams(dimension_semantics=("arbitrary",)),
     )(side, frame, frame, w_mine.reshape(9 * half, outputs), w_other.reshape(9 * half, outputs),
-      gain, shift)
+      gain, shift, later)
 
 
 def edge_temporal_kernel(s_ref, x_ref, wa_ref, wb_ref, gain_ref, shift_ref,
-                         cur_hbm, partner_v, wtm_hbm, wto_v, o_ref,
-                         lhs_ref, edge_v, cur_v, wtm_v, tl_ref, sem,
+                         cur_hbm, partner_hbm, wtm_hbm, wto_hbm, o_ref,
+                         lhs_ref, edge_v, cur_v, partner_v, wtm_v, wto_v, tl_ref, sem,
                          *, width, group):
     copies = [
         pltpu.make_async_copy(src, dst, sem.at[i])
         for i, (src, dst) in enumerate(
-            ((cur_hbm, cur_v), (wtm_hbm, wtm_v))
+            ((cur_hbm, cur_v), (partner_hbm, partner_v), (wtm_hbm, wtm_v), (wto_hbm, wto_v))
         )
     ]
     for copy in copies:
@@ -171,18 +178,20 @@
                 row_block,
                 row_block,
                 anywhere,
-                in_vmem,
-                anywhere,
-                in_vmem,
+                anywhere,
+                anywhere,
+                anywhere,
             ],
             out_specs=pl.BlockSpec((rows, outputs), lambda n, s: (0, 0)),
             scratch_shapes=[
                 pltpu.VMEM((2, rows, 9 * half), jnp.bfloat16),
                 pltpu.VMEM((rows, outputs), jnp.bfloat16),
                 pltpu.VMEM((rows, channels), jnp.bfloat16),
+                pltpu.VMEM((rows, channels), jnp.bfloat16),
+                pltpu.VMEM((3 * half, outputs), jnp.bfloat16),
                 pltpu.VMEM((3 * half, outputs), jnp.bfloat16),
                 pltpu.VMEM((2, rows, 3 * half), jnp.bfloat16),
-                pltpu.SemaphoreType.DMA((2,)),
+                pltpu.SemaphoreType.DMA((4,)),
             ],
         ),
         compiler_params=pltpu.CompilerParams(dimension_semantics=("arbitrary",)),
@@ -212,7 +221,7 @@
     gain = norm_gain.reshape(1, channels)
     shift = norm_shift.reshape(1, channels)
     sides = side.reshape(1).astype(jnp.int32)
-    hidden = conv_norm(frame, w_spatial, other_spatial, gain, shift, sides, width)
+    hidden = conv_norm(frame, w_spatial, other_spatial, gain, shift, sides, width, other_time)
     partner = swap_pair(hidden)
     keep_prev = (position % CLIP != 0).astype(jnp.int32)
     keep_next = (position % CLIP != CLIP - 1).astype(jnp.int32)

time: 27.9 us -> 27.3 us (0.978)
  Pallas kernels: 16.7 us -> 16.4 us
    ppermute x1, waiting for transfers between devices: 2.46 us -> 1.08 us  [body(): edge_video = lax.ppermute(frame, ('video', 'fsdp'), route)]
    ppermute x3, waiting for transfers between devices: 0.86 us -> 2 us  [swap_pair(): return lax.ppermute(block, 'fsdp', [(0, 1), (1, 0)])]
    pallas_call x1, Pallas kernels: 9.52 us -> 9.22 us  [edge_temporal(): pl.pallas_call(kernel, out_shape=jax.ShapeDtypeStruct((rows, outputs), jn...]
where the time goes in v15:
time: 27.3 us; the launch traced here: 27.1 us
  Pallas kernels  16.4 us (60%)
  starting transfers between devices  4.56 us (17%)
  waiting for transfers between devices  3.08 us (11%)
  local copies, waits for them, and re-layouts  2.45 us (9%)
  other arithmetic  0.65 us (2%)
    pallas_call x1, Pallas kernels, edge_temporal(): pl.pallas_call(kernel, out_shape=jax.ShapeDtypeStruct((rows, outputs), jn...  9.22 us
    pallas_call x1, Pallas kernels, conv_norm(): pl.pallas_call(kernel, out_shape=jax.ShapeDtypeStruct((rows, outputs), jn...  7.15 us
    ppermute x1, starting transfers between devices, body(): edge_video = lax.ppermute(frame, ('video', 'fsdp'), route)  3.5 us
    unnamed x6, local copies, waits for them, and re-layouts  2.45 us
    ppermute x3, waiting for transfers between devices, swap_pair(): return lax.ppermute(block, 'fsdp', [(0, 1), (1, 0)])  2 us
    ppermute x1, waiting for transfers between devices, body(): edge_video = lax.ppermute(frame, ('video', 'fsdp'), route)  1.08 us
    ppermute x3, starting transfers between devices, swap_pair(): return lax.ppermute(block, 'fsdp', [(0, 1), (1, 0)])  1.06 us
    another operation x1, other arithmetic, body(): scalars = jnp.stack([side.astype(jnp.int32), keep_edge, keep_partner])  0.65 us
  transfers between devices with their start and end apart: 4, of which 2 were waited for; matrix products, arithmetic and copies ran while one was open for 2% of the time, Pallas kernels for 26%

profile of v15, /device:TPU:17, one launch (start us, length us, event | category | flops | bytes accessed | tf_op | source)
XLA Modules:
  0.0 27.1 jit_solution(10483525647535352861)
XLA Ops:
  0.0 0.7 %collective-permute-start.1 = (bf16[3,3,256,512]{3,2,1,0:T(8,128)(2,1)}, bf16[3,3,256,512]{3,2,1,0:T(8,128)(2,1)S(1)}, u32[]{:S(2)}, u32[]{:S(2)}) collective-permute-start(bf16[3,3,256,512]{3,2,1,0:T(8,128)(2,1)} %param.6), channel_id=1, source_target_pairs={{0,1},{1,0},{2,3},{3,2},{4,5},{5,4},{6,7},{7,6},{8,9},{9,8},{10,11... | collective-permute-start | bytes 7077896 | tf_op jit(solution)/shard_map/ppermute | solution.py:16
  0.7 0.0 collective-permute-start.2
  0.7 3.5 %collective-permute-start = (bf16[512,512]{1,0:T(8,128)(2,1)}, bf16[512,512]{1,0:T(8,128)(2,1)}, u32[]{:S(2)}, u32[]{:S(2)}) collective-permute-start(bf16[512,512]{1,0:T(8,128)(2,1)} %bitcast.16), channel_id=1, source_target_pairs={{1,2},{2,1},{3,4},{4,3},{5,6},{6,5},{7,8},{8,7},{9,10},{10,9},{11,... | collective-permute-start | bytes 1572872 | tf_op jit(solution)/shard_map/ppermute | solution.py:217
  4.2 2.0 %collective-permute-done.2.later_hbm = bf16[3,256,512]{2,1,0:T(8,128)(2,1)S(1)} collective-permute-done((bf16[3,256,512]{2,1,0:T(8,128)(2,1)}, bf16[3,256,512]{2,1,0:T(8,128)(2,1)S(1)}, u32[]{:S(2)}, u32[]{:S(2)}) %collective-permute-start.2) | collective-permute-done | bytes 786464 | tf_op jit(solution)/shard_map/ppermute | solution.py:16
  6.2 0.0 copy-start.1
  6.2 0.0 collective-permute-done.1
  6.2 0.0 copy-start
  6.2 0.9 %copy-done.1 = bf16[3,256,512]{2,1,0:T(8,128)(2,1)} copy-done((bf16[3,256,512]{2,1,0:T(8,128)(2,1)}, bf16[3,256,512]{2,1,0:T(8,128)(2,1)S(1)}, u32[]{:S(2)}) %copy-start.1) | copy-done | bytes 786456
  7.1 0.8 %copy-done = bf16[3,3,256,512]{3,2,1,0:T(8,128)(2,1)} copy-done((bf16[3,3,256,512]{3,2,1,0:T(8,128)(2,1)}, bf16[3,3,256,512]{3,2,1,0:T(8,128)(2,1)S(1)}, u32[]{:S(2)}) %copy-start) | copy-done | bytes 2359320
  7.8 7.2 %shard_map.55.cur_hbm = bf16[512,512]{1,0:T(8,128)(2,1)} custom-call(s32[1]{0:T(128)} %bitcast.side_ref, bf16[512,512]{1,0:T(8,128)(2,1)} %bitcast.17, bf16[512,512]{1,0:T(8,128)(2,1)} %bitcast.18, bf16[2304,512]{1,0:T(8,128)(2,1)} %bitcast.11, bf16[2304,512]{1,0:T(8,128)(2,1)} %bitcast.13, f32[1,512]{1,0:T(1,128)} %bitcast.20, f32[1,512]{1,0:T(1,128)} %bitcast.22, ...), custom_call_target="tpu_custom_call" | custom-call | tf_op jit(solution)/shard_map/pallas_call | solution.py:89
  15.0 0.4 %collective-permute-start.3 = (bf16[512,512]{1,0:T(8,128)(2,1)}, bf16[512,512]{1,0:T(8,128)(2,1)S(1)}, u32[]{:S(2)}, u32[]{:S(2)}) collective-permute-start(bf16[512,512]{1,0:T(8,128)(2,1)} %shard_map.55.cur_hbm), channel_id=1, source_target_pairs={{0,1},{1,0},{2,3},{3,2},{4,5},{5,4},{6,7},{7,6},{8,9},{9,8},{10,11... | collective-permute-start | bytes 1572872 | tf_op jit(solution)/shard_map/ppermute | solution.py:16
  15.4 0.7 %pad_add_fusion.s_ref = s32[3]{0:T(128)} fusion(s32[1]{0:T(128)} %bitcast.2, s32[1]{0:T(128)} %bitcast.1, s32[1]{0:T(128)} %bitcast.side_ref), kind=kLoop, calls=%fused_computation | loop fusion | flops 6 | bytes 24 | tf_op jit(solution)/shard_map/stack | solution.py:230
  16.0 1.1 %collective-permute-done.x_ref = bf16[512,512]{1,0:T(8,128)(2,1)} collective-permute-done((bf16[512,512]{1,0:T(8,128)(2,1)}, bf16[512,512]{1,0:T(8,128)(2,1)}, u32[]{:S(2)}, u32[]{:S(2)}) %collective-permute-start) | collective-permute-done | bytes 524320 | tf_op jit(solution)/shard_map/ppermute | solution.py:217
  17.1 0.0 collective-permute-done.3.partner_hbm
  17.1 0.0 copy-start.2
  17.1 0.8 %copy-done.2 = bf16[512,512]{1,0:T(8,128)(2,1)} copy-done((bf16[512,512]{1,0:T(8,128)(2,1)}, bf16[512,512]{1,0:T(8,128)(2,1)S(1)}, u32[]{:S(2)}) %copy-start.2) | copy-done | bytes 524312
  17.9 9.2 %shard_map.56 = bf16[512,512]{1,0:T(8,128)(2,1)} custom-call(s32[3]{0:T(128)} %pad_add_fusion.s_ref, bf16[512,512]{1,0:T(8,128)(2,1)} %collective-permute-done.x_ref, bf16[2304,512]{1,0:T(8,128)(2,1)} %bitcast.12, bf16[2304,512]{1,0:T(8,128)(2,1)} %bitcast.14, f32[1,512]{1,0:T(1,128)} %bitcast.21, f32[1,512]{1,0:T(1,128)} %bitcast.23, ...), custom_call_target="tpu_custom_call" | custom-call | tf_op jit(solution)/shard_map/pallas_call | solution.py:168
Async XLA Ops:
  0.0 6.2 %collective-permute-start.1 = (bf16[3,3,256,512]{3,2,1,0:T(8,128)(2,1)}, bf16[3,3,256,512]{3,2,1,0:T(8,128)(2,1)S(1)}, u32[]{:S(2)}, u32[]{:S(2)}) collective-permute-start(bf16[3,3,256,512]{3,2,1,0:T(8,128)(2,1)} %param.6), channel_id=1, source_target_pairs={{0,1},{1,0},{2,3},{3,2},{4,5},{5,4},{6,7},{7,6},{8,9},{9,8},{10,11... | collective-permute-start | bytes 7077896 | tf_op jit(solution)/shard_map/ppermute | solution.py:16
  0.7 5.5 %collective-permute-start.2 = (bf16[3,256,512]{2,1,0:T(8,128)(2,1)}, bf16[3,256,512]{2,1,0:T(8,128)(2,1)S(1)}, u32[]{:S(2)}, u32[]{:S(2)}) collective-permute-start(bf16[3,256,512]{2,1,0:T(8,128)(2,1)} %param.9), channel_id=1, source_target_pairs={{0,1},{1,0},{2,3},{3,2},{4,5},{5,4},{6,7},{7,6},{8,9},{9,8},{10,11... | collective-permute-start | bytes 2359304 | tf_op jit(solution)/shard_map/ppermute | solution.py:16
  0.7 16.4 %collective-permute-start = (bf16[512,512]{1,0:T(8,128)(2,1)}, bf16[512,512]{1,0:T(8,128)(2,1)}, u32[]{:S(2)}, u32[]{:S(2)}) collective-permute-start(bf16[512,512]{1,0:T(8,128)(2,1)} %bitcast.16), channel_id=1, source_target_pairs={{1,2},{2,1},{3,4},{4,3},{5,6},{6,5},{7,8},{8,7},{9,10},{10,9},{11,... | collective-permute-start | bytes 1572872 | tf_op jit(solution)/shard_map/ppermute | solution.py:217
  6.2 0.9 %copy-start.1 = (bf16[3,256,512]{2,1,0:T(8,128)(2,1)}, bf16[3,256,512]{2,1,0:T(8,128)(2,1)S(1)}, u32[]{:S(2)}) copy-start(bf16[3,256,512]{2,1,0:T(8,128)(2,1)S(1)} %collective-permute-done.2.later_hbm) | copy-start | bytes 2359300
  6.2 1.7 %copy-start = (bf16[3,3,256,512]{3,2,1,0:T(8,128)(2,1)}, bf16[3,3,256,512]{3,2,1,0:T(8,128)(2,1)S(1)}, u32[]{:S(2)}) copy-start(bf16[3,3,256,512]{3,2,1,0:T(8,128)(2,1)S(1)} %collective-permute-done.1) | copy-start | bytes 7077892
  15.0 2.1 %collective-permute-start.3 = (bf16[512,512]{1,0:T(8,128)(2,1)}, bf16[512,512]{1,0:T(8,128)(2,1)S(1)}, u32[]{:S(2)}, u32[]{:S(2)}) collective-permute-start(bf16[512,512]{1,0:T(8,128)(2,1)} %shard_map.55.cur_hbm), channel_id=1, source_target_pairs={{0,1},{1,0},{2,3},{3,2},{4,5},{5,4},{6,7},{7,6},{8,9},{9,8},{10,11... | collective-permute-start | bytes 1572872 | tf_op jit(solution)/shard_map/ppermute | solution.py:16
  17.1 0.8 %copy-start.2 = (bf16[512,512]{1,0:T(8,128)(2,1)}, bf16[512,512]{1,0:T(8,128)(2,1)S(1)}, u32[]{:S(2)}) copy-start(bf16[512,512]{1,0:T(8,128)(2,1)S(1)} %collective-permute-done.3.partner_hbm) | copy-start | bytes 1572868

commit v16 on v15

--- a/solution.py
+++ b/solution.py
@@ -110,13 +110,13 @@
 
 
 def edge_temporal_kernel(s_ref, x_ref, wa_ref, wb_ref, gain_ref, shift_ref,
-                         cur_hbm, partner_hbm, wtm_hbm, wto_hbm, o_ref,
-                         lhs_ref, edge_v, cur_v, partner_v, wtm_v, wto_v, tl_ref, sem,
+                         cur_hbm, partner_v, wtm_hbm, wto_hbm, o_ref,
+                         lhs_ref, edge_v, cur_v, wtm_v, wto_v, tl_ref, sem,
                          *, width, group):
     copies = [
         pltpu.make_async_copy(src, dst, sem.at[i])
         for i, (src, dst) in enumerate(
-            ((cur_hbm, cur_v), (partner_hbm, partner_v), (wtm_hbm, wtm_v), (wto_hbm, wto_v))
+            ((cur_hbm, cur_v), (wtm_hbm, wtm_v), (wto_hbm, wto_v))
         )
     ]
     for copy in copies:
@@ -178,7 +178,7 @@
                 row_block,
                 row_block,
                 anywhere,
-                anywhere,
+                in_vmem,
                 anywhere,
                 anywhere,
             ],
@@ -187,11 +187,10 @@
                 pltpu.VMEM((2, rows, 9 * half), jnp.bfloat16),
                 pltpu.VMEM((rows, outputs), jnp.bfloat16),
                 pltpu.VMEM((rows, channels), jnp.bfloat16),
-                pltpu.VMEM((rows, channels), jnp.bfloat16),
                 pltpu.VMEM((3 * half, outputs), jnp.bfloat16),
                 pltpu.VMEM((3 * half, outputs), jnp.bfloat16),
                 pltpu.VMEM((2, rows, 3 * half), jnp.bfloat16),
-                pltpu.SemaphoreType.DMA((4,)),
+                pltpu.SemaphoreType.DMA((3,)),
             ],
         ),
         compiler_params=pltpu.CompilerParams(dimension_semantics=("arbitrary",)),

time: 27.3 us -> 27.4 us (level)
  no operation moved by 1% of the time
where the time goes in v16:
time: 27.4 us; the launch traced here: 27.2 us
  Pallas kernels  16.4 us (60%)
  starting transfers between devices  4.56 us (17%)
  waiting for transfers between devices  3.08 us (11%)
  local copies, waits for them, and re-layouts  2.45 us (9%)
  other arithmetic  0.65 us (2%)
    pallas_call x1, Pallas kernels, edge_temporal(): pl.pallas_call(kernel, out_shape=jax.ShapeDtypeStruct((rows, outputs), jn...  9.29 us
    pallas_call x1, Pallas kernels, conv_norm(): pl.pallas_call(kernel, out_shape=jax.ShapeDtypeStruct((rows, outputs), jn...  7.15 us
    ppermute x1, starting transfers between devices, body(): edge_video = lax.ppermute(frame, ('video', 'fsdp'), route)  3.5 us
    unnamed x6, local copies, waits for them, and re-layouts  2.45 us
    ppermute x3, waiting for transfers between devices, swap_pair(): return lax.ppermute(block, 'fsdp', [(0, 1), (1, 0)])  2 us
    ppermute x1, waiting for transfers between devices, body(): edge_video = lax.ppermute(frame, ('video', 'fsdp'), route)  1.08 us
    ppermute x3, starting transfers between devices, swap_pair(): return lax.ppermute(block, 'fsdp', [(0, 1), (1, 0)])  1.06 us
    another operation x1, other arithmetic, body(): scalars = jnp.stack([side.astype(jnp.int32), keep_edge, keep_partner])  0.65 us
  transfers between devices with their start and end apart: 4, of which 2 were waited for; matrix products, arithmetic and copies ran while one was open for 2% of the time, Pallas kernels for 26%

profile of v16, /device:TPU:17, one launch (start us, length us, event | category | flops | bytes accessed | tf_op | source)
XLA Modules:
  0.0 27.2 jit_solution(13938861574229443930)
XLA Ops:
  0.0 0.7 %collective-permute-start.1 = (bf16[3,3,256,512]{3,2,1,0:T(8,128)(2,1)}, bf16[3,3,256,512]{3,2,1,0:T(8,128)(2,1)S(1)}, u32[]{:S(2)}, u32[]{:S(2)}) collective-permute-start(bf16[3,3,256,512]{3,2,1,0:T(8,128)(2,1)} %param.6), channel_id=1, source_target_pairs={{0,1},{1,0},{2,3},{3,2},{4,5},{5,4},{6,7},{7,6},{8,9},{9,8},{10,11... | collective-permute-start | bytes 7077896 | tf_op jit(solution)/shard_map/ppermute | solution.py:16
  0.7 0.0 collective-permute-start.2
  0.7 3.5 %collective-permute-start = (bf16[512,512]{1,0:T(8,128)(2,1)}, bf16[512,512]{1,0:T(8,128)(2,1)}, u32[]{:S(2)}, u32[]{:S(2)}) collective-permute-start(bf16[512,512]{1,0:T(8,128)(2,1)} %bitcast.16), channel_id=1, source_target_pairs={{1,2},{2,1},{3,4},{4,3},{5,6},{6,5},{7,8},{8,7},{9,10},{10,9},{11,... | collective-permute-start | bytes 1572872 | tf_op jit(solution)/shard_map/ppermute | solution.py:216
  4.2 2.0 %collective-permute-done.2.later_hbm = bf16[3,256,512]{2,1,0:T(8,128)(2,1)S(1)} collective-permute-done((bf16[3,256,512]{2,1,0:T(8,128)(2,1)}, bf16[3,256,512]{2,1,0:T(8,128)(2,1)S(1)}, u32[]{:S(2)}, u32[]{:S(2)}) %collective-permute-start.2) | collective-permute-done | bytes 786464 | tf_op jit(solution)/shard_map/ppermute | solution.py:16
  6.2 0.0 copy-start.1
  6.2 0.0 collective-permute-done.1
  6.2 0.0 copy-start
  6.2 0.9 %copy-done.1 = bf16[3,256,512]{2,1,0:T(8,128)(2,1)} copy-done((bf16[3,256,512]{2,1,0:T(8,128)(2,1)}, bf16[3,256,512]{2,1,0:T(8,128)(2,1)S(1)}, u32[]{:S(2)}) %copy-start.1) | copy-done | bytes 786456
  7.1 0.8 %copy-done = bf16[3,3,256,512]{3,2,1,0:T(8,128)(2,1)} copy-done((bf16[3,3,256,512]{3,2,1,0:T(8,128)(2,1)}, bf16[3,3,256,512]{3,2,1,0:T(8,128)(2,1)S(1)}, u32[]{:S(2)}) %copy-start) | copy-done | bytes 2359320
  7.8 7.2 %shard_map.55.cur_hbm = bf16[512,512]{1,0:T(8,128)(2,1)} custom-call(s32[1]{0:T(128)} %bitcast.side_ref, bf16[512,512]{1,0:T(8,128)(2,1)} %bitcast.17, bf16[512,512]{1,0:T(8,128)(2,1)} %bitcast.18, bf16[2304,512]{1,0:T(8,128)(2,1)} %bitcast.11, bf16[2304,512]{1,0:T(8,128)(2,1)} %bitcast.13, f32[1,512]{1,0:T(1,128)} %bitcast.20, f32[1,512]{1,0:T(1,128)} %bitcast.22, ...), custom_call_target="tpu_custom_call" | custom-call | tf_op jit(solution)/shard_map/pallas_call | solution.py:89
  15.0 0.4 %collective-permute-start.3 = (bf16[512,512]{1,0:T(8,128)(2,1)}, bf16[512,512]{1,0:T(8,128)(2,1)S(1)}, u32[]{:S(2)}, u32[]{:S(2)}) collective-permute-start(bf16[512,512]{1,0:T(8,128)(2,1)} %shard_map.55.cur_hbm), channel_id=1, source_target_pairs={{0,1},{1,0},{2,3},{3,2},{4,5},{5,4},{6,7},{7,6},{8,9},{9,8},{10,11... | collective-permute-start | bytes 1572872 | tf_op jit(solution)/shard_map/ppermute | solution.py:16
  15.4 0.7 %pad_add_fusion.s_ref = s32[3]{0:T(128)} fusion(s32[1]{0:T(128)} %bitcast.2, s32[1]{0:T(128)} %bitcast.1, s32[1]{0:T(128)} %bitcast.side_ref), kind=kLoop, calls=%fused_computation | loop fusion | flops 6 | bytes 24 | tf_op jit(solution)/shard_map/stack | solution.py:229
  16.0 1.1 %collective-permute-done.x_ref = bf16[512,512]{1,0:T(8,128)(2,1)} collective-permute-done((bf16[512,512]{1,0:T(8,128)(2,1)}, bf16[512,512]{1,0:T(8,128)(2,1)}, u32[]{:S(2)}, u32[]{:S(2)}) %collective-permute-start) | collective-permute-done | bytes 524320 | tf_op jit(solution)/shard_map/ppermute | solution.py:216
  17.1 0.0 collective-permute-done.3.partner_v
  17.1 0.0 copy-start.2
  17.1 0.8 %copy-done.2 = bf16[512,512]{1,0:T(8,128)(2,1)} copy-done((bf16[512,512]{1,0:T(8,128)(2,1)}, bf16[512,512]{1,0:T(8,128)(2,1)S(1)}, u32[]{:S(2)}) %copy-start.2) | copy-done | bytes 524312
  17.9 9.3 %shard_map.56 = bf16[512,512]{1,0:T(8,128)(2,1)} custom-call(s32[3]{0:T(128)} %pad_add_fusion.s_ref, bf16[512,512]{1,0:T(8,128)(2,1)} %collective-permute-done.x_ref, bf16[2304,512]{1,0:T(8,128)(2,1)} %bitcast.12, bf16[2304,512]{1,0:T(8,128)(2,1)} %bitcast.14, f32[1,512]{1,0:T(1,128)} %bitcast.21, f32[1,512]{1,0:T(1,128)} %bitcast.23, ...), custom_call_target="tpu_custom_call" | custom-call | tf_op jit(solution)/shard_map/pallas_call | solution.py:168
Async XLA Ops:
  0.0 6.2 %collective-permute-start.1 = (bf16[3,3,256,512]{3,2,1,0:T(8,128)(2,1)}, bf16[3,3,256,512]{3,2,1,0:T(8,128)(2,1)S(1)}, u32[]{:S(2)}, u32[]{:S(2)}) collective-permute-start(bf16[3,3,256,512]{3,2,1,0:T(8,128)(2,1)} %param.6), channel_id=1, source_target_pairs={{0,1},{1,0},{2,3},{3,2},{4,5},{5,4},{6,7},{7,6},{8,9},{9,8},{10,11... | collective-permute-start | bytes 7077896 | tf_op jit(solution)/shard_map/ppermute | solution.py:16
  0.7 5.5 %collective-permute-start.2 = (bf16[3,256,512]{2,1,0:T(8,128)(2,1)}, bf16[3,256,512]{2,1,0:T(8,128)(2,1)S(1)}, u32[]{:S(2)}, u32[]{:S(2)}) collective-permute-start(bf16[3,256,512]{2,1,0:T(8,128)(2,1)} %param.9), channel_id=1, source_target_pairs={{0,1},{1,0},{2,3},{3,2},{4,5},{5,4},{6,7},{7,6},{8,9},{9,8},{10,11... | collective-permute-start | bytes 2359304 | tf_op jit(solution)/shard_map/ppermute | solution.py:16
  0.7 16.4 %collective-permute-start = (bf16[512,512]{1,0:T(8,128)(2,1)}, bf16[512,512]{1,0:T(8,128)(2,1)}, u32[]{:S(2)}, u32[]{:S(2)}) collective-permute-start(bf16[512,512]{1,0:T(8,128)(2,1)} %bitcast.16), channel_id=1, source_target_pairs={{1,2},{2,1},{3,4},{4,3},{5,6},{6,5},{7,8},{8,7},{9,10},{10,9},{11,... | collective-permute-start | bytes 1572872 | tf_op jit(solution)/shard_map/ppermute | solution.py:216
  6.2 0.9 %copy-start.1 = (bf16[3,256,512]{2,1,0:T(8,128)(2,1)}, bf16[3,256,512]{2,1,0:T(8,128)(2,1)S(1)}, u32[]{:S(2)}) copy-start(bf16[3,256,512]{2,1,0:T(8,128)(2,1)S(1)} %collective-permute-done.2.later_hbm) | copy-start | bytes 2359300
  6.2 1.7 %copy-start = (bf16[3,3,256,512]{3,2,1,0:T(8,128)(2,1)}, bf16[3,3,256,512]{3,2,1,0:T(8,128)(2,1)S(1)}, u32[]{:S(2)}) copy-start(bf16[3,3,256,512]{3,2,1,0:T(8,128)(2,1)S(1)} %collective-permute-done.1) | copy-start | bytes 7077892
  15.0 2.1 %collective-permute-start.3 = (bf16[512,512]{1,0:T(8,128)(2,1)}, bf16[512,512]{1,0:T(8,128)(2,1)S(1)}, u32[]{:S(2)}, u32[]{:S(2)}) collective-permute-start(bf16[512,512]{1,0:T(8,128)(2,1)} %shard_map.55.cur_hbm), channel_id=1, source_target_pairs={{0,1},{1,0},{2,3},{3,2},{4,5},{5,4},{6,7},{7,6},{8,9},{9,8},{10,11... | collective-permute-start | bytes 1572872 | tf_op jit(solution)/shard_map/ppermute | solution.py:16
  17.1 0.8 %copy-start.2 = (bf16[512,512]{1,0:T(8,128)(2,1)}, bf16[512,512]{1,0:T(8,128)(2,1)S(1)}, u32[]{:S(2)}) copy-start(bf16[512,512]{1,0:T(8,128)(2,1)S(1)} %collective-permute-done.3.partner_v) | copy-start | bytes 1572868

commit v17 on v8

--- a/solution.py
+++ b/solution.py
@@ -63,7 +63,8 @@
     spread = jnp.broadcast_to(jnp.sum(d * d, axis=0, keepdims=True), (8, acc.shape[1]))
     variance = group_sum(spread, group)[0:1] / count
     v = d * lax.rsqrt(variance + EPS) * gain_ref[...] + shift_ref[...]
-    o_ref[...] = (v / (1.0 + jnp.exp(-v))).astype(o_ref.dtype)
+    half_v = 0.5 * v
+    o_ref[...] = (half_v + half_v * jnp.tanh(half_v)).astype(o_ref.dtype)
 
 
 def conv_norm(frame, w_mine, w_other, gain, shift, side, width, split=1):

time: 27.1 us -> 27 us (level)
  no operation moved by 1% of the time
where the time goes in v17:
time: 27 us; the launch traced here: 26.8 us
  Pallas kernels  16.1 us (60%)
  starting transfers between devices  4.55 us (17%)
  waiting for transfers between devices  3.14 us (12%)
  local copies, waits for them, and re-layouts  2.37 us (9%)
  other arithmetic  0.65 us (2%)
    pallas_call x1, Pallas kernels, edge_temporal(): pl.pallas_call(kernel, out_shape=jax.ShapeDtypeStruct((rows, outputs), jn...  8.85 us
    pallas_call x1, Pallas kernels, conv_norm(): pl.pallas_call(kernel, out_shape=jax.ShapeDtypeStruct((rows, outputs), jn...  7.24 us
    ppermute x1, starting transfers between devices, body(): edge_video = lax.ppermute(frame, ('video', 'fsdp'), route)  3.5 us
    unnamed x6, local copies, waits for them, and re-layouts  2.37 us
    ppermute x3, waiting for transfers between devices, swap_pair(): return lax.ppermute(block, 'fsdp', [(0, 1), (1, 0)])  1.99 us
    ppermute x1, waiting for transfers between devices, body(): edge_video = lax.ppermute(frame, ('video', 'fsdp'), route)  1.15 us
    ppermute x3, starting transfers between devices, swap_pair(): return lax.ppermute(block, 'fsdp', [(0, 1), (1, 0)])  1.05 us
    another operation x1, other arithmetic, body(): scalars = jnp.stack([side.astype(jnp.int32), keep_edge, keep_partner])  0.65 us
  transfers between devices with their start and end apart: 4, of which 2 were waited for; matrix products, arithmetic and copies ran while one was open for 2% of the time, Pallas kernels for 27%

profile of v17, /device:TPU:17, one launch (start us, length us, event | category | flops | bytes accessed | tf_op | source)
XLA Modules:
  0.0 26.8 jit_solution(11029485189502782266)
XLA Ops:
  0.0 0.7 %collective-permute-start.1 = (bf16[3,3,256,512]{3,2,1,0:T(8,128)(2,1)}, bf16[3,3,256,512]{3,2,1,0:T(8,128)(2,1)S(1)}, u32[]{:S(2)}, u32[]{:S(2)}) collective-permute-start(bf16[3,3,256,512]{3,2,1,0:T(8,128)(2,1)} %param.6), channel_id=1, source_target_pairs={{0,1},{1,0},{2,3},{3,2},{4,5},{5,4},{6,7},{7,6},{8,9},{9,8},{10,11... | collective-permute-start | bytes 7077896 | tf_op jit(solution)/shard_map/ppermute | solution.py:16
  0.7 0.0 collective-permute-start.3
  0.7 3.5 %collective-permute-start = (bf16[512,512]{1,0:T(8,128)(2,1)}, bf16[512,512]{1,0:T(8,128)(2,1)S(1)}, u32[]{:S(2)}, u32[]{:S(2)}) collective-permute-start(bf16[512,512]{1,0:T(8,128)(2,1)} %bitcast.15), channel_id=1, source_target_pairs={{1,2},{2,1},{3,4},{4,3},{5,6},{6,5},{7,8},{8,7},{9,10},{10,9},{11,... | collective-permute-start | bytes 1572872 | tf_op jit(solution)/shard_map/ppermute | solution.py:203
  4.2 2.0 %collective-permute-done.1 = bf16[3,3,256,512]{3,2,1,0:T(8,128)(2,1)S(1)} collective-permute-done((bf16[3,3,256,512]{3,2,1,0:T(8,128)(2,1)}, bf16[3,3,256,512]{3,2,1,0:T(8,128)(2,1)S(1)}, u32[]{:S(2)}, u32[]{:S(2)}) %collective-permute-start.1) | collective-permute-done | bytes 2359328 | tf_op jit(solution)/shard_map/ppermute | solution.py:16
  6.2 0.0 copy-start
  6.2 1.4 %copy-done = bf16[3,3,256,512]{3,2,1,0:T(8,128)(2,1)} copy-done((bf16[3,3,256,512]{3,2,1,0:T(8,128)(2,1)}, bf16[3,3,256,512]{3,2,1,0:T(8,128)(2,1)S(1)}, u32[]{:S(2)}) %copy-start) | copy-done | bytes 2359320
  7.6 7.2 %shard_map.55.cur_hbm = bf16[512,512]{1,0:T(8,128)(2,1)} custom-call(s32[1]{0:T(128)} %bitcast.side_ref, bf16[512,512]{1,0:T(8,128)(2,1)} %bitcast.16, bf16[512,512]{1,0:T(8,128)(2,1)} %bitcast.17, bf16[2304,512]{1,0:T(8,128)(2,1)} %bitcast.11, bf16[2304,512]{1,0:T(8,128)(2,1)} %bitcast.13, f32[1,512]{1,0:T(1,128)} %bitcast.19, f32[1,512]{1,0:T(1,128)} %bitcast.21), custom_call_target="tpu_custom_call" | custom-call | tf_op jit(solution)/shard_map/pallas_call | solution.py:79
  14.8 0.4 %collective-permute-start.2 = (bf16[512,512]{1,0:T(8,128)(2,1)}, bf16[512,512]{1,0:T(8,128)(2,1)S(1)}, u32[]{:S(2)}, u32[]{:S(2)}) collective-permute-start(bf16[512,512]{1,0:T(8,128)(2,1)} %shard_map.55.cur_hbm), channel_id=1, source_target_pairs={{0,1},{1,0},{2,3},{3,2},{4,5},{5,4},{6,7},{7,6},{8,9},{9,8},{10,11... | collective-permute-start | bytes 1572872 | tf_op jit(solution)/shard_map/ppermute | solution.py:16
  15.2 0.7 %pad_add_fusion.s_ref = s32[3]{0:T(128)} fusion(s32[1]{0:T(128)} %bitcast.2, s32[1]{0:T(128)} %bitcast.1, s32[1]{0:T(128)} %bitcast.side_ref), kind=kLoop, calls=%fused_computation | loop fusion | flops 6 | bytes 24 | tf_op jit(solution)/shard_map/stack | solution.py:216
  15.8 1.2 %collective-permute-done.xa_ref.xb_ref = bf16[512,512]{1,0:T(8,128)(2,1)S(1)} collective-permute-done((bf16[512,512]{1,0:T(8,128)(2,1)}, bf16[512,512]{1,0:T(8,128)(2,1)S(1)}, u32[]{:S(2)}, u32[]{:S(2)}) %collective-permute-start) | collective-permute-done | bytes 524320 | tf_op jit(solution)/shard_map/ppermute | solution.py:203
  17.0 0.0 copy-start.1
  17.0 0.0 collective-permute-done.3
  17.0 0.0 collective-permute-done.2.partner_hbm
  17.0 0.0 copy-start.2
  17.0 0.8 %copy-done.1 = bf16[512,512]{1,0:T(8,128)(2,1)} copy-done((bf16[512,512]{1,0:T(8,128)(2,1)}, bf16[512,512]{1,0:T(8,128)(2,1)S(1)}, u32[]{:S(2)}) %copy-start.1) | copy-done | bytes 524312
  17.8 0.2 copy-done.2
  18.0 8.9 %shard_map.56 = bf16[512,512]{1,0:T(8,128)(2,1)} custom-call(s32[3]{0:T(128)} %pad_add_fusion.s_ref, bf16[512,512]{1,0:T(8,128)(2,1)} %copy-done.1, bf16[512,512]{1,0:T(8,128)(2,1)} %copy-done.1, bf16[2304,512]{1,0:T(8,128)(2,1)} %bitcast.12, bf16[2304,512]{1,0:T(8,128)(2,1)} %bitcast.14, f32[1,512]{1,0:T(1,128)} %bitcast.20, f32[1,512]{1,0:T(1,128)} %bitcast.22, ...), custom_call_target="tpu_custom_call" | custom-call | tf_op jit(solution)/shard_map/pallas_call | solution.py:153
Async XLA Ops:
  0.0 6.2 %collective-permute-start.1 = (bf16[3,3,256,512]{3,2,1,0:T(8,128)(2,1)}, bf16[3,3,256,512]{3,2,1,0:T(8,128)(2,1)S(1)}, u32[]{:S(2)}, u32[]{:S(2)}) collective-permute-start(bf16[3,3,256,512]{3,2,1,0:T(8,128)(2,1)} %param.6), channel_id=1, source_target_pairs={{0,1},{1,0},{2,3},{3,2},{4,5},{5,4},{6,7},{7,6},{8,9},{9,8},{10,11... | collective-permute-start | bytes 7077896 | tf_op jit(solution)/shard_map/ppermute | solution.py:16
  0.7 16.3 %collective-permute-start.3 = (bf16[3,256,512]{2,1,0:T(8,128)(2,1)}, bf16[3,256,512]{2,1,0:T(8,128)(2,1)}, u32[]{:S(2)}, u32[]{:S(2)}) collective-permute-start(bf16[3,256,512]{2,1,0:T(8,128)(2,1)} %param.9), channel_id=1, source_target_pairs={{0,1},{1,0},{2,3},{3,2},{4,5},{5,4},{6,7},{7,6},{8,9},{9,8},{10,11... | collective-permute-start | bytes 2359304 | tf_op jit(solution)/shard_map/ppermute | solution.py:16
  0.7 16.3 %collective-permute-start = (bf16[512,512]{1,0:T(8,128)(2,1)}, bf16[512,512]{1,0:T(8,128)(2,1)S(1)}, u32[]{:S(2)}, u32[]{:S(2)}) collective-permute-start(bf16[512,512]{1,0:T(8,128)(2,1)} %bitcast.15), channel_id=1, source_target_pairs={{1,2},{2,1},{3,4},{4,3},{5,6},{6,5},{7,8},{8,7},{9,10},{10,9},{11,... | collective-permute-start | bytes 1572872 | tf_op jit(solution)/shard_map/ppermute | solution.py:203
  6.2 1.4 %copy-start = (bf16[3,3,256,512]{3,2,1,0:T(8,128)(2,1)}, bf16[3,3,256,512]{3,2,1,0:T(8,128)(2,1)S(1)}, u32[]{:S(2)}) copy-start(bf16[3,3,256,512]{3,2,1,0:T(8,128)(2,1)S(1)} %collective-permute-done.1) | copy-start | bytes 7077892
  14.8 2.2 %collective-permute-start.2 = (bf16[512,512]{1,0:T(8,128)(2,1)}, bf16[512,512]{1,0:T(8,128)(2,1)S(1)}, u32[]{:S(2)}, u32[]{:S(2)}) collective-permute-start(bf16[512,512]{1,0:T(8,128)(2,1)} %shard_map.55.cur_hbm), channel_id=1, source_target_pairs={{0,1},{1,0},{2,3},{3,2},{4,5},{5,4},{6,7},{7,6},{8,9},{9,8},{10,11... | collective-permute-start | bytes 1572872 | tf_op jit(solution)/shard_map/ppermute | solution.py:16
  17.0 0.8 %copy-start.1 = (bf16[512,512]{1,0:T(8,128)(2,1)}, bf16[512,512]{1,0:T(8,128)(2,1)S(1)}, u32[]{:S(2)}) copy-start(bf16[512,512]{1,0:T(8,128)(2,1)S(1)} %collective-permute-done.xa_ref.xb_ref) | copy-start | bytes 1572868
  17.0 1.0 %copy-start.2 = (bf16[512,512]{1,0:T(8,128)(2,1)}, bf16[512,512]{1,0:T(8,128)(2,1)S(1)}, u32[]{:S(2)}) copy-start(bf16[512,512]{1,0:T(8,128)(2,1)S(1)} %collective-permute-done.2.partner_hbm) | copy-start | bytes 1572868

commit v18 on v15

--- a/solution.py
+++ b/solution.py
@@ -122,9 +122,13 @@
     for copy in copies:
         copy.start()
     half = x_ref.shape[1] // 2
-    build_lhs(
-        [((h + s_ref[0]) % 2, x_ref[:, h * half : (h + 1) * half]) for h in range(2)], lhs_ref, width
-    )
+    for side in range(2):
+        @pl.when(s_ref[0] == side)
+        def _prepare():
+            build_lhs(
+                [((h + side) % 2, x_ref[:, h * half : (h + 1) * half]) for h in range(2)],
+                lhs_ref, width,
+            )
     dots_norm(lhs_ref, wa_ref, wb_ref, gain_ref, shift_ref, edge_v, group)
     for copy in copies:
         copy.wait()

time: 27.3 us -> 27.4 us (level)
  no operation moved by 1% of the time
where the time goes in v18:
time: 27.4 us; the launch traced here: 27.2 us
  Pallas kernels  16.4 us (60%)
  starting transfers between devices  4.56 us (17%)
  waiting for transfers between devices  3.08 us (11%)
  local copies, waits for them, and re-layouts  2.45 us (9%)
  other arithmetic  0.65 us (2%)
    pallas_call x1, Pallas kernels, edge_temporal(): pl.pallas_call(kernel, out_shape=jax.ShapeDtypeStruct((rows, outputs), jn...  9.29 us
    pallas_call x1, Pallas kernels, conv_norm(): pl.pallas_call(kernel, out_shape=jax.ShapeDtypeStruct((rows, outputs), jn...  7.15 us
    ppermute x1, starting transfers between devices, body(): edge_video = lax.ppermute(frame, ('video', 'fsdp'), route)  3.5 us
    unnamed x6, local copies, waits for them, and re-layouts  2.45 us
    ppermute x3, waiting for transfers between devices, swap_pair(): return lax.ppermute(block, 'fsdp', [(0, 1), (1, 0)])  2 us
    ppermute x1, waiting for transfers between devices, body(): edge_video = lax.ppermute(frame, ('video', 'fsdp'), route)  1.08 us
    ppermute x3, starting transfers between devices, swap_pair(): return lax.ppermute(block, 'fsdp', [(0, 1), (1, 0)])  1.06 us
    another operation x1, other arithmetic, body(): scalars = jnp.stack([side.astype(jnp.int32), keep_edge, keep_partner])  0.65 us
  transfers between devices with their start and end apart: 4, of which 2 were waited for; matrix products, arithmetic and copies ran while one was open for 2% of the time, Pallas kernels for 26%

profile of v18, /device:TPU:17, one launch (start us, length us, event | category | flops | bytes accessed | tf_op | source)
XLA Modules:
  0.0 27.2 jit_solution(3033566577821146150)
XLA Ops:
  0.0 0.7 %collective-permute-start.1 = (bf16[3,3,256,512]{3,2,1,0:T(8,128)(2,1)}, bf16[3,3,256,512]{3,2,1,0:T(8,128)(2,1)S(1)}, u32[]{:S(2)}, u32[]{:S(2)}) collective-permute-start(bf16[3,3,256,512]{3,2,1,0:T(8,128)(2,1)} %param.6), channel_id=1, source_target_pairs={{0,1},{1,0},{2,3},{3,2},{4,5},{5,4},{6,7},{7,6},{8,9},{9,8},{10,11... | collective-permute-start | bytes 7077896 | tf_op jit(solution)/shard_map/ppermute | solution.py:16
  0.7 0.0 collective-permute-start.2
  0.7 3.5 %collective-permute-start = (bf16[512,512]{1,0:T(8,128)(2,1)}, bf16[512,512]{1,0:T(8,128)(2,1)}, u32[]{:S(2)}, u32[]{:S(2)}) collective-permute-start(bf16[512,512]{1,0:T(8,128)(2,1)} %bitcast.16), channel_id=1, source_target_pairs={{1,2},{2,1},{3,4},{4,3},{5,6},{6,5},{7,8},{8,7},{9,10},{10,9},{11,... | collective-permute-start | bytes 1572872 | tf_op jit(solution)/shard_map/ppermute | solution.py:221
  4.2 2.0 %collective-permute-done.2.later_hbm = bf16[3,256,512]{2,1,0:T(8,128)(2,1)S(1)} collective-permute-done((bf16[3,256,512]{2,1,0:T(8,128)(2,1)}, bf16[3,256,512]{2,1,0:T(8,128)(2,1)S(1)}, u32[]{:S(2)}, u32[]{:S(2)}) %collective-permute-start.2) | collective-permute-done | bytes 786464 | tf_op jit(solution)/shard_map/ppermute | solution.py:16
  6.2 0.0 copy-start.1
  6.2 0.0 collective-permute-done.1
  6.2 0.0 copy-start
  6.2 0.9 %copy-done.1 = bf16[3,256,512]{2,1,0:T(8,128)(2,1)} copy-done((bf16[3,256,512]{2,1,0:T(8,128)(2,1)}, bf16[3,256,512]{2,1,0:T(8,128)(2,1)S(1)}, u32[]{:S(2)}) %copy-start.1) | copy-done | bytes 786456
  7.1 0.8 %copy-done = bf16[3,3,256,512]{3,2,1,0:T(8,128)(2,1)} copy-done((bf16[3,3,256,512]{3,2,1,0:T(8,128)(2,1)}, bf16[3,3,256,512]{3,2,1,0:T(8,128)(2,1)S(1)}, u32[]{:S(2)}) %copy-start) | copy-done | bytes 2359320
  7.8 7.2 %shard_map.55.cur_hbm = bf16[512,512]{1,0:T(8,128)(2,1)} custom-call(s32[1]{0:T(128)} %bitcast.side_ref, bf16[512,512]{1,0:T(8,128)(2,1)} %bitcast.17, bf16[512,512]{1,0:T(8,128)(2,1)} %bitcast.18, bf16[2304,512]{1,0:T(8,128)(2,1)} %bitcast.11, bf16[2304,512]{1,0:T(8,128)(2,1)} %bitcast.13, f32[1,512]{1,0:T(1,128)} %bitcast.20, f32[1,512]{1,0:T(1,128)} %bitcast.22, ...), custom_call_target="tpu_custom_call" | custom-call | tf_op jit(solution)/shard_map/pallas_call | solution.py:89
  15.0 0.4 %collective-permute-start.3 = (bf16[512,512]{1,0:T(8,128)(2,1)}, bf16[512,512]{1,0:T(8,128)(2,1)S(1)}, u32[]{:S(2)}, u32[]{:S(2)}) collective-permute-start(bf16[512,512]{1,0:T(8,128)(2,1)} %shard_map.55.cur_hbm), channel_id=1, source_target_pairs={{0,1},{1,0},{2,3},{3,2},{4,5},{5,4},{6,7},{7,6},{8,9},{9,8},{10,11... | collective-permute-start | bytes 1572872 | tf_op jit(solution)/shard_map/ppermute | solution.py:16
  15.4 0.7 %pad_add_fusion.s_ref = s32[3]{0:T(128)} fusion(s32[1]{0:T(128)} %bitcast.2, s32[1]{0:T(128)} %bitcast.1, s32[1]{0:T(128)} %bitcast.side_ref), kind=kLoop, calls=%fused_computation | loop fusion | flops 6 | bytes 24 | tf_op jit(solution)/shard_map/stack | solution.py:234
  16.0 1.1 %collective-permute-done.x_ref = bf16[512,512]{1,0:T(8,128)(2,1)} collective-permute-done((bf16[512,512]{1,0:T(8,128)(2,1)}, bf16[512,512]{1,0:T(8,128)(2,1)}, u32[]{:S(2)}, u32[]{:S(2)}) %collective-permute-start) | collective-permute-done | bytes 524320 | tf_op jit(solution)/shard_map/ppermute | solution.py:221
  17.1 0.0 collective-permute-done.3.partner_hbm
  17.1 0.0 copy-start.2
  17.1 0.8 %copy-done.2 = bf16[512,512]{1,0:T(8,128)(2,1)} copy-done((bf16[512,512]{1,0:T(8,128)(2,1)}, bf16[512,512]{1,0:T(8,128)(2,1)S(1)}, u32[]{:S(2)}) %copy-start.2) | copy-done | bytes 524312
  17.9 9.3 %shard_map.56 = bf16[512,512]{1,0:T(8,128)(2,1)} custom-call(s32[3]{0:T(128)} %pad_add_fusion.s_ref, bf16[512,512]{1,0:T(8,128)(2,1)} %collective-permute-done.x_ref, bf16[2304,512]{1,0:T(8,128)(2,1)} %bitcast.12, bf16[2304,512]{1,0:T(8,128)(2,1)} %bitcast.14, f32[1,512]{1,0:T(1,128)} %bitcast.21, f32[1,512]{1,0:T(1,128)} %bitcast.23, ...), custom_call_target="tpu_custom_call" | custom-call | tf_op jit(solution)/shard_map/pallas_call | solution.py:172
Async XLA Ops:
  0.0 6.2 %collective-permute-start.1 = (bf16[3,3,256,512]{3,2,1,0:T(8,128)(2,1)}, bf16[3,3,256,512]{3,2,1,0:T(8,128)(2,1)S(1)}, u32[]{:S(2)}, u32[]{:S(2)}) collective-permute-start(bf16[3,3,256,512]{3,2,1,0:T(8,128)(2,1)} %param.6), channel_id=1, source_target_pairs={{0,1},{1,0},{2,3},{3,2},{4,5},{5,4},{6,7},{7,6},{8,9},{9,8},{10,11... | collective-permute-start | bytes 7077896 | tf_op jit(solution)/shard_map/ppermute | solution.py:16
  0.7 5.5 %collective-permute-start.2 = (bf16[3,256,512]{2,1,0:T(8,128)(2,1)}, bf16[3,256,512]{2,1,0:T(8,128)(2,1)S(1)}, u32[]{:S(2)}, u32[]{:S(2)}) collective-permute-start(bf16[3,256,512]{2,1,0:T(8,128)(2,1)} %param.9), channel_id=1, source_target_pairs={{0,1},{1,0},{2,3},{3,2},{4,5},{5,4},{6,7},{7,6},{8,9},{9,8},{10,11... | collective-permute-start | bytes 2359304 | tf_op jit(solution)/shard_map/ppermute | solution.py:16
  0.7 16.4 %collective-permute-start = (bf16[512,512]{1,0:T(8,128)(2,1)}, bf16[512,512]{1,0:T(8,128)(2,1)}, u32[]{:S(2)}, u32[]{:S(2)}) collective-permute-start(bf16[512,512]{1,0:T(8,128)(2,1)} %bitcast.16), channel_id=1, source_target_pairs={{1,2},{2,1},{3,4},{4,3},{5,6},{6,5},{7,8},{8,7},{9,10},{10,9},{11,... | collective-permute-start | bytes 1572872 | tf_op jit(solution)/shard_map/ppermute | solution.py:221
  6.2 0.9 %copy-start.1 = (bf16[3,256,512]{2,1,0:T(8,128)(2,1)}, bf16[3,256,512]{2,1,0:T(8,128)(2,1)S(1)}, u32[]{:S(2)}) copy-start(bf16[3,256,512]{2,1,0:T(8,128)(2,1)S(1)} %collective-permute-done.2.later_hbm) | copy-start | bytes 2359300
  6.2 1.7 %copy-start = (bf16[3,3,256,512]{3,2,1,0:T(8,128)(2,1)}, bf16[3,3,256,512]{3,2,1,0:T(8,128)(2,1)S(1)}, u32[]{:S(2)}) copy-start(bf16[3,3,256,512]{3,2,1,0:T(8,128)(2,1)S(1)} %collective-permute-done.1) | copy-start | bytes 7077892
  15.0 2.1 %collective-permute-start.3 = (bf16[512,512]{1,0:T(8,128)(2,1)}, bf16[512,512]{1,0:T(8,128)(2,1)S(1)}, u32[]{:S(2)}, u32[]{:S(2)}) collective-permute-start(bf16[512,512]{1,0:T(8,128)(2,1)} %shard_map.55.cur_hbm), channel_id=1, source_target_pairs={{0,1},{1,0},{2,3},{3,2},{4,5},{5,4},{6,7},{7,6},{8,9},{9,8},{10,11... | collective-permute-start | bytes 1572872 | tf_op jit(solution)/shard_map/ppermute | solution.py:16
  17.1 0.8 %copy-start.2 = (bf16[512,512]{1,0:T(8,128)(2,1)}, bf16[512,512]{1,0:T(8,128)(2,1)S(1)}, u32[]{:S(2)}) copy-start(bf16[512,512]{1,0:T(8,128)(2,1)S(1)} %collective-permute-done.3.partner_hbm) | copy-start | bytes 1572868

commit v19 on v13

--- a/solution.py
+++ b/solution.py
@@ -63,7 +63,10 @@
     spread = jnp.broadcast_to(jnp.sum(d * d, axis=0, keepdims=True), (8, acc.shape[1]))
     variance = group_sum(spread, group)[0:1] / count
     v = d * lax.rsqrt(variance + EPS) * gain_ref[...] + shift_ref[...]
-    o_ref[...] = (v / (1.0 + jnp.exp(-v))).astype(o_ref.dtype)
+    hidden = (v / (1.0 + jnp.exp(-v))).astype(jnp.bfloat16)
+    if o_ref is None:
+        return hidden
+    o_ref[...] = hidden.astype(o_ref.dtype)
 
 
 def conv_norm(frame, w_mine, w_other, gain, shift, side, width, split=1):
@@ -99,7 +102,7 @@
 
 def edge_temporal_kernel(s_ref, xa_ref, xb_ref, wa_ref, wb_ref, gain_ref, shift_ref,
                          cur_hbm, partner_hbm, wtm_hbm, wto_hbm, o_ref,
-                         lhs_ref, edge_v, cur_v, partner_v, wtm_v, wto_v, tl_ref, sem,
+                         lhs_ref, cur_v, partner_v, wtm_v, wto_v, tl_ref, sem,
                          *, width, group):
     copies = [
         pltpu.make_async_copy(src, dst, sem.at[i])
@@ -107,30 +110,35 @@
             ((cur_hbm, cur_v), (partner_hbm, partner_v), (wtm_hbm, wtm_v), (wto_hbm, wto_v))
         )
     ]
-    conv_norm_kernel(s_ref, xa_ref, xb_ref, wa_ref, wb_ref, gain_ref, shift_ref, edge_v,
-                     lhs_ref, width=width, group=group)
     for copy in copies:
         copy.start()
-    for copy in copies:
-        copy.wait()
-
+    edge_h = conv_norm_kernel(s_ref, xa_ref, xb_ref, wa_ref, wb_ref, gain_ref, shift_ref, None,
+                              lhs_ref, width=width, group=group)
     rows, half = xa_ref.shape
     keep_edge = s_ref[1] != 0
     keep_partner = s_ref[2] != 0
+    edge_h = jnp.where(keep_edge, edge_h, jnp.zeros_like(edge_h))
+    for side in range(2):
+        @pl.when(s_ref[0] == side)
+        def _edge():
+            mine = slice(side * half, (side + 1) * half)
+            other = slice((1 - side) * half, (2 - side) * half)
+            at = slice(0, half) if side == 0 else slice(2 * half, 3 * half)
+            for h, cols in enumerate((mine, other)):
+                tl_ref[h, :, at] = edge_h[:, cols]
+    for copy in copies:
+        copy.wait()
+
     for side in range(2):
         @pl.when(s_ref[0] == side)
         def _fill():
             mine = slice(side * half, (side + 1) * half)
             other = slice((1 - side) * half, (2 - side) * half)
+            at = slice(2 * half, 3 * half) if side == 0 else slice(0, half)
             for h, cols in enumerate((mine, other)):
-                e = edge_v[:, cols]
                 p = partner_v[:, cols]
-                e = jnp.where(keep_edge, e, jnp.zeros_like(e))
-                p = jnp.where(keep_partner, p, jnp.zeros_like(p))
-                before, after = (e, p) if side == 0 else (p, e)
-                tl_ref[h, :, :half] = before
+                tl_ref[h, :, at] = jnp.where(keep_partner, p, jnp.zeros_like(p))
                 tl_ref[h, :, half : 2 * half] = cur_v[:, cols]
-                tl_ref[h, :, 2 * half :] = after
 
     f32 = jnp.float32
     total = jnp.dot(tl_ref[0], wtm_v[...], preferred_element_type=f32) + jnp.dot(
@@ -170,7 +178,6 @@
             out_specs=pl.BlockSpec((rows, outputs), lambda n, s: (0, 0)),
             scratch_shapes=[
                 pltpu.VMEM((2, rows, 9 * half), jnp.bfloat16),
-                pltpu.VMEM((rows, outputs), jnp.bfloat16),
                 pltpu.VMEM((rows, channels), jnp.bfloat16),
                 pltpu.VMEM((rows, channels), jnp.bfloat16),
                 pltpu.VMEM((3 * half, outputs), jnp.bfloat16),

time: 27.1 us -> 27.1 us (level)
  no operation moved by 1% of the time
where the time goes in v19:
time: 27.1 us; the launch traced here: 26.9 us
  Pallas kernels  16.1 us (59%)
  starting transfers between devices  4.55 us (17%)
  waiting for transfers between devices  3.22 us (12%)
  local copies, waits for them, and re-layouts  2.37 us (9%)
  other arithmetic  0.65 us (2%)
    pallas_call x1, Pallas kernels, edge_temporal(): pl.pallas_call(kernel, out_shape=jax.ShapeDtypeStruct((rows, outputs), jn...  8.91 us
    pallas_call x1, Pallas kernels, conv_norm(): pl.pallas_call(kernel, out_shape=jax.ShapeDtypeStruct((rows, outputs), jn...  7.16 us
    ppermute x1, starting transfers between devices, body(): edge_video = lax.ppermute(frame, ('video', 'fsdp'), route)  3.5 us
    unnamed x6, local copies, waits for them, and re-layouts  2.37 us
    ppermute x3, waiting for transfers between devices, swap_pair(): return lax.ppermute(block, 'fsdp', [(0, 1), (1, 0)])  1.99 us
    ppermute x1, waiting for transfers between devices, body(): edge_video = lax.ppermute(frame, ('video', 'fsdp'), route)  1.23 us
    ppermute x3, starting transfers between devices, swap_pair(): return lax.ppermute(block, 'fsdp', [(0, 1), (1, 0)])  1.05 us
    another operation x1, other arithmetic, body(): scalars = jnp.stack([side.astype(jnp.int32), keep_edge, keep_partner])  0.65 us
  transfers between devices with their start and end apart: 4, of which 2 were waited for; matrix products, arithmetic and copies ran while one was open for 2% of the time, Pallas kernels for 27%

profile of v19, /device:TPU:17, one launch (start us, length us, event | category | flops | bytes accessed | tf_op | source)
XLA Modules:
  0.0 26.9 jit_solution(5519562066143367165)
XLA Ops:
  0.0 0.7 %collective-permute-start.1 = (bf16[3,3,256,512]{3,2,1,0:T(8,128)(2,1)}, bf16[3,3,256,512]{3,2,1,0:T(8,128)(2,1)S(1)}, u32[]{:S(2)}, u32[]{:S(2)}) collective-permute-start(bf16[3,3,256,512]{3,2,1,0:T(8,128)(2,1)} %param.6), channel_id=1, source_target_pairs={{0,1},{1,0},{2,3},{3,2},{4,5},{5,4},{6,7},{7,6},{8,9},{9,8},{10,11... | collective-permute-start | bytes 7077896 | tf_op jit(solution)/shard_map/ppermute | solution.py:16
  0.7 0.0 collective-permute-start.3
  0.7 3.5 %collective-permute-start = (bf16[512,512]{1,0:T(8,128)(2,1)}, bf16[512,512]{1,0:T(8,128)(2,1)S(1)}, u32[]{:S(2)}, u32[]{:S(2)}) collective-permute-start(bf16[512,512]{1,0:T(8,128)(2,1)} %bitcast.15), channel_id=1, source_target_pairs={{1,2},{2,1},{3,4},{4,3},{5,6},{6,5},{7,8},{8,7},{9,10},{10,9},{11,... | collective-permute-start | bytes 1572872 | tf_op jit(solution)/shard_map/ppermute | solution.py:209
  4.2 2.0 %collective-permute-done.1 = bf16[3,3,256,512]{3,2,1,0:T(8,128)(2,1)S(1)} collective-permute-done((bf16[3,3,256,512]{3,2,1,0:T(8,128)(2,1)}, bf16[3,3,256,512]{3,2,1,0:T(8,128)(2,1)S(1)}, u32[]{:S(2)}, u32[]{:S(2)}) %collective-permute-start.1) | collective-permute-done | bytes 2359328 | tf_op jit(solution)/shard_map/ppermute | solution.py:16
  6.2 0.0 copy-start
  6.2 1.4 %copy-done = bf16[3,3,256,512]{3,2,1,0:T(8,128)(2,1)} copy-done((bf16[3,3,256,512]{3,2,1,0:T(8,128)(2,1)}, bf16[3,3,256,512]{3,2,1,0:T(8,128)(2,1)S(1)}, u32[]{:S(2)}) %copy-start) | copy-done | bytes 2359320
  7.6 7.2 %shard_map.55.cur_hbm = bf16[512,512]{1,0:T(8,128)(2,1)} custom-call(s32[1]{0:T(128)} %bitcast.side_ref, bf16[512,512]{1,0:T(8,128)(2,1)} %bitcast.16, bf16[512,512]{1,0:T(8,128)(2,1)} %bitcast.17, bf16[2304,512]{1,0:T(8,128)(2,1)} %bitcast.11, bf16[2304,512]{1,0:T(8,128)(2,1)} %bitcast.13, f32[1,512]{1,0:T(1,128)} %bitcast.19, f32[1,512]{1,0:T(1,128)} %bitcast.21), custom_call_target="tpu_custom_call" | custom-call | tf_op jit(solution)/shard_map/pallas_call | solution.py:81
  14.7 0.4 %collective-permute-start.2 = (bf16[512,512]{1,0:T(8,128)(2,1)}, bf16[512,512]{1,0:T(8,128)(2,1)S(1)}, u32[]{:S(2)}, u32[]{:S(2)}) collective-permute-start(bf16[512,512]{1,0:T(8,128)(2,1)} %shard_map.55.cur_hbm), channel_id=1, source_target_pairs={{0,1},{1,0},{2,3},{3,2},{4,5},{5,4},{6,7},{7,6},{8,9},{9,8},{10,11... | collective-permute-start | bytes 1572872 | tf_op jit(solution)/shard_map/ppermute | solution.py:16
  15.1 0.7 %pad_add_fusion.s_ref = s32[3]{0:T(128)} fusion(s32[1]{0:T(128)} %bitcast.2, s32[1]{0:T(128)} %bitcast.1, s32[1]{0:T(128)} %bitcast.side_ref), kind=kLoop, calls=%fused_computation | loop fusion | flops 6 | bytes 24 | tf_op jit(solution)/shard_map/stack | solution.py:222
  15.8 1.2 %collective-permute-done.xa_ref.xb_ref = bf16[512,512]{1,0:T(8,128)(2,1)S(1)} collective-permute-done((bf16[512,512]{1,0:T(8,128)(2,1)}, bf16[512,512]{1,0:T(8,128)(2,1)S(1)}, u32[]{:S(2)}, u32[]{:S(2)}) %collective-permute-start) | collective-permute-done | bytes 524320 | tf_op jit(solution)/shard_map/ppermute | solution.py:209
  17.0 0.0 copy-start.1
  17.0 0.0 collective-permute-done.3
  17.0 0.0 collective-permute-done.2.partner_hbm
  17.0 0.0 copy-start.2
  17.0 0.8 %copy-done.1 = bf16[512,512]{1,0:T(8,128)(2,1)} copy-done((bf16[512,512]{1,0:T(8,128)(2,1)}, bf16[512,512]{1,0:T(8,128)(2,1)S(1)}, u32[]{:S(2)}) %copy-start.1) | copy-done | bytes 524312
  17.8 0.2 copy-done.2
  18.0 8.9 %shard_map.56 = bf16[512,512]{1,0:T(8,128)(2,1)} custom-call(s32[3]{0:T(128)} %pad_add_fusion.s_ref, bf16[512,512]{1,0:T(8,128)(2,1)} %copy-done.1, bf16[512,512]{1,0:T(8,128)(2,1)} %copy-done.1, bf16[2304,512]{1,0:T(8,128)(2,1)} %bitcast.12, bf16[2304,512]{1,0:T(8,128)(2,1)} %bitcast.14, f32[1,512]{1,0:T(1,128)} %bitcast.20, f32[1,512]{1,0:T(1,128)} %bitcast.22, ...), custom_call_target="tpu_custom_call" | custom-call | tf_op jit(solution)/shard_map/pallas_call | solution.py:160
Async XLA Ops:
  0.0 6.2 %collective-permute-start.1 = (bf16[3,3,256,512]{3,2,1,0:T(8,128)(2,1)}, bf16[3,3,256,512]{3,2,1,0:T(8,128)(2,1)S(1)}, u32[]{:S(2)}, u32[]{:S(2)}) collective-permute-start(bf16[3,3,256,512]{3,2,1,0:T(8,128)(2,1)} %param.6), channel_id=1, source_target_pairs={{0,1},{1,0},{2,3},{3,2},{4,5},{5,4},{6,7},{7,6},{8,9},{9,8},{10,11... | collective-permute-start | bytes 7077896 | tf_op jit(solution)/shard_map/ppermute | solution.py:16
  0.7 16.3 %collective-permute-start.3 = (bf16[3,256,512]{2,1,0:T(8,128)(2,1)}, bf16[3,256,512]{2,1,0:T(8,128)(2,1)}, u32[]{:S(2)}, u32[]{:S(2)}) collective-permute-start(bf16[3,256,512]{2,1,0:T(8,128)(2,1)} %param.9), channel_id=1, source_target_pairs={{0,1},{1,0},{2,3},{3,2},{4,5},{5,4},{6,7},{7,6},{8,9},{9,8},{10,11... | collective-permute-start | bytes 2359304 | tf_op jit(solution)/shard_map/ppermute | solution.py:16
  0.7 16.3 %collective-permute-start = (bf16[512,512]{1,0:T(8,128)(2,1)}, bf16[512,512]{1,0:T(8,128)(2,1)S(1)}, u32[]{:S(2)}, u32[]{:S(2)}) collective-permute-start(bf16[512,512]{1,0:T(8,128)(2,1)} %bitcast.15), channel_id=1, source_target_pairs={{1,2},{2,1},{3,4},{4,3},{5,6},{6,5},{7,8},{8,7},{9,10},{10,9},{11,... | collective-permute-start | bytes 1572872 | tf_op jit(solution)/shard_map/ppermute | solution.py:209
  6.2 1.4 %copy-start = (bf16[3,3,256,512]{3,2,1,0:T(8,128)(2,1)}, bf16[3,3,256,512]{3,2,1,0:T(8,128)(2,1)S(1)}, u32[]{:S(2)}) copy-start(bf16[3,3,256,512]{3,2,1,0:T(8,128)(2,1)S(1)} %collective-permute-done.1) | copy-start | bytes 7077892
  14.7 2.3 %collective-permute-start.2 = (bf16[512,512]{1,0:T(8,128)(2,1)}, bf16[512,512]{1,0:T(8,128)(2,1)S(1)}, u32[]{:S(2)}, u32[]{:S(2)}) collective-permute-start(bf16[512,512]{1,0:T(8,128)(2,1)} %shard_map.55.cur_hbm), channel_id=1, source_target_pairs={{0,1},{1,0},{2,3},{3,2},{4,5},{5,4},{6,7},{7,6},{8,9},{9,8},{10,11... | collective-permute-start | bytes 1572872 | tf_op jit(solution)/shard_map/ppermute | solution.py:16
  17.0 0.8 %copy-start.1 = (bf16[512,512]{1,0:T(8,128)(2,1)}, bf16[512,512]{1,0:T(8,128)(2,1)S(1)}, u32[]{:S(2)}) copy-start(bf16[512,512]{1,0:T(8,128)(2,1)S(1)} %collective-permute-done.xa_ref.xb_ref) | copy-start | bytes 1572868
  17.0 1.0 %copy-start.2 = (bf16[512,512]{1,0:T(8,128)(2,1)}, bf16[512,512]{1,0:T(8,128)(2,1)S(1)}, u32[]{:S(2)}) copy-start(bf16[512,512]{1,0:T(8,128)(2,1)S(1)} %collective-permute-done.2.partner_hbm) | copy-start | bytes 1572868
